TPU v7x, 128 devices: a whole 4x4x4 slice. The times are simulated.
128 devices in a mesh: amp: 64 (over x, z, y_hi, core), grp: 2 (over y_lo).
Axes of the slice: x: 4, y: 4 (y_hi: 2, y_lo: 2; y = y_hi * 2 + y_lo), z: 4, core: 2. Of those that a mesh axis runs over, the one named last changes fastest.
Arguments:
- amplitudes: bfloat16 [16384, 128, 128], P(('amp', 'grp')), may hold values from -6 to 6
- adjoint: bfloat16 [16384, 128, 128], P(('amp', 'grp')), may hold values from -6 to 6
- gate_mats: bfloat16 [20, 128, 128], replicated, as said below
- gate_order: int32 [20], replicated, may hold values from 0 to 19, each once
- gate_window: int32 [20], replicated, may hold values from 0 to 1
- swap_window: int32 [3], replicated, may hold values from 0 to 1
Outputs:
- final_state: bfloat16 [16384, 128, 128], P(('amp', 'grp'))
- environment: float32 [512, 512], P('grp')
Inputs may be any that keep to these rules, and one draw needn't show every extreme that they name: `gate_mats`: each gate matrix is an orthogonal matrix rounded to bfloat16.
All inputs are finite; a program needn't handle non-finite values.
Results may differ from a plain program's by a relative error of at most 0.04.
Values may be sent and summed in bfloat16 or wider, within the bound.
No kernel may reach another device: no remote copies, remote signals or barrier semaphores. Data moves between devices by JAX's collectives and lax.ppermute only.
A program may use at most 128 MiB of HBM per device.

v0:
```python
import jax
import jax.numpy as jnp
from jax import lax
from jax.experimental import pallas as pl
from jax.experimental.pallas import tpu as pltpu
from jax.sharding import PartitionSpec as P

SEGS = 4
GATES = 5
BLOCK = 32


def make_kernel(slab_in, slab_out):
    def kernel(order_ref, flip_ref, gates_ref, x_ref, o_ref, held):
        half, wide, pair = held.shape
        lanes = pair // 2
        if slab_in:
            slabs = x_ref[...]
        else:
            slabs = jnp.swapaxes(x_ref[...], 0, 1)
        held[:, :, :lanes] = slabs[:half]
        held[:, :, lanes:] = slabs[half:]

        def flip():
            held[:, :, :lanes] = jnp.swapaxes(held[:, :, :lanes], 1, 2)
            held[:, :, lanes:] = jnp.swapaxes(held[:, :, lanes:], 1, 2)

        def one_gate(position, carry):
            pl.when(flip_ref[position] == 1)(flip)
            matrix = gates_ref[order_ref[position]]
            flat = held[...].reshape(half * wide, pair)
            out = jnp.dot(flat, matrix, preferred_element_type=jnp.float32)
            held[...] = out.astype(jnp.bfloat16).reshape(half, wide, pair)
            return carry

        lax.fori_loop(0, GATES, one_gate, 0)
        pl.when(flip_ref[GATES] == 1)(flip)

        first = held[:, :, :lanes]
        second = held[:, :, lanes:]
        if slab_out:
            o_ref[:half] = first
            o_ref[half:] = second
        else:
            o_ref[:, :half, :] = jnp.swapaxes(first, 0, 1)
            o_ref[:, half:, :] = jnp.swapaxes(second, 0, 1)

    return kernel


def block_diagonal(gate_mats):
    transposed = jnp.swapaxes(gate_mats, 1, 2)
    zeros = jnp.zeros_like(transposed)
    top = jnp.concatenate([transposed, zeros], axis=2)
    bottom = jnp.concatenate([zeros, transposed], axis=2)
    return jnp.concatenate([top, bottom], axis=1)


def run_segment(values, gates_bd, order, flips, slab_in, slab_out):
    wide = gates_bd.shape[1] // 2
    slabs = values.shape[0] if slab_in else values.shape[1]
    lanes = values.shape[2]
    slab_spec = pl.BlockSpec((BLOCK, wide, lanes), lambda i, o, f: (i, 0, 0))
    major_spec = pl.BlockSpec((wide, BLOCK, lanes), lambda i, o, f: (0, i, 0))
    out_shape = (slabs, wide, lanes) if slab_out else (wide, slabs, lanes)
    grid_spec = pltpu.PrefetchScalarGridSpec(
        num_scalar_prefetch=2,
        grid=(slabs // BLOCK,),
        in_specs=[
            pl.BlockSpec(gates_bd.shape, lambda i, o, f: (0, 0, 0)),
            slab_spec if slab_in else major_spec,
        ],
        out_specs=slab_spec if slab_out else major_spec,
        scratch_shapes=[pltpu.VMEM((BLOCK // 2, wide, 2 * lanes), jnp.bfloat16)],
    )
    return pl.pallas_call(
        make_kernel(slab_in, slab_out),
        grid_spec=grid_spec,
        out_shape=jax.ShapeDtypeStruct(out_shape, values.dtype),
        compiler_params=pltpu.CompilerParams(dimension_semantics=("arbitrary",)),
    )(order, flips, gates_bd, values)


def swap_major(values):
    amp_count = lax.axis_size("amp")
    wide, slabs, lanes = values.shape
    split = values.reshape(amp_count, wide // amp_count, slabs, lanes)
    swapped = lax.all_to_all(split, "amp", split_axis=0, concat_axis=0, tiled=True)
    return swapped.reshape(wide, slabs, lanes)


def all_sum(values, axes):
    count = lax.axis_size(axes)
    pieces = values.reshape(count, -1)
    gathered = lax.all_to_all(pieces, axes, split_axis=0, concat_axis=0, tiled=True)
    reduced = jnp.sum(gathered, axis=0, keepdims=True)
    spread = jnp.broadcast_to(reduced, pieces.shape)
    whole = lax.all_to_all(spread, axes, split_axis=0, concat_axis=0, tiled=True)
    return whole.reshape(values.shape)


def on_device(amplitudes, adjoint, gate_mats, gate_order, gate_window, swap_window):
    current = amplitudes
    gates_bd = block_diagonal(gate_mats)
    lanes_window = jnp.int32(0)
    for segment in range(SEGS):
        order = lax.dynamic_slice_in_dim(gate_order, segment * GATES, GATES)
        window = lax.dynamic_slice_in_dim(gate_window, segment * GATES, GATES)
        before = jnp.concatenate([lanes_window.reshape(1), window[:-1]])
        wanted = 1 - swap_window[segment] if segment < SEGS - 1 else jnp.int32(0)
        flips = jnp.concatenate([window != before, (window[-1] != wanted).reshape(1)])
        current = run_segment(
            current, gates_bd, order, flips.astype(jnp.int32),
            slab_in=segment == 0, slab_out=segment == SEGS - 1,
        )
        lanes_window = wanted
        if segment < SEGS - 1:
            current = swap_major(current)
    order = 4 * amplitudes.shape[2]
    owned_rows = order // lax.axis_size("grp")
    flattened = current.reshape(-1, order)
    adjoint_flat = adjoint.reshape(-1, order)
    partial_correlation = lax.dot_general(
        adjoint_flat, flattened, (((0,), (0,)), ((), ())), preferred_element_type=jnp.float32
    )
    summed = all_sum(partial_correlation, ("amp", "grp"))
    owned = lax.dynamic_slice_in_dim(summed, lax.axis_index("grp") * owned_rows, owned_rows, 0)
    gram = lax.dot_general(
        summed,
        summed,
        (((0,), (0,)), ((), ())),
        precision=lax.Precision.HIGHEST,
        preferred_element_type=jnp.float32,
    )
    scale = 1.0 / jnp.sqrt(jnp.trace(gram) / order + 1e-06)
    product = jnp.dot(owned, gram, precision=lax.Precision.HIGHEST)
    environment = jnp.sqrt(jnp.float32(order)) * (
        1.5 * scale * owned - 0.5 * scale * scale * scale * product
    )
    return (current, environment)


def solution(mesh):
    in_specs = (P(("amp", "grp"), None, None), P(("amp", "grp"), None, None), P(), P(), P(), P())
    out_specs = (P(("amp", "grp"), None, None), P("grp", None))
    return jax.shard_map(
        on_device, mesh=mesh, in_specs=in_specs, out_specs=out_specs, check_vma=False
    )
```

profile of v0, /device:TPU:1, one launch (start us, length us, event | category | flops | bytes accessed | tf_op | source)
XLA Modules:
  0.0 355.9 jit_solution(9749101440189668521)
XLA Ops:
  0.7 0.9 fusion.7
  1.5 1.4 fusion.8
  3.0 1.4 fusion.10
  6.3 1.4 copy.11
  7.7 2.0 fusion.2.gates_ref
  9.7 0.6 fusion.9
  11.0 0.7 add_convert_fusion.3.flip_ref
  11.7 18.5 %shard_map.77 = bf16[128,128,128]{2,1,0:T(8,128)(2,1)} custom-call(s32[5]{0:T(128)} %get-tuple-element.14.order_ref, s32[6]{0:T(128)} %add_convert_fusion.3.flip_ref, bf16[20,256,256]{2,1,0:T(8,128)(2,1)} %fusion.2.gates_ref, bf16[128,128,128]{2,1,0:T(8,128)(2,1)} %x_ref.1), custom_call_target="tpu_custom_call" | custom-call | tf_op jit(solution)/shard_map/pallas_call | solution.py:76
  30.2 12.7 %all-to-all-start = ((bf16[64,2,128,128]{3,2,1,0:T(8,128)(2,1)}), bf16[64,2,128,128]{3,2,1,0:T(8,128)(2,1)}, u32[]{:S(2)}, u32[]{:S(2)}) async-start(bf16[64,2,128,128]{3,2,1,0:T(8,128)(2,1)} %bitcast.16), calls=%async_computation | async-start | bytes 8388608 | tf_op jit(solution)/shard_map/all_to_all | solution.py:88
  43.4 0.6 add_convert_fusion.2.flip_ref
  44.0 51.5 %all-to-all-done = bf16[64,2,128,128]{3,2,1,0:T(8,128)(2,1)} async-done(((bf16[64,2,128,128]{3,2,1,0:T(8,128)(2,1)}), bf16[64,2,128,128]{3,2,1,0:T(8,128)(2,1)}, u32[]{:S(2)}, u32[]{:S(2)}) %all-to-all-start) | async-done | bytes 4194336 | tf_op jit(solution)/shard_map/all_to_all | solution.py:88
  95.5 17.8 %shard_map.78 = bf16[128,128,128]{2,1,0:T(8,128)(2,1)} custom-call(s32[5]{0:T(128)} %get-tuple-element.17.order_ref, s32[6]{0:T(128)} %add_convert_fusion.2.flip_ref, bf16[20,256,256]{2,1,0:T(8,128)(2,1)} %fusion.2.gates_ref, bf16[128,128,128]{2,1,0:T(8,128)(2,1)} %bitcast.2.x_ref), custom_call_target="tpu_custom_call" | custom-call | tf_op jit(solution)/shard_map/pallas_call | solution.py:76
  113.3 10.8 %all-to-all-start.1 = ((bf16[64,2,128,128]{3,2,1,0:T(8,128)(2,1)}), bf16[64,2,128,128]{3,2,1,0:T(8,128)(2,1)}, u32[]{:S(2)}, u32[]{:S(2)}) async-start(bf16[64,2,128,128]{3,2,1,0:T(8,128)(2,1)} %bitcast.15), calls=%async_computation.1 | async-start | bytes 8388608 | tf_op jit(solution)/shard_map/all_to_all | solution.py:88
  124.7 0.6 add_convert_fusion.1.flip_ref
  125.3 51.4 %all-to-all-done.1 = bf16[64,2,128,128]{3,2,1,0:T(8,128)(2,1)} async-done(((bf16[64,2,128,128]{3,2,1,0:T(8,128)(2,1)}), bf16[64,2,128,128]{3,2,1,0:T(8,128)(2,1)}, u32[]{:S(2)}, u32[]{:S(2)}) %all-to-all-start.1) | async-done | bytes 4194336 | tf_op jit(solution)/shard_map/all_to_all | solution.py:88
  176.7 19.1 %shard_map.79 = bf16[128,128,128]{2,1,0:T(8,128)(2,1)} custom-call(s32[5]{0:T(128)} %get-tuple-element.15.order_ref, s32[6]{0:T(128)} %add_convert_fusion.1.flip_ref, bf16[20,256,256]{2,1,0:T(8,128)(2,1)} %fusion.2.gates_ref, bf16[128,128,128]{2,1,0:T(8,128)(2,1)} %bitcast.4.x_ref), custom_call_target="tpu_custom_call" | custom-call | tf_op jit(solution)/shard_map/pallas_call | solution.py:76
  195.8 10.8 %all-to-all-start.2 = ((bf16[64,2,128,128]{3,2,1,0:T(8,128)(2,1)}), bf16[64,2,128,128]{3,2,1,0:T(8,128)(2,1)}, u32[]{:S(2)}, u32[]{:S(2)}) async-start(bf16[64,2,128,128]{3,2,1,0:T(8,128)(2,1)} %bitcast.14), calls=%async_computation.2 | async-start | bytes 8388608 | tf_op jit(solution)/shard_map/all_to_all | solution.py:88
  207.2 7.6 %reshape.74 = bf16[4096,512]{1,0:T(8,128)(2,1)} reshape(bf16[128,128,128]{2,1,0:T(8,128)(2,1)} %param.7) | data formatting | bytes 8388608 | tf_op jit(solution)/shard_map/reshape | solution.py:122
  214.8 0.6 add_convert_fusion.flip_ref
  215.4 43.8 %all-to-all-done.2 = bf16[64,2,128,128]{3,2,1,0:T(8,128)(2,1)} async-done(((bf16[64,2,128,128]{3,2,1,0:T(8,128)(2,1)}), bf16[64,2,128,128]{3,2,1,0:T(8,128)(2,1)}, u32[]{:S(2)}, u32[]{:S(2)}) %all-to-all-start.2) | async-done | bytes 4194336 | tf_op jit(solution)/shard_map/all_to_all | solution.py:88
  259.2 19.9 %shard_map.80 = bf16[128,128,128]{2,1,0:T(8,128)(2,1)} custom-call(s32[5]{0:T(128)} %get-tuple-element.16.order_ref, s32[6]{0:T(128)} %add_convert_fusion.flip_ref, bf16[20,256,256]{2,1,0:T(8,128)(2,1)} %fusion.2.gates_ref, bf16[128,128,128]{2,1,0:T(8,128)(2,1)} %bitcast.6.x_ref), custom_call_target="tpu_custom_call" | custom-call | tf_op jit(solution)/shard_map/pallas_call | solution.py:76
  279.1 7.5 %reshape.73 = bf16[4096,512]{1,0:T(8,128)(2,1)} reshape(bf16[128,128,128]{2,1,0:T(8,128)(2,1)} %shard_map.80) | data formatting | bytes 8388608 | tf_op jit(solution)/shard_map/reshape | solution.py:121
  286.6 5.8 %convolution_bitcast_fusion = f32[512,512]{0,1:T(8,128)S(1)} fusion(bf16[4096,512]{1,0:T(8,128)(2,1)} %reshape.73, bf16[4096,512]{1,0:T(8,128)(2,1)} %reshape.74), kind=kOutput, calls=%fused_computation.5 | convolution fusion | flops 2147483648 | bytes 9437184 | tf_op jit(solution)/shard_map/dot_general | solution.py:123
  292.8 1.2 all_to_all.25
  294.0 28.4 %all_to_all.31 = f32[128,1,2048]{2,1,0:T(1,128)S(1)} all-to-all(f32[128,1,2048]{2,1,0:T(1,128)S(1)} %all_to_all.25), channel_id=1, replica_groups=mesh['amp'=64,'grp'=2] {'amp','grp'}, dimensions={0} | all-to-all | bytes 2097152 | tf_op jit(solution)/shard_map/all_to_all | solution.py:95
  322.4 0.6 reduce_sum.19
  323.0 1.5 broadcast_in_dim.5
  324.5 5.2 %all-to-all-start.4 = ((f32[128,1,2048]{2,1,0:T(1,128)}), f32[128,1,2048]{2,1,0:T(1,128)S(1)}, u32[]{:S(2)}, u32[]{:S(2)}) async-start(f32[128,1,2048]{2,1,0:T(1,128)} %broadcast_in_dim.5), calls=%async_computation.4 | async-start | bytes 2097152 | tf_op jit(solution)/shard_map/all_to_all | solution.py:98
  329.7 18.4 %all-to-all-done.4 = f32[128,1,2048]{2,1,0:T(1,128)S(1)} async-done(((f32[128,1,2048]{2,1,0:T(1,128)}), f32[128,1,2048]{2,1,0:T(1,128)S(1)}, u32[]{:S(2)}, u32[]{:S(2)}) %all-to-all-start.4) | async-done | bytes 1048608 | tf_op jit(solution)/shard_map/all_to_all | solution.py:98
  348.1 2.5 reduce.1
  350.9 2.4 select_reduce_fusion
  354.0 1.9 fusion.4
  (7 shorter events, 0.7 us)
Async XLA Ops:
  0.6 10.3 %copy-start = (s32[20]{0:T(128)S(1)}, s32[20]{0:T(128)}, u32[]{:S(2)}) copy-start(s32[20]{0:T(128)} %param.10) | copy-start | bytes 244
  0.6 9.0 %copy-start.1 = (s32[20]{0:T(128)S(1)}, s32[20]{0:T(128)}, u32[]{:S(2)}) copy-start(s32[20]{0:T(128)} %param.9) | copy-start | bytes 244
  30.2 65.3 %all-to-all-start = ((bf16[64,2,128,128]{3,2,1,0:T(8,128)(2,1)}), bf16[64,2,128,128]{3,2,1,0:T(8,128)(2,1)}, u32[]{:S(2)}, u32[]{:S(2)}) async-start(bf16[64,2,128,128]{3,2,1,0:T(8,128)(2,1)} %bitcast.16), calls=%async_computation | async-start | bytes 8388608 | tf_op jit(solution)/shard_map/all_to_all | solution.py:88
  113.3 63.4 %all-to-all-start.1 = ((bf16[64,2,128,128]{3,2,1,0:T(8,128)(2,1)}), bf16[64,2,128,128]{3,2,1,0:T(8,128)(2,1)}, u32[]{:S(2)}, u32[]{:S(2)}) async-start(bf16[64,2,128,128]{3,2,1,0:T(8,128)(2,1)} %bitcast.15), calls=%async_computation.1 | async-start | bytes 8388608 | tf_op jit(solution)/shard_map/all_to_all | solution.py:88
  195.8 63.4 %all-to-all-start.2 = ((bf16[64,2,128,128]{3,2,1,0:T(8,128)(2,1)}), bf16[64,2,128,128]{3,2,1,0:T(8,128)(2,1)}, u32[]{:S(2)}, u32[]{:S(2)}) async-start(bf16[64,2,128,128]{3,2,1,0:T(8,128)(2,1)} %bitcast.14), calls=%async_computation.2 | async-start | bytes 8388608 | tf_op jit(solution)/shard_map/all_to_all | solution.py:88
  324.5 23.6 %all-to-all-start.4 = ((f32[128,1,2048]{2,1,0:T(1,128)}), f32[128,1,2048]{2,1,0:T(1,128)S(1)}, u32[]{:S(2)}, u32[]{:S(2)}) async-start(f32[128,1,2048]{2,1,0:T(1,128)} %broadcast_in_dim.5), calls=%async_computation.4 | async-start | bytes 2097152 | tf_op jit(solution)/shard_map/all_to_all | solution.py:98
where the time goes:
time: 356 us
  waiting for transfers between devices  165 us (46%)
  Pallas kernels  75.3 us (21%)
  starting transfers between devices  39.4 us (11%)
  blocking collectives  28.4 us (8%)
  local copies, waits for them, and re-layouts  24.3 us (7%)
  matrix products  10.1 us (3%)
  other arithmetic  7.57 us (2%)
  between operations  5.77 us (2%)
    all_to_all x3, waiting for transfers between devices, swap_major(): lax.all_to_all(split, 'amp', split_axis=0, concat_axis=0, tiled=True)  147 us
    pallas_call x4, Pallas kernels, run_segment(): pl.pallas_call(make_kernel(slab_in, slab_out), grid_spec=grid_spec, out_s...  75.3 us
    all_to_all x3, starting transfers between devices, swap_major(): lax.all_to_all(split, 'amp', split_axis=0, concat_axis=0, tiled=True)  34.2 us
    all_to_all x1, blocking collectives, all_sum(): lax.all_to_all(pieces, axes, split_axis=0, concat_axis=0, tiled=True)  28.4 us
    all_to_all x1, waiting for transfers between devices, all_sum(): lax.all_to_all(spread, axes, split_axis=0, concat_axis=0, tiled=True)  18.4 us
    reshape x1, local copies, waits for them, and re-layouts, on_device(): adjoint_flat = adjoint.reshape(-1, order)  7.57 us
    reshape x1, local copies, waits for them, and re-layouts, on_device(): flattened = current.reshape(-1, order)  7.51 us
  transfers between devices with their start and end apart: 4, of which 4 were waited for; matrix products, arithmetic and copies ran while one was open for 3% of the time, Pallas kernels for 0%

commit v1 on v0

--- a/solution.py
+++ b/solution.py
@@ -91,12 +91,12 @@
 
 def all_sum(values, axes):
     count = lax.axis_size(axes)
-    pieces = values.reshape(count, -1)
+    pieces = values.reshape(count, -1).astype(jnp.bfloat16)
     gathered = lax.all_to_all(pieces, axes, split_axis=0, concat_axis=0, tiled=True)
-    reduced = jnp.sum(gathered, axis=0, keepdims=True)
-    spread = jnp.broadcast_to(reduced, pieces.shape)
+    reduced = jnp.sum(gathered.astype(jnp.float32), axis=0, keepdims=True)
+    spread = jnp.broadcast_to(reduced.astype(jnp.bfloat16), pieces.shape)
     whole = lax.all_to_all(spread, axes, split_axis=0, concat_axis=0, tiled=True)
-    return whole.reshape(values.shape)
+    return whole.reshape(values.shape).astype(jnp.float32)
 
 
 def on_device(amplitudes, adjoint, gate_mats, gate_order, gate_window, swap_window):

time: 356 us -> 349 us (0.980)
  other arithmetic: 7.57 us -> 15.8 us
  Pallas kernels: 75.3 us -> 70.1 us
  blocking collectives: 28.4 us -> 23.3 us
  waiting for transfers between devices: 165 us -> 160 us
    pallas_call x4, Pallas kernels: 75.3 us -> 70.1 us  [run_segment(): pl.pallas_call(make_kernel(slab_in, slab_out), grid_spec=grid_spec, out_s...]
    all_to_all x1, waiting for transfers between devices: 18.4 us -> 13.2 us  [all_sum(): lax.all_to_all(spread, axes, split_axis=0, concat_axis=0, tiled=True)]
    all_to_all x1, blocking collectives: 28.4 us -> 23.3 us  [all_sum(): lax.all_to_all(pieces, axes, split_axis=0, concat_axis=0, tiled=True)]
    broadcast_in_dim x0 -> x1, other arithmetic: none -> 3.71 us  [all_sum(): spread = jnp.broadcast_to(reduced.astype(jnp.bfloat16), pieces.shape)]
    convert_element_type x0 -> x1, other arithmetic: none -> 3.7 us  [all_sum(): pieces = values.reshape(count, -1).astype(jnp.bfloat16)]
where the time goes in v1:
time: 349 us; the launch traced here: 348 us
  waiting for transfers between devices  160 us (46%)
  Pallas kernels  70.1 us (20%)
  starting transfers between devices  39.1 us (11%)
  local copies, waits for them, and re-layouts  25.2 us (7%)
  blocking collectives  23.3 us (7%)
  other arithmetic  15.8 us (5%)
  matrix products  8.36 us (2%)
  between operations  5.87 us (2%)
    all_to_all x3, waiting for transfers between devices, swap_major(): lax.all_to_all(split, 'amp', split_axis=0, concat_axis=0, tiled=True)  147 us
    pallas_call x4, Pallas kernels, run_segment(): pl.pallas_call(make_kernel(slab_in, slab_out), grid_spec=grid_spec, out_s...  70.1 us
    all_to_all x3, starting transfers between devices, swap_major(): lax.all_to_all(split, 'amp', split_axis=0, concat_axis=0, tiled=True)  34.2 us
    all_to_all x1, blocking collectives, all_sum(): lax.all_to_all(pieces, axes, split_axis=0, concat_axis=0, tiled=True)  23.3 us
    all_to_all x1, waiting for transfers between devices, all_sum(): lax.all_to_all(spread, axes, split_axis=0, concat_axis=0, tiled=True)  13.2 us
    reshape x1, local copies, waits for them, and re-layouts, on_device(): adjoint_flat = adjoint.reshape(-1, order)  7.54 us
    reshape x1, local copies, waits for them, and re-layouts, on_device(): flattened = current.reshape(-1, order)  7.52 us
  transfers between devices with their start and end apart: 4, of which 4 were waited for; matrix products, arithmetic and copies ran while one was open for 3% of the time, Pallas kernels for 0%

profile of v1, /device:TPU:1, one launch (start us, length us, event | category | flops | bytes accessed | tf_op | source)
XLA Modules:
  0.0 347.6 jit_solution(5771366156945518596)
XLA Ops:
  0.7 0.9 fusion.8
  1.5 1.5 fusion.9
  3.0 1.4 fusion.11
  6.4 1.4 copy.14
  7.8 1.9 fusion.2.gates_ref
  9.7 0.7 fusion.10
  11.1 0.6 add_convert_fusion.3.flip_ref
  11.7 19.8 %shard_map.77 = bf16[128,128,128]{2,1,0:T(8,128)(2,1)} custom-call(s32[5]{0:T(128)} %get-tuple-element.14.order_ref, s32[6]{0:T(128)} %add_convert_fusion.3.flip_ref, bf16[20,256,256]{2,1,0:T(8,128)(2,1)} %fusion.2.gates_ref, bf16[128,128,128]{2,1,0:T(8,128)(2,1)} %x_ref.1), custom_call_target="tpu_custom_call" | custom-call | tf_op jit(solution)/shard_map/pallas_call | solution.py:76
  31.5 12.6 %all-to-all-start = ((bf16[64,2,128,128]{3,2,1,0:T(8,128)(2,1)}), bf16[64,2,128,128]{3,2,1,0:T(8,128)(2,1)}, u32[]{:S(2)}, u32[]{:S(2)}) async-start(bf16[64,2,128,128]{3,2,1,0:T(8,128)(2,1)} %bitcast.16), calls=%async_computation | async-start | bytes 8388608 | tf_op jit(solution)/shard_map/all_to_all | solution.py:88
  44.6 0.6 add_convert_fusion.2.flip_ref
  45.2 51.5 %all-to-all-done = bf16[64,2,128,128]{3,2,1,0:T(8,128)(2,1)} async-done(((bf16[64,2,128,128]{3,2,1,0:T(8,128)(2,1)}), bf16[64,2,128,128]{3,2,1,0:T(8,128)(2,1)}, u32[]{:S(2)}, u32[]{:S(2)}) %all-to-all-start) | async-done | bytes 4194336 | tf_op jit(solution)/shard_map/all_to_all | solution.py:88
  96.7 17.8 %shard_map.78 = bf16[128,128,128]{2,1,0:T(8,128)(2,1)} custom-call(s32[5]{0:T(128)} %get-tuple-element.17.order_ref, s32[6]{0:T(128)} %add_convert_fusion.2.flip_ref, bf16[20,256,256]{2,1,0:T(8,128)(2,1)} %fusion.2.gates_ref, bf16[128,128,128]{2,1,0:T(8,128)(2,1)} %bitcast.2.x_ref), custom_call_target="tpu_custom_call" | custom-call | tf_op jit(solution)/shard_map/pallas_call | solution.py:76
  114.5 10.8 %all-to-all-start.1 = ((bf16[64,2,128,128]{3,2,1,0:T(8,128)(2,1)}), bf16[64,2,128,128]{3,2,1,0:T(8,128)(2,1)}, u32[]{:S(2)}, u32[]{:S(2)}) async-start(bf16[64,2,128,128]{3,2,1,0:T(8,128)(2,1)} %bitcast.15), calls=%async_computation.1 | async-start | bytes 8388608 | tf_op jit(solution)/shard_map/all_to_all | solution.py:88
  125.8 0.6 add_convert_fusion.1.flip_ref
  126.4 51.4 %all-to-all-done.1 = bf16[64,2,128,128]{3,2,1,0:T(8,128)(2,1)} async-done(((bf16[64,2,128,128]{3,2,1,0:T(8,128)(2,1)}), bf16[64,2,128,128]{3,2,1,0:T(8,128)(2,1)}, u32[]{:S(2)}, u32[]{:S(2)}) %all-to-all-start.1) | async-done | bytes 4194336 | tf_op jit(solution)/shard_map/all_to_all | solution.py:88
  177.9 16.6 %shard_map.79 = bf16[128,128,128]{2,1,0:T(8,128)(2,1)} custom-call(s32[5]{0:T(128)} %get-tuple-element.15.order_ref, s32[6]{0:T(128)} %add_convert_fusion.1.flip_ref, bf16[20,256,256]{2,1,0:T(8,128)(2,1)} %fusion.2.gates_ref, bf16[128,128,128]{2,1,0:T(8,128)(2,1)} %bitcast.4.x_ref), custom_call_target="tpu_custom_call" | custom-call | tf_op jit(solution)/shard_map/pallas_call | solution.py:76
  194.4 10.8 %all-to-all-start.2 = ((bf16[64,2,128,128]{3,2,1,0:T(8,128)(2,1)}), bf16[64,2,128,128]{3,2,1,0:T(8,128)(2,1)}, u32[]{:S(2)}, u32[]{:S(2)}) async-start(bf16[64,2,128,128]{3,2,1,0:T(8,128)(2,1)} %bitcast.14), calls=%async_computation.2 | async-start | bytes 8388608 | tf_op jit(solution)/shard_map/all_to_all | solution.py:88
  205.9 7.5 %reshape.88 = bf16[4096,512]{1,0:T(8,128)(2,1)} reshape(bf16[128,128,128]{2,1,0:T(8,128)(2,1)} %param.7) | data formatting | bytes 8388608 | tf_op jit(solution)/shard_map/reshape | solution.py:122
  214.1 43.8 %all-to-all-done.2 = bf16[64,2,128,128]{3,2,1,0:T(8,128)(2,1)} async-done(((bf16[64,2,128,128]{3,2,1,0:T(8,128)(2,1)}), bf16[64,2,128,128]{3,2,1,0:T(8,128)(2,1)}, u32[]{:S(2)}, u32[]{:S(2)}) %all-to-all-start.2) | async-done | bytes 4194336 | tf_op jit(solution)/shard_map/all_to_all | solution.py:88
  257.8 16.0 %shard_map.80 = bf16[128,128,128]{2,1,0:T(8,128)(2,1)} custom-call(s32[5]{0:T(128)} %get-tuple-element.16.order_ref, s32[6]{0:T(128)} %add_convert_fusion.flip_ref, bf16[20,256,256]{2,1,0:T(8,128)(2,1)} %fusion.2.gates_ref, bf16[128,128,128]{2,1,0:T(8,128)(2,1)} %bitcast.6.x_ref), custom_call_target="tpu_custom_call" | custom-call | tf_op jit(solution)/shard_map/pallas_call | solution.py:76
  273.8 7.5 %reshape.87 = bf16[4096,512]{1,0:T(8,128)(2,1)} reshape(bf16[128,128,128]{2,1,0:T(8,128)(2,1)} %shard_map.80) | data formatting | bytes 8388608 | tf_op jit(solution)/shard_map/reshape | solution.py:121
  281.3 5.8 %fusion.5 = bf16[512,512]{0,1:T(8,128)(2,1)S(1)} fusion(bf16[4096,512]{1,0:T(8,128)(2,1)} %reshape.87, bf16[4096,512]{1,0:T(8,128)(2,1)} %reshape.88), kind=kOutput, calls=%fused_computation.9 | convolution fusion | flops 2147745792 | bytes 8912896 | tf_op jit(solution)/shard_map/dot_general | solution.py:123
  288.2 3.7 %reduce.3 = bf16[128,2048]{1,0:T(8,128)(2,1)S(1)} reduce(bf16[128,1,2048]{2,1,0:T(2,128)(2,1)S(1)} %convert_element_type.46, bf16[]{:T(256)} %broadcast.15), dimensions={1}, to_apply=%convert_element_type.46.reduce_sub_computation | reduce | bytes 1048578 | tf_op jit(solution)/shard_map/convert_element_type | solution.py:94
  292.3 23.3 %all_to_all.27 = bf16[128,2,1024]{2,1,0:T(2,128)(2,1)S(1)} all-to-all(bf16[128,2,1024]{2,1,0:T(2,128)(2,1)S(1)} %reshape.91), channel_id=1, replica_groups=mesh['amp'=64,'grp'=2] {'amp','grp'}, dimensions={0} | all-to-all | bytes 1048576 | tf_op jit(solution)/shard_map/all_to_all | solution.py:95
  316.0 0.9 reduce_sum.22
  317.5 3.7 %reduce.4 = bf16[128,2048]{1,0:T(8,128)(2,1)S(1)} reduce(bf16[128,1,2048]{2,1,0:T(2,128)(2,1)S(1)} %broadcast_in_dim.5, bf16[]{:T(256)} %broadcast.15), dimensions={1}, to_apply=%broadcast_in_dim.5.reduce_sub_computation | reduce | bytes 1048578 | tf_op jit(solution)/shard_map/broadcast_in_dim | solution.py:97
  321.2 1.2 reshape.93
  322.4 4.9 %all-to-all-start.4 = ((bf16[128,2,1024]{2,1,0:T(2,128)(2,1)}), bf16[128,2,1024]{2,1,0:T(2,128)(2,1)S(1)}, u32[]{:S(2)}, u32[]{:S(2)}) async-start(bf16[128,2,1024]{2,1,0:T(2,128)(2,1)} %reshape.93), calls=%async_computation.4 | async-start | bytes 1048576 | tf_op jit(solution)/shard_map/all_to_all | solution.py:98
  327.3 13.2 %all-to-all-done.4 = bf16[128,2,1024]{2,1,0:T(2,128)(2,1)S(1)} async-done(((bf16[128,2,1024]{2,1,0:T(2,128)(2,1)}), bf16[128,2,1024]{2,1,0:T(2,128)(2,1)S(1)}, u32[]{:S(2)}, u32[]{:S(2)}) %all-to-all-start.4) | async-done | bytes 524320 | tf_op jit(solution)/shard_map/all_to_all | solution.py:98
  340.9 3.1 reduce.2
  344.3 1.1 select_reduce_fusion
  346.1 1.5 fusion.4
  (14 shorter events, 3.8 us)
Async XLA Ops:
  0.6 10.4 %copy-start = (s32[20]{0:T(128)S(1)}, s32[20]{0:T(128)}, u32[]{:S(2)}) copy-start(s32[20]{0:T(128)} %param.10) | copy-start | bytes 244
  0.6 9.1 %copy-start.1 = (s32[20]{0:T(128)S(1)}, s32[20]{0:T(128)}, u32[]{:S(2)}) copy-start(s32[20]{0:T(128)} %param.9) | copy-start | bytes 244
  31.5 65.2 %all-to-all-start = ((bf16[64,2,128,128]{3,2,1,0:T(8,128)(2,1)}), bf16[64,2,128,128]{3,2,1,0:T(8,128)(2,1)}, u32[]{:S(2)}, u32[]{:S(2)}) async-start(bf16[64,2,128,128]{3,2,1,0:T(8,128)(2,1)} %bitcast.16), calls=%async_computation | async-start | bytes 8388608 | tf_op jit(solution)/shard_map/all_to_all | solution.py:88
  114.5 63.4 %all-to-all-start.1 = ((bf16[64,2,128,128]{3,2,1,0:T(8,128)(2,1)}), bf16[64,2,128,128]{3,2,1,0:T(8,128)(2,1)}, u32[]{:S(2)}, u32[]{:S(2)}) async-start(bf16[64,2,128,128]{3,2,1,0:T(8,128)(2,1)} %bitcast.15), calls=%async_computation.1 | async-start | bytes 8388608 | tf_op jit(solution)/shard_map/all_to_all | solution.py:88
  194.4 63.4 %all-to-all-start.2 = ((bf16[64,2,128,128]{3,2,1,0:T(8,128)(2,1)}), bf16[64,2,128,128]{3,2,1,0:T(8,128)(2,1)}, u32[]{:S(2)}, u32[]{:S(2)}) async-start(bf16[64,2,128,128]{3,2,1,0:T(8,128)(2,1)} %bitcast.14), calls=%async_computation.2 | async-start | bytes 8388608 | tf_op jit(solution)/shard_map/all_to_all | solution.py:88
  322.4 18.1 %all-to-all-start.4 = ((bf16[128,2,1024]{2,1,0:T(2,128)(2,1)}), bf16[128,2,1024]{2,1,0:T(2,128)(2,1)S(1)}, u32[]{:S(2)}, u32[]{:S(2)}) async-start(bf16[128,2,1024]{2,1,0:T(2,128)(2,1)} %reshape.93), calls=%async_computation.4 | async-start | bytes 1048576 | tf_op jit(solution)/shard_map/all_to_all | solution.py:98

commit v2 on v1

--- a/solution.py
+++ b/solution.py
@@ -8,18 +8,30 @@
 SEGS = 4
 GATES = 5
 BLOCK = 32
+CHUNKS = 2
 
 
-def make_kernel(slab_in, slab_out):
-    def kernel(order_ref, flip_ref, gates_ref, x_ref, o_ref, held):
+def make_kernel(slab_in, slab_out, sources, blocks_per_source):
+    def kernel(order_ref, flip_ref, gates_ref, *refs):
+        x_refs, o_ref, held = refs[:sources], refs[sources], refs[sources + 1]
         half, wide, pair = held.shape
         lanes = pair // 2
-        if slab_in:
-            slabs = x_ref[...]
+
+        def load(x_ref):
+            if slab_in:
+                slabs = x_ref[...]
+            else:
+                slabs = jnp.swapaxes(x_ref[...], 0, 1)
+            held[:, :, :lanes] = slabs[:half]
+            held[:, :, lanes:] = slabs[half:]
+
+        if sources == 1:
+            load(x_refs[0])
         else:
-            slabs = jnp.swapaxes(x_ref[...], 0, 1)
-        held[:, :, :lanes] = slabs[:half]
-        held[:, :, lanes:] = slabs[half:]
+            step = pl.program_id(0)
+            for index, x_ref in enumerate(x_refs):
+                inside = (step >= index * blocks_per_source) & (step < (index + 1) * blocks_per_source)
+                pl.when(inside)(lambda x_ref=x_ref: load(x_ref))
 
         def flip():
             held[:, :, :lanes] = jnp.swapaxes(held[:, :, :lanes], 1, 2)
@@ -56,29 +68,40 @@
     return jnp.concatenate([top, bottom], axis=1)
 
 
-def run_segment(values, gates_bd, order, flips, slab_in, slab_out):
+def run_segment(sources, gates_bd, order, flips, slab_in, slab_out, slabs, offset=0):
     wide = gates_bd.shape[1] // 2
-    slabs = values.shape[0] if slab_in else values.shape[1]
-    lanes = values.shape[2]
-    slab_spec = pl.BlockSpec((BLOCK, wide, lanes), lambda i, o, f: (i, 0, 0))
-    major_spec = pl.BlockSpec((wide, BLOCK, lanes), lambda i, o, f: (0, i, 0))
-    out_shape = (slabs, wide, lanes) if slab_out else (wide, slabs, lanes)
+    lanes = sources[0].shape[2]
+    blocks = slabs // BLOCK
+    per_source = blocks // len(sources)
+
+    def source_spec(index):
+        def pick(i, o, f):
+            local = jnp.clip(i - index * per_source, 0, per_source - 1) + offset
+            return (local, 0, 0) if slab_in else (0, local, 0)
+
+        shape = (BLOCK, wide, lanes) if slab_in else (wide, BLOCK, lanes)
+        return pl.BlockSpec(shape, pick)
+
+    if slab_out:
+        out_spec = pl.BlockSpec((BLOCK, wide, lanes), lambda i, o, f: (i, 0, 0))
+        out_shape = (slabs, wide, lanes)
+    else:
+        out_spec = pl.BlockSpec((wide, BLOCK, lanes), lambda i, o, f: (0, i, 0))
+        out_shape = (wide, slabs, lanes)
     grid_spec = pltpu.PrefetchScalarGridSpec(
         num_scalar_prefetch=2,
-        grid=(slabs // BLOCK,),
-        in_specs=[
-            pl.BlockSpec(gates_bd.shape, lambda i, o, f: (0, 0, 0)),
-            slab_spec if slab_in else major_spec,
-        ],
-        out_specs=slab_spec if slab_out else major_spec,
+        grid=(blocks,),
+        in_specs=[pl.BlockSpec(gates_bd.shape, lambda i, o, f: (0, 0, 0))]
+        + [source_spec(index) for index in range(len(sources))],
+        out_specs=out_spec,
         scratch_shapes=[pltpu.VMEM((BLOCK // 2, wide, 2 * lanes), jnp.bfloat16)],
     )
     return pl.pallas_call(
-        make_kernel(slab_in, slab_out),
+        make_kernel(slab_in, slab_out, len(sources), per_source),
         grid_spec=grid_spec,
-        out_shape=jax.ShapeDtypeStruct(out_shape, values.dtype),
+        out_shape=jax.ShapeDtypeStruct(out_shape, sources[0].dtype),
         compiler_params=pltpu.CompilerParams(dimension_semantics=("arbitrary",)),
-    )(order, flips, gates_bd, values)
+    )(order, flips, gates_bd, *sources)
 
 
 def swap_major(values):
@@ -100,22 +123,30 @@
 
 
 def on_device(amplitudes, adjoint, gate_mats, gate_order, gate_window, swap_window):
-    current = amplitudes
     gates_bd = block_diagonal(gate_mats)
+    slabs = amplitudes.shape[0]
+    chunk = slabs // CHUNKS
     lanes_window = jnp.int32(0)
+    chunks = None
     for segment in range(SEGS):
         order = lax.dynamic_slice_in_dim(gate_order, segment * GATES, GATES)
         window = lax.dynamic_slice_in_dim(gate_window, segment * GATES, GATES)
         before = jnp.concatenate([lanes_window.reshape(1), window[:-1]])
         wanted = 1 - swap_window[segment] if segment < SEGS - 1 else jnp.int32(0)
         flips = jnp.concatenate([window != before, (window[-1] != wanted).reshape(1)])
-        current = run_segment(
-            current, gates_bd, order, flips.astype(jnp.int32),
-            slab_in=segment == 0, slab_out=segment == SEGS - 1,
-        )
+        flips = flips.astype(jnp.int32)
         lanes_window = wanted
+        if segment == 0:
+            chunks = [
+                run_segment([amplitudes], gates_bd, order, flips, True, False, chunk, c * (chunk // BLOCK))
+                for c in range(CHUNKS)
+            ]
+        elif segment < SEGS - 1:
+            chunks = [run_segment([part], gates_bd, order, flips, False, False, chunk) for part in chunks]
+        else:
+            current = run_segment(chunks, gates_bd, order, flips, False, True, slabs)
         if segment < SEGS - 1:
-            current = swap_major(current)
+            chunks = [swap_major(part) for part in chunks]
     order = 4 * amplitudes.shape[2]
     owned_rows = order // lax.axis_size("grp")
     flattened = current.reshape(-1, order)

time: 349 us -> 349 us (level)
  waiting for transfers between devices: 160 us -> 125 us
  Pallas kernels: 70.1 us -> 89.8 us
  starting transfers between devices: 39.1 us -> 52.8 us
    all_to_all x3 -> x6, waiting for transfers between devices: 147 us -> 112 us  [swap_major(): lax.all_to_all(split, 'amp', split_axis=0, concat_axis=0, tiled=True)]
    pallas_call x4 -> x7, Pallas kernels: 70.1 us -> 89.8 us  [run_segment(): pl.pallas_call(make_kernel(slab_in, slab_out, len(sources), per_source),...]
    all_to_all x3 -> x6, starting transfers between devices: 34.2 us -> 47.9 us  [swap_major(): lax.all_to_all(split, 'amp', split_axis=0, concat_axis=0, tiled=True)]
  transfers between devices with their start and end apart: 4 -> 7, of which waited for: 4 -> 7; matrix products, arithmetic and copies ran while one was open for 3% -> 3% of each run, Pallas kernels for 0% -> 17%
where the time goes in v2:
time: 349 us; the launch traced here: 345 us
  waiting for transfers between devices  125 us (36%)
  Pallas kernels  89.8 us (26%)
  starting transfers between devices  52.8 us (15%)
  local copies, waits for them, and re-layouts  25.3 us (7%)
  blocking collectives  21.9 us (6%)
  other arithmetic  15.7 us (4%)
  matrix products  8.36 us (2%)
  between operations  6.29 us (2%)
    all_to_all x6, waiting for transfers between devices, swap_major(): lax.all_to_all(split, 'amp', split_axis=0, concat_axis=0, tiled=True)  112 us
    pallas_call x7, Pallas kernels, run_segment(): pl.pallas_call(make_kernel(slab_in, slab_out, len(sources), per_source),...  89.8 us
    all_to_all x6, starting transfers between devices, swap_major(): lax.all_to_all(split, 'amp', split_axis=0, concat_axis=0, tiled=True)  47.9 us
    all_to_all x1, blocking collectives, all_sum(): lax.all_to_all(pieces, axes, split_axis=0, concat_axis=0, tiled=True)  21.9 us
    all_to_all x1, waiting for transfers between devices, all_sum(): lax.all_to_all(spread, axes, split_axis=0, concat_axis=0, tiled=True)  13.2 us
    reshape x1, local copies, waits for them, and re-layouts, on_device(): flattened = current.reshape(-1, order)  7.6 us
    reshape x1, local copies, waits for them, and re-layouts, on_device(): adjoint_flat = adjoint.reshape(-1, order)  7.54 us
  transfers between devices with their start and end apart: 7, of which 7 were waited for; matrix products, arithmetic and copies ran while one was open for 3% of the time, Pallas kernels for 17%

profile of v2, /device:TPU:1, one launch (start us, length us, event | category | flops | bytes accessed | tf_op | source)
XLA Modules:
  0.0 345.1 jit_solution(11584857815549890020)
XLA Ops:
  1.5 1.5 fusion.9
  3.0 1.4 fusion.11
  7.7 1.9 fusion.2.gates_ref
  11.6 9.9 %shard_map.80 = bf16[128,64,128]{2,1,0:T(8,128)(2,1)} custom-call(s32[5]{0:T(128)} %get-tuple-element.14.order_ref, s32[6]{0:T(128)} %add_convert_fusion.3.flip_ref, bf16[20,256,256]{2,1,0:T(8,128)(2,1)} %fusion.2.gates_ref, bf16[128,128,128]{2,1,0:T(8,128)(2,1)} %refs_0_.3), custom_call_target="tpu_custom_call" | custom-call | tf_op jit(solution)/shard_map/pallas_call | solution.py:99
  21.6 12.4 %all-to-all-start.3 = ((bf16[64,2,64,128]{3,2,1,0:T(8,128)(2,1)}), bf16[64,2,64,128]{3,2,1,0:T(8,128)(2,1)S(1)}, u32[]{:S(2)}, u32[]{:S(2)}) async-start(bf16[64,2,64,128]{3,2,1,0:T(8,128)(2,1)} %bitcast.21), calls=%async_computation.3 | async-start | bytes 4194304 | tf_op jit(solution)/shard_map/all_to_all | solution.py:111
  34.0 9.8 %shard_map.77 = bf16[128,64,128]{2,1,0:T(8,128)(2,1)} custom-call(s32[5]{0:T(128)} %get-tuple-element.14.order_ref, s32[6]{0:T(128)} %add_convert_fusion.3.flip_ref, bf16[20,256,256]{2,1,0:T(8,128)(2,1)} %fusion.2.gates_ref, bf16[128,128,128]{2,1,0:T(8,128)(2,1)} %refs_0_.3), custom_call_target="tpu_custom_call" | custom-call | tf_op jit(solution)/shard_map/pallas_call | solution.py:99
  43.8 20.6 %all-to-all-done.3 = bf16[64,2,64,128]{3,2,1,0:T(8,128)(2,1)S(1)} async-done(((bf16[64,2,64,128]{3,2,1,0:T(8,128)(2,1)}), bf16[64,2,64,128]{3,2,1,0:T(8,128)(2,1)S(1)}, u32[]{:S(2)}, u32[]{:S(2)}) %all-to-all-start.3) | async-done | bytes 2097184 | tf_op jit(solution)/shard_map/all_to_all | solution.py:111
  64.5 5.1 %all-to-all-start = ((bf16[64,2,64,128]{3,2,1,0:T(8,128)(2,1)}), bf16[64,2,64,128]{3,2,1,0:T(8,128)(2,1)}, u32[]{:S(2)}, u32[]{:S(2)}) async-start(bf16[64,2,64,128]{3,2,1,0:T(8,128)(2,1)} %bitcast.20), calls=%async_computation | async-start | bytes 4194304 | tf_op jit(solution)/shard_map/all_to_all | solution.py:111
  70.8 12.8 %shard_map.81 = bf16[128,64,128]{2,1,0:T(8,128)(2,1)} custom-call(s32[5]{0:T(128)} %get-tuple-element.17.order_ref, s32[6]{0:T(128)} %add_convert_fusion.2.flip_ref, bf16[20,256,256]{2,1,0:T(8,128)(2,1)} %fusion.2.gates_ref, bf16[128,64,128]{2,1,0:T(8,128)(2,1)} %bitcast.23), custom_call_target="tpu_custom_call" | custom-call | tf_op jit(solution)/shard_map/pallas_call | solution.py:99
  83.6 16.4 %all-to-all-done = bf16[64,2,64,128]{3,2,1,0:T(8,128)(2,1)} async-done(((bf16[64,2,64,128]{3,2,1,0:T(8,128)(2,1)}), bf16[64,2,64,128]{3,2,1,0:T(8,128)(2,1)}, u32[]{:S(2)}, u32[]{:S(2)}) %all-to-all-start) | async-done | bytes 2097184 | tf_op jit(solution)/shard_map/all_to_all | solution.py:111
  100.0 4.9 %all-to-all-start.4 = ((bf16[64,2,64,128]{3,2,1,0:T(8,128)(2,1)}), bf16[64,2,64,128]{3,2,1,0:T(8,128)(2,1)S(1)}, u32[]{:S(2)}, u32[]{:S(2)}) async-start(bf16[64,2,64,128]{3,2,1,0:T(8,128)(2,1)} %bitcast.26), calls=%async_computation.4 | async-start | bytes 4194304 | tf_op jit(solution)/shard_map/all_to_all | solution.py:111
  105.0 12.7 %shard_map.78 = bf16[128,64,128]{2,1,0:T(8,128)(2,1)} custom-call(s32[5]{0:T(128)} %get-tuple-element.17.order_ref, s32[6]{0:T(128)} %add_convert_fusion.2.flip_ref, bf16[20,256,256]{2,1,0:T(8,128)(2,1)} %fusion.2.gates_ref, bf16[128,64,128]{2,1,0:T(8,128)(2,1)} %bitcast.2.refs_0_), custom_call_target="tpu_custom_call" | custom-call | tf_op jit(solution)/shard_map/pallas_call | solution.py:99
  117.6 17.8 %all-to-all-done.4 = bf16[64,2,64,128]{3,2,1,0:T(8,128)(2,1)S(1)} async-done(((bf16[64,2,64,128]{3,2,1,0:T(8,128)(2,1)}), bf16[64,2,64,128]{3,2,1,0:T(8,128)(2,1)S(1)}, u32[]{:S(2)}, u32[]{:S(2)}) %all-to-all-start.4) | async-done | bytes 2097184 | tf_op jit(solution)/shard_map/all_to_all | solution.py:111
  135.4 15.2 %all-to-all-start.1 = ((bf16[64,2,64,128]{3,2,1,0:T(8,128)(2,1)}), bf16[64,2,64,128]{3,2,1,0:T(8,128)(2,1)}, u32[]{:S(2)}, u32[]{:S(2)}) async-start(bf16[64,2,64,128]{3,2,1,0:T(8,128)(2,1)} %bitcast.25), calls=%async_computation.1 | async-start | bytes 4194304 | tf_op jit(solution)/shard_map/all_to_all | solution.py:111
  151.8 12.2 %shard_map.82 = bf16[128,64,128]{2,1,0:T(8,128)(2,1)} custom-call(s32[5]{0:T(128)} %get-tuple-element.15.order_ref, s32[6]{0:T(128)} %add_convert_fusion.1.flip_ref, bf16[20,256,256]{2,1,0:T(8,128)(2,1)} %fusion.2.gates_ref, bf16[128,64,128]{2,1,0:T(8,128)(2,1)} %bitcast.22), custom_call_target="tpu_custom_call" | custom-call | tf_op jit(solution)/shard_map/pallas_call | solution.py:99
  164.0 16.7 %all-to-all-done.1 = bf16[64,2,64,128]{3,2,1,0:T(8,128)(2,1)} async-done(((bf16[64,2,64,128]{3,2,1,0:T(8,128)(2,1)}), bf16[64,2,64,128]{3,2,1,0:T(8,128)(2,1)}, u32[]{:S(2)}, u32[]{:S(2)}) %all-to-all-start.1) | async-done | bytes 2097184 | tf_op jit(solution)/shard_map/all_to_all | solution.py:111
  180.8 5.1 %all-to-all-start.5 = ((bf16[64,2,64,128]{3,2,1,0:T(8,128)(2,1)}), bf16[64,2,64,128]{3,2,1,0:T(8,128)(2,1)S(1)}, u32[]{:S(2)}, u32[]{:S(2)}) async-start(bf16[64,2,64,128]{3,2,1,0:T(8,128)(2,1)} %bitcast.27), calls=%async_computation.5 | async-start | bytes 4194304 | tf_op jit(solution)/shard_map/all_to_all | solution.py:111
  185.9 12.1 %shard_map.79 = bf16[128,64,128]{2,1,0:T(8,128)(2,1)} custom-call(s32[5]{0:T(128)} %get-tuple-element.15.order_ref, s32[6]{0:T(128)} %add_convert_fusion.1.flip_ref, bf16[20,256,256]{2,1,0:T(8,128)(2,1)} %fusion.2.gates_ref, bf16[128,64,128]{2,1,0:T(8,128)(2,1)} %bitcast.4.refs_0_), custom_call_target="tpu_custom_call" | custom-call | tf_op jit(solution)/shard_map/pallas_call | solution.py:99
  198.0 18.4 %all-to-all-done.5 = bf16[64,2,64,128]{3,2,1,0:T(8,128)(2,1)S(1)} async-done(((bf16[64,2,64,128]{3,2,1,0:T(8,128)(2,1)}), bf16[64,2,64,128]{3,2,1,0:T(8,128)(2,1)S(1)}, u32[]{:S(2)}, u32[]{:S(2)}) %all-to-all-start.5) | async-done | bytes 2097184 | tf_op jit(solution)/shard_map/all_to_all | solution.py:111
  216.4 5.1 %all-to-all-start.2 = ((bf16[64,2,64,128]{3,2,1,0:T(8,128)(2,1)}), bf16[64,2,64,128]{3,2,1,0:T(8,128)(2,1)}, u32[]{:S(2)}, u32[]{:S(2)}) async-start(bf16[64,2,64,128]{3,2,1,0:T(8,128)(2,1)} %bitcast.24), calls=%async_computation.2 | async-start | bytes 4194304 | tf_op jit(solution)/shard_map/all_to_all | solution.py:111
  222.2 7.5 %reshape.112 = bf16[4096,512]{1,0:T(8,128)(2,1)} reshape(bf16[128,128,128]{2,1,0:T(8,128)(2,1)} %param.7) | data formatting | bytes 8388608 | tf_op jit(solution)/shard_map/reshape | solution.py:153
  230.3 21.6 %all-to-all-done.2 = bf16[64,2,64,128]{3,2,1,0:T(8,128)(2,1)} async-done(((bf16[64,2,64,128]{3,2,1,0:T(8,128)(2,1)}), bf16[64,2,64,128]{3,2,1,0:T(8,128)(2,1)}, u32[]{:S(2)}, u32[]{:S(2)}) %all-to-all-start.2) | async-done | bytes 2097184 | tf_op jit(solution)/shard_map/all_to_all | solution.py:111
  251.9 20.3 %shard_map.83 = bf16[128,128,128]{2,1,0:T(8,128)(2,1)} custom-call(s32[5]{0:T(128)} %get-tuple-element.16.order_ref, s32[6]{0:T(128)} %add_convert_fusion.flip_ref, bf16[20,256,256]{2,1,0:T(8,128)(2,1)} %fusion.2.gates_ref, bf16[128,64,128]{2,1,0:T(8,128)(2,1)} %bitcast.6.refs_0_, bf16[128,64,128]{2,1,0:T(8,128)(2,1)} %bitcast.28), custom_call_target="tpu_custom_call" | custom-call | tf_op jit(solution)/shard_map/pallas_call | solution.py:99
  272.2 7.6 %reshape.111 = bf16[4096,512]{1,0:T(8,128)(2,1)} reshape(bf16[128,128,128]{2,1,0:T(8,128)(2,1)} %shard_map.83) | data formatting | bytes 8388608 | tf_op jit(solution)/shard_map/reshape | solution.py:152
  279.8 5.8 %fusion.5 = bf16[512,512]{0,1:T(8,128)(2,1)S(1)} fusion(bf16[4096,512]{1,0:T(8,128)(2,1)} %reshape.111, bf16[4096,512]{1,0:T(8,128)(2,1)} %reshape.112), kind=kOutput, calls=%fused_computation.9 | convolution fusion | flops 2147745792 | bytes 8912896 | tf_op jit(solution)/shard_map/dot_general | solution.py:154
  286.7 3.7 %reduce.3 = bf16[128,2048]{1,0:T(8,128)(2,1)S(1)} reduce(bf16[128,1,2048]{2,1,0:T(2,128)(2,1)S(1)} %convert_element_type.46, bf16[]{:T(256)} %broadcast.15), dimensions={1}, to_apply=%convert_element_type.46.reduce_sub_computation | reduce | bytes 1048578 | tf_op jit(solution)/shard_map/convert_element_type | solution.py:117
  290.8 21.9 %all_to_all.42 = bf16[128,2,1024]{2,1,0:T(2,128)(2,1)S(1)} all-to-all(bf16[128,2,1024]{2,1,0:T(2,128)(2,1)S(1)} %reshape.115), channel_id=1, replica_groups=mesh['amp'=64,'grp'=2] {'amp','grp'}, dimensions={0} | all-to-all | bytes 1048576 | tf_op jit(solution)/shard_map/all_to_all | solution.py:118
  314.6 3.7 %reduce.4 = bf16[128,2048]{1,0:T(8,128)(2,1)S(1)} reduce(bf16[128,1,2048]{2,1,0:T(2,128)(2,1)S(1)} %broadcast_in_dim.5, bf16[]{:T(256)} %broadcast.15), dimensions={1}, to_apply=%broadcast_in_dim.5.reduce_sub_computation | reduce | bytes 1048578 | tf_op jit(solution)/shard_map/broadcast_in_dim | solution.py:120
  319.5 4.9 %all-to-all-start.7 = ((bf16[128,2,1024]{2,1,0:T(2,128)(2,1)}), bf16[128,2,1024]{2,1,0:T(2,128)(2,1)S(1)}, u32[]{:S(2)}, u32[]{:S(2)}) async-start(bf16[128,2,1024]{2,1,0:T(2,128)(2,1)} %reshape.117), calls=%async_computation.7 | async-start | bytes 1048576 | tf_op jit(solution)/shard_map/all_to_all | solution.py:121
  324.4 13.2 %all-to-all-done.7 = bf16[128,2,1024]{2,1,0:T(2,128)(2,1)S(1)} async-done(((bf16[128,2,1024]{2,1,0:T(2,128)(2,1)}), bf16[128,2,1024]{2,1,0:T(2,128)(2,1)S(1)}, u32[]{:S(2)}, u32[]{:S(2)}) %all-to-all-start.7) | async-done | bytes 524320 | tf_op jit(solution)/shard_map/all_to_all | solution.py:121
  338.1 3.1 reduce.2
  343.2 1.5 fusion.4
  (29 shorter events, 11.7 us)
Async XLA Ops:
  0.6 10.3 %copy-start.3 = (s32[20]{0:T(128)S(1)}, s32[20]{0:T(128)}, u32[]{:S(2)}) copy-start(s32[20]{0:T(128)} %param.10) | copy-start | bytes 244
  0.6 9.0 %copy-start.4 = (s32[20]{0:T(128)S(1)}, s32[20]{0:T(128)}, u32[]{:S(2)}) copy-start(s32[20]{0:T(128)} %param.9) | copy-start | bytes 244
  21.6 42.9 %all-to-all-start.3 = ((bf16[64,2,64,128]{3,2,1,0:T(8,128)(2,1)}), bf16[64,2,64,128]{3,2,1,0:T(8,128)(2,1)S(1)}, u32[]{:S(2)}, u32[]{:S(2)}) async-start(bf16[64,2,64,128]{3,2,1,0:T(8,128)(2,1)} %bitcast.21), calls=%async_computation.3 | async-start | bytes 4194304 | tf_op jit(solution)/shard_map/all_to_all | solution.py:111
  64.5 6.3 %copy-start.1 = (bf16[64,2,64,128]{3,2,1,0:T(8,128)(2,1)}, bf16[64,2,64,128]{3,2,1,0:T(8,128)(2,1)S(1)}, u32[]{:S(2)}) copy-start(bf16[64,2,64,128]{3,2,1,0:T(8,128)(2,1)S(1)} %all-to-all-done.3) | copy-start | bytes 6291460
  64.5 35.5 %all-to-all-start = ((bf16[64,2,64,128]{3,2,1,0:T(8,128)(2,1)}), bf16[64,2,64,128]{3,2,1,0:T(8,128)(2,1)}, u32[]{:S(2)}, u32[]{:S(2)}) async-start(bf16[64,2,64,128]{3,2,1,0:T(8,128)(2,1)} %bitcast.20), calls=%async_computation | async-start | bytes 4194304 | tf_op jit(solution)/shard_map/all_to_all | solution.py:111
  100.0 35.4 %all-to-all-start.4 = ((bf16[64,2,64,128]{3,2,1,0:T(8,128)(2,1)}), bf16[64,2,64,128]{3,2,1,0:T(8,128)(2,1)S(1)}, u32[]{:S(2)}, u32[]{:S(2)}) async-start(bf16[64,2,64,128]{3,2,1,0:T(8,128)(2,1)} %bitcast.26), calls=%async_computation.4 | async-start | bytes 4194304 | tf_op jit(solution)/shard_map/all_to_all | solution.py:111
  135.4 16.4 %copy-start = (bf16[64,2,64,128]{3,2,1,0:T(8,128)(2,1)}, bf16[64,2,64,128]{3,2,1,0:T(8,128)(2,1)S(1)}, u32[]{:S(2)}) copy-start(bf16[64,2,64,128]{3,2,1,0:T(8,128)(2,1)S(1)} %all-to-all-done.4) | copy-start | bytes 6291460
  135.4 45.3 %all-to-all-start.1 = ((bf16[64,2,64,128]{3,2,1,0:T(8,128)(2,1)}), bf16[64,2,64,128]{3,2,1,0:T(8,128)(2,1)}, u32[]{:S(2)}, u32[]{:S(2)}) async-start(bf16[64,2,64,128]{3,2,1,0:T(8,128)(2,1)} %bitcast.25), calls=%async_computation.1 | async-start | bytes 4194304 | tf_op jit(solution)/shard_map/all_to_all | solution.py:111
  180.8 35.6 %all-to-all-start.5 = ((bf16[64,2,64,128]{3,2,1,0:T(8,128)(2,1)}), bf16[64,2,64,128]{3,2,1,0:T(8,128)(2,1)S(1)}, u32[]{:S(2)}, u32[]{:S(2)}) async-start(bf16[64,2,64,128]{3,2,1,0:T(8,128)(2,1)} %bitcast.27), calls=%async_computation.5 | async-start | bytes 4194304 | tf_op jit(solution)/shard_map/all_to_all | solution.py:111
  216.4 13.3 %copy-start.2 = (bf16[64,2,64,128]{3,2,1,0:T(8,128)(2,1)}, bf16[64,2,64,128]{3,2,1,0:T(8,128)(2,1)S(1)}, u32[]{:S(2)}) copy-start(bf16[64,2,64,128]{3,2,1,0:T(8,128)(2,1)S(1)} %all-to-all-done.5) | copy-start | bytes 6291460
  216.4 35.5 %all-to-all-start.2 = ((bf16[64,2,64,128]{3,2,1,0:T(8,128)(2,1)}), bf16[64,2,64,128]{3,2,1,0:T(8,128)(2,1)}, u32[]{:S(2)}, u32[]{:S(2)}) async-start(bf16[64,2,64,128]{3,2,1,0:T(8,128)(2,1)} %bitcast.24), calls=%async_computation.2 | async-start | bytes 4194304 | tf_op jit(solution)/shard_map/all_to_all | solution.py:111
  319.5 18.1 %all-to-all-start.7 = ((bf16[128,2,1024]{2,1,0:T(2,128)(2,1)}), bf16[128,2,1024]{2,1,0:T(2,128)(2,1)S(1)}, u32[]{:S(2)}, u32[]{:S(2)}) async-start(bf16[128,2,1024]{2,1,0:T(2,128)(2,1)} %reshape.117), calls=%async_computation.7 | async-start | bytes 1048576 | tf_op jit(solution)/shard_map/all_to_all | solution.py:121

commit v3 on v2

--- a/solution.py
+++ b/solution.py
@@ -7,7 +7,7 @@
 
 SEGS = 4
 GATES = 5
-BLOCK = 32
+BLOCK = 16
 CHUNKS = 2
 
 

time: 349 us -> 340 us (0.974)
  starting transfers between devices: 52.8 us -> 42.8 us
    all_to_all x6, starting transfers between devices: 47.9 us -> 37.9 us  [swap_major(): lax.all_to_all(split, 'amp', split_axis=0, concat_axis=0, tiled=True)]
  transfers between devices with their start and end apart: 7 -> 7, of which waited for: 7 -> 7; matrix products, arithmetic and copies ran while one was open for 3% -> 3% of each run, Pallas kernels for 17% -> 18%
where the time goes in v3:
time: 340 us; the launch traced here: 336 us
  waiting for transfers between devices  125 us (37%)
  Pallas kernels  91.4 us (27%)
  starting transfers between devices  42.8 us (13%)
  local copies, waits for them, and re-layouts  25.3 us (7%)
  blocking collectives  22.1 us (6%)
  other arithmetic  15.7 us (5%)
  matrix products  8.36 us (2%)
  between operations  5.91 us (2%)
    all_to_all x6, waiting for transfers between devices, swap_major(): lax.all_to_all(split, 'amp', split_axis=0, concat_axis=0, tiled=True)  112 us
    pallas_call x7, Pallas kernels, run_segment(): pl.pallas_call(make_kernel(slab_in, slab_out, len(sources), per_source),...  91.4 us
    all_to_all x6, starting transfers between devices, swap_major(): lax.all_to_all(split, 'amp', split_axis=0, concat_axis=0, tiled=True)  37.9 us
    all_to_all x1, blocking collectives, all_sum(): lax.all_to_all(pieces, axes, split_axis=0, concat_axis=0, tiled=True)  22.1 us
    all_to_all x1, waiting for transfers between devices, all_sum(): lax.all_to_all(spread, axes, split_axis=0, concat_axis=0, tiled=True)  13.2 us
    reshape x1, local copies, waits for them, and re-layouts, on_device(): flattened = current.reshape(-1, order)  7.6 us
    reshape x1, local copies, waits for them, and re-layouts, on_device(): adjoint_flat = adjoint.reshape(-1, order)  7.54 us
  transfers between devices with their start and end apart: 7, of which 7 were waited for; matrix products, arithmetic and copies ran while one was open for 3% of the time, Pallas kernels for 18%

profile of v3, /device:TPU:1, one launch (start us, length us, event | category | flops | bytes accessed | tf_op | source)
XLA Modules:
  0.0 336.5 jit_solution(12894184688138833434)
XLA Ops:
  1.5 1.5 fusion.9
  3.0 1.4 fusion.11
  7.7 1.9 fusion.2.gates_ref
  11.6 12.1 %shard_map.80 = bf16[128,64,128]{2,1,0:T(8,128)(2,1)} custom-call(s32[5]{0:T(128)} %get-tuple-element.14.order_ref, s32[6]{0:T(128)} %add_convert_fusion.3.flip_ref, bf16[20,256,256]{2,1,0:T(8,128)(2,1)} %fusion.2.gates_ref, bf16[128,128,128]{2,1,0:T(8,128)(2,1)} %refs_0_.3), custom_call_target="tpu_custom_call" | custom-call | tf_op jit(solution)/shard_map/pallas_call | solution.py:99
  23.7 12.4 %all-to-all-start.3 = ((bf16[64,2,64,128]{3,2,1,0:T(8,128)(2,1)}), bf16[64,2,64,128]{3,2,1,0:T(8,128)(2,1)S(1)}, u32[]{:S(2)}, u32[]{:S(2)}) async-start(bf16[64,2,64,128]{3,2,1,0:T(8,128)(2,1)} %bitcast.21), calls=%async_computation.3 | async-start | bytes 4194304 | tf_op jit(solution)/shard_map/all_to_all | solution.py:111
  36.2 12.1 %shard_map.77 = bf16[128,64,128]{2,1,0:T(8,128)(2,1)} custom-call(s32[5]{0:T(128)} %get-tuple-element.14.order_ref, s32[6]{0:T(128)} %add_convert_fusion.3.flip_ref, bf16[20,256,256]{2,1,0:T(8,128)(2,1)} %fusion.2.gates_ref, bf16[128,128,128]{2,1,0:T(8,128)(2,1)} %refs_0_.3), custom_call_target="tpu_custom_call" | custom-call | tf_op jit(solution)/shard_map/pallas_call | solution.py:99
  48.3 18.4 %all-to-all-done.3 = bf16[64,2,64,128]{3,2,1,0:T(8,128)(2,1)S(1)} async-done(((bf16[64,2,64,128]{3,2,1,0:T(8,128)(2,1)}), bf16[64,2,64,128]{3,2,1,0:T(8,128)(2,1)S(1)}, u32[]{:S(2)}, u32[]{:S(2)}) %all-to-all-start.3) | async-done | bytes 2097184 | tf_op jit(solution)/shard_map/all_to_all | solution.py:111
  66.7 5.1 %all-to-all-start = ((bf16[64,2,64,128]{3,2,1,0:T(8,128)(2,1)}), bf16[64,2,64,128]{3,2,1,0:T(8,128)(2,1)}, u32[]{:S(2)}, u32[]{:S(2)}) async-start(bf16[64,2,64,128]{3,2,1,0:T(8,128)(2,1)} %bitcast.20), calls=%async_computation | async-start | bytes 4194304 | tf_op jit(solution)/shard_map/all_to_all | solution.py:111
  73.0 12.3 %shard_map.81 = bf16[128,64,128]{2,1,0:T(8,128)(2,1)} custom-call(s32[5]{0:T(128)} %get-tuple-element.17.order_ref, s32[6]{0:T(128)} %add_convert_fusion.2.flip_ref, bf16[20,256,256]{2,1,0:T(8,128)(2,1)} %fusion.2.gates_ref, bf16[128,64,128]{2,1,0:T(8,128)(2,1)} %bitcast.23), custom_call_target="tpu_custom_call" | custom-call | tf_op jit(solution)/shard_map/pallas_call | solution.py:99
  85.4 16.9 %all-to-all-done = bf16[64,2,64,128]{3,2,1,0:T(8,128)(2,1)} async-done(((bf16[64,2,64,128]{3,2,1,0:T(8,128)(2,1)}), bf16[64,2,64,128]{3,2,1,0:T(8,128)(2,1)}, u32[]{:S(2)}, u32[]{:S(2)}) %all-to-all-start) | async-done | bytes 2097184 | tf_op jit(solution)/shard_map/all_to_all | solution.py:111
  102.2 4.9 %all-to-all-start.4 = ((bf16[64,2,64,128]{3,2,1,0:T(8,128)(2,1)}), bf16[64,2,64,128]{3,2,1,0:T(8,128)(2,1)S(1)}, u32[]{:S(2)}, u32[]{:S(2)}) async-start(bf16[64,2,64,128]{3,2,1,0:T(8,128)(2,1)} %bitcast.26), calls=%async_computation.4 | async-start | bytes 4194304 | tf_op jit(solution)/shard_map/all_to_all | solution.py:111
  107.1 12.3 %shard_map.78 = bf16[128,64,128]{2,1,0:T(8,128)(2,1)} custom-call(s32[5]{0:T(128)} %get-tuple-element.17.order_ref, s32[6]{0:T(128)} %add_convert_fusion.2.flip_ref, bf16[20,256,256]{2,1,0:T(8,128)(2,1)} %fusion.2.gates_ref, bf16[128,64,128]{2,1,0:T(8,128)(2,1)} %bitcast.2.refs_0_), custom_call_target="tpu_custom_call" | custom-call | tf_op jit(solution)/shard_map/pallas_call | solution.py:99
  119.4 18.2 %all-to-all-done.4 = bf16[64,2,64,128]{3,2,1,0:T(8,128)(2,1)S(1)} async-done(((bf16[64,2,64,128]{3,2,1,0:T(8,128)(2,1)}), bf16[64,2,64,128]{3,2,1,0:T(8,128)(2,1)S(1)}, u32[]{:S(2)}, u32[]{:S(2)}) %all-to-all-start.4) | async-done | bytes 2097184 | tf_op jit(solution)/shard_map/all_to_all | solution.py:111
  137.6 5.1 %all-to-all-start.1 = ((bf16[64,2,64,128]{3,2,1,0:T(8,128)(2,1)}), bf16[64,2,64,128]{3,2,1,0:T(8,128)(2,1)}, u32[]{:S(2)}, u32[]{:S(2)}) async-start(bf16[64,2,64,128]{3,2,1,0:T(8,128)(2,1)} %bitcast.25), calls=%async_computation.1 | async-start | bytes 4194304 | tf_op jit(solution)/shard_map/all_to_all | solution.py:111
  144.0 11.6 %shard_map.82 = bf16[128,64,128]{2,1,0:T(8,128)(2,1)} custom-call(s32[5]{0:T(128)} %get-tuple-element.15.order_ref, s32[6]{0:T(128)} %add_convert_fusion.1.flip_ref, bf16[20,256,256]{2,1,0:T(8,128)(2,1)} %fusion.2.gates_ref, bf16[128,64,128]{2,1,0:T(8,128)(2,1)} %bitcast.22), custom_call_target="tpu_custom_call" | custom-call | tf_op jit(solution)/shard_map/pallas_call | solution.py:99
  155.6 17.6 %all-to-all-done.1 = bf16[64,2,64,128]{3,2,1,0:T(8,128)(2,1)} async-done(((bf16[64,2,64,128]{3,2,1,0:T(8,128)(2,1)}), bf16[64,2,64,128]{3,2,1,0:T(8,128)(2,1)}, u32[]{:S(2)}, u32[]{:S(2)}) %all-to-all-start.1) | async-done | bytes 2097184 | tf_op jit(solution)/shard_map/all_to_all | solution.py:111
  173.2 4.9 %all-to-all-start.5 = ((bf16[64,2,64,128]{3,2,1,0:T(8,128)(2,1)}), bf16[64,2,64,128]{3,2,1,0:T(8,128)(2,1)S(1)}, u32[]{:S(2)}, u32[]{:S(2)}) async-start(bf16[64,2,64,128]{3,2,1,0:T(8,128)(2,1)} %bitcast.27), calls=%async_computation.5 | async-start | bytes 4194304 | tf_op jit(solution)/shard_map/all_to_all | solution.py:111
  178.1 11.5 %shard_map.79 = bf16[128,64,128]{2,1,0:T(8,128)(2,1)} custom-call(s32[5]{0:T(128)} %get-tuple-element.15.order_ref, s32[6]{0:T(128)} %add_convert_fusion.1.flip_ref, bf16[20,256,256]{2,1,0:T(8,128)(2,1)} %fusion.2.gates_ref, bf16[128,64,128]{2,1,0:T(8,128)(2,1)} %bitcast.4.refs_0_), custom_call_target="tpu_custom_call" | custom-call | tf_op jit(solution)/shard_map/pallas_call | solution.py:99
  189.6 19.0 %all-to-all-done.5 = bf16[64,2,64,128]{3,2,1,0:T(8,128)(2,1)S(1)} async-done(((bf16[64,2,64,128]{3,2,1,0:T(8,128)(2,1)}), bf16[64,2,64,128]{3,2,1,0:T(8,128)(2,1)S(1)}, u32[]{:S(2)}, u32[]{:S(2)}) %all-to-all-start.5) | async-done | bytes 2097184 | tf_op jit(solution)/shard_map/all_to_all | solution.py:111
  208.6 5.3 %all-to-all-start.2 = ((bf16[64,2,64,128]{3,2,1,0:T(8,128)(2,1)}), bf16[64,2,64,128]{3,2,1,0:T(8,128)(2,1)}, u32[]{:S(2)}, u32[]{:S(2)}) async-start(bf16[64,2,64,128]{3,2,1,0:T(8,128)(2,1)} %bitcast.24), calls=%async_computation.2 | async-start | bytes 4194304 | tf_op jit(solution)/shard_map/all_to_all | solution.py:111
  214.5 7.5 %reshape.112 = bf16[4096,512]{1,0:T(8,128)(2,1)} reshape(bf16[128,128,128]{2,1,0:T(8,128)(2,1)} %param.7) | data formatting | bytes 8388608 | tf_op jit(solution)/shard_map/reshape | solution.py:153
  222.7 21.6 %all-to-all-done.2 = bf16[64,2,64,128]{3,2,1,0:T(8,128)(2,1)} async-done(((bf16[64,2,64,128]{3,2,1,0:T(8,128)(2,1)}), bf16[64,2,64,128]{3,2,1,0:T(8,128)(2,1)}, u32[]{:S(2)}, u32[]{:S(2)}) %all-to-all-start.2) | async-done | bytes 2097184 | tf_op jit(solution)/shard_map/all_to_all | solution.py:111
  244.3 19.5 %shard_map.83 = bf16[128,128,128]{2,1,0:T(8,128)(2,1)} custom-call(s32[5]{0:T(128)} %get-tuple-element.16.order_ref, s32[6]{0:T(128)} %add_convert_fusion.flip_ref, bf16[20,256,256]{2,1,0:T(8,128)(2,1)} %fusion.2.gates_ref, bf16[128,64,128]{2,1,0:T(8,128)(2,1)} %bitcast.6.refs_0_, bf16[128,64,128]{2,1,0:T(8,128)(2,1)} %bitcast.28), custom_call_target="tpu_custom_call" | custom-call | tf_op jit(solution)/shard_map/pallas_call | solution.py:99
  263.8 7.6 %reshape.111 = bf16[4096,512]{1,0:T(8,128)(2,1)} reshape(bf16[128,128,128]{2,1,0:T(8,128)(2,1)} %shard_map.83) | data formatting | bytes 8388608 | tf_op jit(solution)/shard_map/reshape | solution.py:152
  271.4 5.8 %fusion.5 = bf16[512,512]{0,1:T(8,128)(2,1)S(1)} fusion(bf16[4096,512]{1,0:T(8,128)(2,1)} %reshape.111, bf16[4096,512]{1,0:T(8,128)(2,1)} %reshape.112), kind=kOutput, calls=%fused_computation.9 | convolution fusion | flops 2147745792 | bytes 8912896 | tf_op jit(solution)/shard_map/dot_general | solution.py:154
  278.3 3.7 %reduce.3 = bf16[128,2048]{1,0:T(8,128)(2,1)S(1)} reduce(bf16[128,1,2048]{2,1,0:T(2,128)(2,1)S(1)} %convert_element_type.46, bf16[]{:T(256)} %broadcast.15), dimensions={1}, to_apply=%convert_element_type.46.reduce_sub_computation | reduce | bytes 1048578 | tf_op jit(solution)/shard_map/convert_element_type | solution.py:117
  282.4 22.1 %all_to_all.42 = bf16[128,2,1024]{2,1,0:T(2,128)(2,1)S(1)} all-to-all(bf16[128,2,1024]{2,1,0:T(2,128)(2,1)S(1)} %reshape.115), channel_id=1, replica_groups=mesh['amp'=64,'grp'=2] {'amp','grp'}, dimensions={0} | all-to-all | bytes 1048576 | tf_op jit(solution)/shard_map/all_to_all | solution.py:118
  306.4 3.7 %reduce.4 = bf16[128,2048]{1,0:T(8,128)(2,1)S(1)} reduce(bf16[128,1,2048]{2,1,0:T(2,128)(2,1)S(1)} %broadcast_in_dim.5, bf16[]{:T(256)} %broadcast.15), dimensions={1}, to_apply=%broadcast_in_dim.5.reduce_sub_computation | reduce | bytes 1048578 | tf_op jit(solution)/shard_map/broadcast_in_dim | solution.py:120
  311.3 4.9 %all-to-all-start.7 = ((bf16[128,2,1024]{2,1,0:T(2,128)(2,1)}), bf16[128,2,1024]{2,1,0:T(2,128)(2,1)S(1)}, u32[]{:S(2)}, u32[]{:S(2)}) async-start(bf16[128,2,1024]{2,1,0:T(2,128)(2,1)} %reshape.117), calls=%async_computation.7 | async-start | bytes 1048576 | tf_op jit(solution)/shard_map/all_to_all | solution.py:121
  316.2 13.2 %all-to-all-done.7 = bf16[128,2,1024]{2,1,0:T(2,128)(2,1)S(1)} async-done(((bf16[128,2,1024]{2,1,0:T(2,128)(2,1)}), bf16[128,2,1024]{2,1,0:T(2,128)(2,1)S(1)}, u32[]{:S(2)}, u32[]{:S(2)}) %all-to-all-start.7) | async-done | bytes 524320 | tf_op jit(solution)/shard_map/all_to_all | solution.py:121
  329.8 3.1 reduce.2
  335.0 1.5 fusion.4
  (29 shorter events, 11.7 us)
Async XLA Ops:
  0.6 10.3 %copy-start.3 = (s32[20]{0:T(128)S(1)}, s32[20]{0:T(128)}, u32[]{:S(2)}) copy-start(s32[20]{0:T(128)} %param.10) | copy-start | bytes 244
  0.6 9.0 %copy-start.4 = (s32[20]{0:T(128)S(1)}, s32[20]{0:T(128)}, u32[]{:S(2)}) copy-start(s32[20]{0:T(128)} %param.9) | copy-start | bytes 244
  23.7 42.9 %all-to-all-start.3 = ((bf16[64,2,64,128]{3,2,1,0:T(8,128)(2,1)}), bf16[64,2,64,128]{3,2,1,0:T(8,128)(2,1)S(1)}, u32[]{:S(2)}, u32[]{:S(2)}) async-start(bf16[64,2,64,128]{3,2,1,0:T(8,128)(2,1)} %bitcast.21), calls=%async_computation.3 | async-start | bytes 4194304 | tf_op jit(solution)/shard_map/all_to_all | solution.py:111
  66.7 6.3 %copy-start.1 = (bf16[64,2,64,128]{3,2,1,0:T(8,128)(2,1)}, bf16[64,2,64,128]{3,2,1,0:T(8,128)(2,1)S(1)}, u32[]{:S(2)}) copy-start(bf16[64,2,64,128]{3,2,1,0:T(8,128)(2,1)S(1)} %all-to-all-done.3) | copy-start | bytes 6291460
  66.7 35.5 %all-to-all-start = ((bf16[64,2,64,128]{3,2,1,0:T(8,128)(2,1)}), bf16[64,2,64,128]{3,2,1,0:T(8,128)(2,1)}, u32[]{:S(2)}, u32[]{:S(2)}) async-start(bf16[64,2,64,128]{3,2,1,0:T(8,128)(2,1)} %bitcast.20), calls=%async_computation | async-start | bytes 4194304 | tf_op jit(solution)/shard_map/all_to_all | solution.py:111
  102.2 35.4 %all-to-all-start.4 = ((bf16[64,2,64,128]{3,2,1,0:T(8,128)(2,1)}), bf16[64,2,64,128]{3,2,1,0:T(8,128)(2,1)S(1)}, u32[]{:S(2)}, u32[]{:S(2)}) async-start(bf16[64,2,64,128]{3,2,1,0:T(8,128)(2,1)} %bitcast.26), calls=%async_computation.4 | async-start | bytes 4194304 | tf_op jit(solution)/shard_map/all_to_all | solution.py:111
  137.6 6.4 %copy-start = (bf16[64,2,64,128]{3,2,1,0:T(8,128)(2,1)}, bf16[64,2,64,128]{3,2,1,0:T(8,128)(2,1)S(1)}, u32[]{:S(2)}) copy-start(bf16[64,2,64,128]{3,2,1,0:T(8,128)(2,1)S(1)} %all-to-all-done.4) | copy-start | bytes 6291460
  137.6 35.5 %all-to-all-start.1 = ((bf16[64,2,64,128]{3,2,1,0:T(8,128)(2,1)}), bf16[64,2,64,128]{3,2,1,0:T(8,128)(2,1)}, u32[]{:S(2)}, u32[]{:S(2)}) async-start(bf16[64,2,64,128]{3,2,1,0:T(8,128)(2,1)} %bitcast.25), calls=%async_computation.1 | async-start | bytes 4194304 | tf_op jit(solution)/shard_map/all_to_all | solution.py:111
  173.2 35.4 %all-to-all-start.5 = ((bf16[64,2,64,128]{3,2,1,0:T(8,128)(2,1)}), bf16[64,2,64,128]{3,2,1,0:T(8,128)(2,1)S(1)}, u32[]{:S(2)}, u32[]{:S(2)}) async-start(bf16[64,2,64,128]{3,2,1,0:T(8,128)(2,1)} %bitcast.27), calls=%async_computation.5 | async-start | bytes 4194304 | tf_op jit(solution)/shard_map/all_to_all | solution.py:111
  208.6 13.5 %copy-start.2 = (bf16[64,2,64,128]{3,2,1,0:T(8,128)(2,1)}, bf16[64,2,64,128]{3,2,1,0:T(8,128)(2,1)S(1)}, u32[]{:S(2)}) copy-start(bf16[64,2,64,128]{3,2,1,0:T(8,128)(2,1)S(1)} %all-to-all-done.5) | copy-start | bytes 6291460
  208.6 35.7 %all-to-all-start.2 = ((bf16[64,2,64,128]{3,2,1,0:T(8,128)(2,1)}), bf16[64,2,64,128]{3,2,1,0:T(8,128)(2,1)}, u32[]{:S(2)}, u32[]{:S(2)}) async-start(bf16[64,2,64,128]{3,2,1,0:T(8,128)(2,1)} %bitcast.24), calls=%async_computation.2 | async-start | bytes 4194304 | tf_op jit(solution)/shard_map/all_to_all | solution.py:111
  311.3 18.1 %all-to-all-start.7 = ((bf16[128,2,1024]{2,1,0:T(2,128)(2,1)}), bf16[128,2,1024]{2,1,0:T(2,128)(2,1)S(1)}, u32[]{:S(2)}, u32[]{:S(2)}) async-start(bf16[128,2,1024]{2,1,0:T(2,128)(2,1)} %reshape.117), calls=%async_computation.7 | async-start | bytes 1048576 | tf_op jit(solution)/shard_map/all_to_all | solution.py:121

commit v4 on v3

--- a/solution.py
+++ b/solution.py
@@ -11,7 +11,7 @@
 CHUNKS = 2
 
 
-def make_kernel(slab_in, slab_out, sources, blocks_per_source):
+def make_kernel(slab_in, slab_out, sources, blocks_per_source, segment):
     def kernel(order_ref, flip_ref, gates_ref, *refs):
         x_refs, o_ref, held = refs[:sources], refs[sources], refs[sources + 1]
         half, wide, pair = held.shape
@@ -38,15 +38,17 @@
             held[:, :, lanes:] = jnp.swapaxes(held[:, :, lanes:], 1, 2)
 
         def one_gate(position, carry):
-            pl.when(flip_ref[position] == 1)(flip)
-            matrix = gates_ref[order_ref[position]]
+            pl.when(flip_ref[segment, position] == 1)(flip)
+            matrix = gates_ref[order_ref[segment, position]]
             flat = held[...].reshape(half * wide, pair)
-            out = jnp.dot(flat, matrix, preferred_element_type=jnp.float32)
+            out = lax.dot_general(
+                flat, matrix, (((1,), (1,)), ((), ())), preferred_element_type=jnp.float32
+            )
             held[...] = out.astype(jnp.bfloat16).reshape(half, wide, pair)
             return carry
 
         lax.fori_loop(0, GATES, one_gate, 0)
-        pl.when(flip_ref[GATES] == 1)(flip)
+        pl.when(flip_ref[segment, GATES] == 1)(flip)
 
         first = held[:, :, :lanes]
         second = held[:, :, lanes:]
@@ -61,14 +63,13 @@
 
 
 def block_diagonal(gate_mats):
-    transposed = jnp.swapaxes(gate_mats, 1, 2)
-    zeros = jnp.zeros_like(transposed)
-    top = jnp.concatenate([transposed, zeros], axis=2)
-    bottom = jnp.concatenate([zeros, transposed], axis=2)
+    zeros = jnp.zeros_like(gate_mats)
+    top = jnp.concatenate([gate_mats, zeros], axis=2)
+    bottom = jnp.concatenate([zeros, gate_mats], axis=2)
     return jnp.concatenate([top, bottom], axis=1)
 
 
-def run_segment(sources, gates_bd, order, flips, slab_in, slab_out, slabs, offset=0):
+def run_segment(sources, gates_bd, order, flips, segment, slab_in, slab_out, slabs, offset=0):
     wide = gates_bd.shape[1] // 2
     lanes = sources[0].shape[2]
     blocks = slabs // BLOCK
@@ -97,7 +98,7 @@
         scratch_shapes=[pltpu.VMEM((BLOCK // 2, wide, 2 * lanes), jnp.bfloat16)],
     )
     return pl.pallas_call(
-        make_kernel(slab_in, slab_out, len(sources), per_source),
+        make_kernel(slab_in, slab_out, len(sources), per_source, segment),
         grid_spec=grid_spec,
         out_shape=jax.ShapeDtypeStruct(out_shape, sources[0].dtype),
         compiler_params=pltpu.CompilerParams(dimension_semantics=("arbitrary",)),
@@ -114,7 +115,7 @@
 
 def all_sum(values, axes):
     count = lax.axis_size(axes)
-    pieces = values.reshape(count, -1).astype(jnp.bfloat16)
+    pieces = values.reshape(count, -1, 128).astype(jnp.bfloat16)
     gathered = lax.all_to_all(pieces, axes, split_axis=0, concat_axis=0, tiled=True)
     reduced = jnp.sum(gathered.astype(jnp.float32), axis=0, keepdims=True)
     spread = jnp.broadcast_to(reduced.astype(jnp.bfloat16), pieces.shape)
@@ -126,25 +127,24 @@
     gates_bd = block_diagonal(gate_mats)
     slabs = amplitudes.shape[0]
     chunk = slabs // CHUNKS
-    lanes_window = jnp.int32(0)
+    windows = gate_window.reshape(SEGS, GATES)
+    starting = jnp.concatenate([jnp.zeros((1,), jnp.int32), 1 - swap_window])
+    wanted = jnp.concatenate([1 - swap_window, jnp.zeros((1,), jnp.int32)])
+    before = jnp.concatenate([starting[:, None], windows[:, :-1]], axis=1)
+    flips = jnp.concatenate([windows != before, (windows[:, -1] != wanted)[:, None]], axis=1)
+    flips = flips.astype(jnp.int32)
+    order = gate_order.reshape(SEGS, GATES)
     chunks = None
     for segment in range(SEGS):
-        order = lax.dynamic_slice_in_dim(gate_order, segment * GATES, GATES)
-        window = lax.dynamic_slice_in_dim(gate_window, segment * GATES, GATES)
-        before = jnp.concatenate([lanes_window.reshape(1), window[:-1]])
-        wanted = 1 - swap_window[segment] if segment < SEGS - 1 else jnp.int32(0)
-        flips = jnp.concatenate([window != before, (window[-1] != wanted).reshape(1)])
-        flips = flips.astype(jnp.int32)
-        lanes_window = wanted
         if segment == 0:
             chunks = [
-                run_segment([amplitudes], gates_bd, order, flips, True, False, chunk, c * (chunk // BLOCK))
+                run_segment([amplitudes], gates_bd, order, flips, segment, True, False, chunk, c * (chunk // BLOCK))
                 for c in range(CHUNKS)
             ]
         elif segment < SEGS - 1:
-            chunks = [run_segment([part], gates_bd, order, flips, False, False, chunk) for part in chunks]
+            chunks = [run_segment([part], gates_bd, order, flips, segment, False, False, chunk) for part in chunks]
         else:
-            current = run_segment(chunks, gates_bd, order, flips, False, True, slabs)
+            current = run_segment(chunks, gates_bd, order, flips, segment, False, True, slabs)
         if segment < SEGS - 1:
             chunks = [swap_major(part) for part in chunks]
     order = 4 * amplitudes.shape[2]

time: 340 us -> 327 us (0.962); the launches traced: 336 us -> 328 us
  Pallas kernels: 91.4 us -> 107 us
  other arithmetic: 15.7 us -> 4.98 us
  between operations: 5.91 us -> 1.44 us
  local copies, waits for them, and re-layouts: 25.3 us -> 21.1 us
  waiting for transfers between devices: 125 us -> 121 us
    pallas_call x7, Pallas kernels: 91.4 us -> 107 us  [run_segment(): pl.pallas_call(make_kernel(slab_in, slab_out, len(sources), per_source, s...]
    slice x3 -> x0, local copies, waits for them, and re-layouts: 3.76 us -> none  [the longest x1 1.45 us: on_device(): window[-1] != wanted]
    convert_element_type x1 -> x0, other arithmetic: 3.7 us -> none  [all_sum(): pieces = values.reshape(count, -1).astype(jnp.bfloat16)]
    broadcast_in_dim x1, other arithmetic: 3.71 us -> 0.08 us  [on_device(): before = jnp.concatenate([starting[:, None], windows[:, :-1]], axis=1)]
    all_to_all x6, waiting for transfers between devices: 112 us -> 108 us  [swap_major(): lax.all_to_all(split, 'amp', split_axis=0, concat_axis=0, tiled=True)]
  transfers between devices with their start and end apart: 7 -> 7, of which waited for: 7 -> 7; matrix products, arithmetic and copies ran while one was open for 3% -> 2% of each run, Pallas kernels for 18% -> 20%
where the time goes in v4:
time: 327 us; the launch traced here: 328 us
  waiting for transfers between devices  121 us (37%)
  Pallas kernels  107 us (33%)
  starting transfers between devices  42.6 us (13%)
  blocking collectives  21.6 us (7%)
  local copies, waits for them, and re-layouts  21.1 us (6%)
  matrix products  8.37 us (3%)
  other arithmetic  4.98 us (2%)
    all_to_all x6, waiting for transfers between devices, swap_major(): lax.all_to_all(split, 'amp', split_axis=0, concat_axis=0, tiled=True)  108 us
    pallas_call x7, Pallas kernels, run_segment(): pl.pallas_call(make_kernel(slab_in, slab_out, len(sources), per_source, s...  107 us
    all_to_all x6, starting transfers between devices, swap_major(): lax.all_to_all(split, 'amp', split_axis=0, concat_axis=0, tiled=True)  37.6 us
    all_to_all x1, blocking collectives, all_sum(): lax.all_to_all(pieces, axes, split_axis=0, concat_axis=0, tiled=True)  21.6 us
    all_to_all x1, waiting for transfers between devices, all_sum(): lax.all_to_all(spread, axes, split_axis=0, concat_axis=0, tiled=True)  13.2 us
    reshape x1, local copies, waits for them, and re-layouts, on_device(): flattened = current.reshape(-1, order)  7.58 us
    reshape x1, local copies, waits for them, and re-layouts, on_device(): adjoint_flat = adjoint.reshape(-1, order)  7.54 us
  transfers between devices with their start and end apart: 7, of which 7 were waited for; matrix products, arithmetic and copies ran while one was open for 2% of the time, Pallas kernels for 20%

profile of v4, /device:TPU:1, one launch (start us, length us, event | category | flops | bytes accessed | tf_op | source)
XLA Modules:
  0.0 328.0 jit_solution(7931647627556379375)
XLA Ops:
  0.6 0.7 reshape.64
  2.4 3.2 fusion.2.gates_ref
  7.1 12.8 %shard_map.80 = bf16[128,64,128]{2,1,0:T(8,128)(2,1)} custom-call(s32[4,5]{1,0:T(4,128)} %reshape.63.order_ref, s32[4,6]{1,0:T(4,128)} %add_convert_fusion.flip_ref, bf16[20,256,256]{2,1,0:T(8,128)(2,1)} %fusion.2.gates_ref, bf16[128,128,128]{2,1,0:T(8,128)(2,1)} %refs_0_.3), custom_call_target="tpu_custom_call" | custom-call | tf_op jit(solution)/shard_map/pallas_call | solution.py:100
  19.9 12.5 %all-to-all-start.3 = ((bf16[64,2,64,128]{3,2,1,0:T(8,128)(2,1)}), bf16[64,2,64,128]{3,2,1,0:T(8,128)(2,1)S(1)}, u32[]{:S(2)}, u32[]{:S(2)}) async-start(bf16[64,2,64,128]{3,2,1,0:T(8,128)(2,1)} %bitcast.33), calls=%async_computation.3 | async-start | bytes 4194304 | tf_op jit(solution)/shard_map/all_to_all | solution.py:112
  32.4 12.8 %shard_map.77 = bf16[128,64,128]{2,1,0:T(8,128)(2,1)} custom-call(s32[4,5]{1,0:T(4,128)} %reshape.63.order_ref, s32[4,6]{1,0:T(4,128)} %add_convert_fusion.flip_ref, bf16[20,256,256]{2,1,0:T(8,128)(2,1)} %fusion.2.gates_ref, bf16[128,128,128]{2,1,0:T(8,128)(2,1)} %refs_0_.3), custom_call_target="tpu_custom_call" | custom-call | tf_op jit(solution)/shard_map/pallas_call | solution.py:100
  45.2 17.7 %all-to-all-done.3 = bf16[64,2,64,128]{3,2,1,0:T(8,128)(2,1)S(1)} async-done(((bf16[64,2,64,128]{3,2,1,0:T(8,128)(2,1)}), bf16[64,2,64,128]{3,2,1,0:T(8,128)(2,1)S(1)}, u32[]{:S(2)}, u32[]{:S(2)}) %all-to-all-start.3) | async-done | bytes 2097184 | tf_op jit(solution)/shard_map/all_to_all | solution.py:112
  62.9 1.3 copy-done.3
  64.2 4.9 %all-to-all-start = ((bf16[64,2,64,128]{3,2,1,0:T(8,128)(2,1)}), bf16[64,2,64,128]{3,2,1,0:T(8,128)(2,1)S(1)}, u32[]{:S(2)}, u32[]{:S(2)}) async-start(bf16[64,2,64,128]{3,2,1,0:T(8,128)(2,1)} %bitcast.32), calls=%async_computation | async-start | bytes 4194304 | tf_op jit(solution)/shard_map/all_to_all | solution.py:112
  69.1 12.4 %shard_map.81 = bf16[128,64,128]{2,1,0:T(8,128)(2,1)} custom-call(s32[4,5]{1,0:T(4,128)} %reshape.63.order_ref, s32[4,6]{1,0:T(4,128)} %add_convert_fusion.flip_ref, bf16[20,256,256]{2,1,0:T(8,128)(2,1)} %fusion.2.gates_ref, bf16[128,64,128]{2,1,0:T(8,128)(2,1)} %bitcast.27), custom_call_target="tpu_custom_call" | custom-call | tf_op jit(solution)/shard_map/pallas_call | solution.py:100
  81.5 18.1 %all-to-all-done = bf16[64,2,64,128]{3,2,1,0:T(8,128)(2,1)S(1)} async-done(((bf16[64,2,64,128]{3,2,1,0:T(8,128)(2,1)}), bf16[64,2,64,128]{3,2,1,0:T(8,128)(2,1)S(1)}, u32[]{:S(2)}, u32[]{:S(2)}) %all-to-all-start) | async-done | bytes 2097184 | tf_op jit(solution)/shard_map/all_to_all | solution.py:112
  99.6 5.1 %all-to-all-start.4 = ((bf16[64,2,64,128]{3,2,1,0:T(8,128)(2,1)}), bf16[64,2,64,128]{3,2,1,0:T(8,128)(2,1)}, u32[]{:S(2)}, u32[]{:S(2)}) async-start(bf16[64,2,64,128]{3,2,1,0:T(8,128)(2,1)} %bitcast.28), calls=%async_computation.4 | async-start | bytes 4194304 | tf_op jit(solution)/shard_map/all_to_all | solution.py:112
  104.8 12.4 %shard_map.78 = bf16[128,64,128]{2,1,0:T(8,128)(2,1)} custom-call(s32[4,5]{1,0:T(4,128)} %reshape.63.order_ref, s32[4,6]{1,0:T(4,128)} %add_convert_fusion.flip_ref, bf16[20,256,256]{2,1,0:T(8,128)(2,1)} %fusion.2.gates_ref, bf16[128,64,128]{2,1,0:T(8,128)(2,1)} %bitcast.25), custom_call_target="tpu_custom_call" | custom-call | tf_op jit(solution)/shard_map/pallas_call | solution.py:100
  117.1 18.0 %all-to-all-done.4 = bf16[64,2,64,128]{3,2,1,0:T(8,128)(2,1)} async-done(((bf16[64,2,64,128]{3,2,1,0:T(8,128)(2,1)}), bf16[64,2,64,128]{3,2,1,0:T(8,128)(2,1)}, u32[]{:S(2)}, u32[]{:S(2)}) %all-to-all-start.4) | async-done | bytes 2097184 | tf_op jit(solution)/shard_map/all_to_all | solution.py:112
  135.1 4.9 %all-to-all-start.1 = ((bf16[64,2,64,128]{3,2,1,0:T(8,128)(2,1)}), bf16[64,2,64,128]{3,2,1,0:T(8,128)(2,1)S(1)}, u32[]{:S(2)}, u32[]{:S(2)}) async-start(bf16[64,2,64,128]{3,2,1,0:T(8,128)(2,1)} %bitcast.29), calls=%async_computation.1 | async-start | bytes 4194304 | tf_op jit(solution)/shard_map/all_to_all | solution.py:112
  140.1 14.6 %shard_map.82 = bf16[128,64,128]{2,1,0:T(8,128)(2,1)} custom-call(s32[4,5]{1,0:T(4,128)} %reshape.63.order_ref, s32[4,6]{1,0:T(4,128)} %add_convert_fusion.flip_ref, bf16[20,256,256]{2,1,0:T(8,128)(2,1)} %fusion.2.gates_ref, bf16[128,64,128]{2,1,0:T(8,128)(2,1)} %bitcast.11.refs_0_), custom_call_target="tpu_custom_call" | custom-call | tf_op jit(solution)/shard_map/pallas_call | solution.py:100
  154.7 15.8 %all-to-all-done.1 = bf16[64,2,64,128]{3,2,1,0:T(8,128)(2,1)S(1)} async-done(((bf16[64,2,64,128]{3,2,1,0:T(8,128)(2,1)}), bf16[64,2,64,128]{3,2,1,0:T(8,128)(2,1)S(1)}, u32[]{:S(2)}, u32[]{:S(2)}) %all-to-all-start.1) | async-done | bytes 2097184 | tf_op jit(solution)/shard_map/all_to_all | solution.py:112
  170.6 1.3 copy-done.2
  171.9 4.9 %all-to-all-start.5 = ((bf16[64,2,64,128]{3,2,1,0:T(8,128)(2,1)}), bf16[64,2,64,128]{3,2,1,0:T(8,128)(2,1)S(1)}, u32[]{:S(2)}, u32[]{:S(2)}) async-start(bf16[64,2,64,128]{3,2,1,0:T(8,128)(2,1)} %bitcast.30), calls=%async_computation.5 | async-start | bytes 4194304 | tf_op jit(solution)/shard_map/all_to_all | solution.py:112
  176.8 14.6 %shard_map.79 = bf16[128,64,128]{2,1,0:T(8,128)(2,1)} custom-call(s32[4,5]{1,0:T(4,128)} %reshape.63.order_ref, s32[4,6]{1,0:T(4,128)} %add_convert_fusion.flip_ref, bf16[20,256,256]{2,1,0:T(8,128)(2,1)} %fusion.2.gates_ref, bf16[128,64,128]{2,1,0:T(8,128)(2,1)} %bitcast.26), custom_call_target="tpu_custom_call" | custom-call | tf_op jit(solution)/shard_map/pallas_call | solution.py:100
  191.4 15.8 %all-to-all-done.5 = bf16[64,2,64,128]{3,2,1,0:T(8,128)(2,1)S(1)} async-done(((bf16[64,2,64,128]{3,2,1,0:T(8,128)(2,1)}), bf16[64,2,64,128]{3,2,1,0:T(8,128)(2,1)S(1)}, u32[]{:S(2)}, u32[]{:S(2)}) %all-to-all-start.5) | async-done | bytes 2097184 | tf_op jit(solution)/shard_map/all_to_all | solution.py:112
  207.3 5.3 %all-to-all-start.2 = ((bf16[64,2,64,128]{3,2,1,0:T(8,128)(2,1)}), bf16[64,2,64,128]{3,2,1,0:T(8,128)(2,1)}, u32[]{:S(2)}, u32[]{:S(2)}) async-start(bf16[64,2,64,128]{3,2,1,0:T(8,128)(2,1)} %bitcast.31), calls=%async_computation.2 | async-start | bytes 4194304 | tf_op jit(solution)/shard_map/all_to_all | solution.py:112
  212.6 7.5 %reshape.78 = bf16[4096,512]{1,0:T(8,128)(2,1)} reshape(bf16[128,128,128]{2,1,0:T(8,128)(2,1)} %param.7) | data formatting | bytes 8388608 | tf_op jit(solution)/shard_map/reshape | solution.py:153
  220.1 22.7 %all-to-all-done.2 = bf16[64,2,64,128]{3,2,1,0:T(8,128)(2,1)} async-done(((bf16[64,2,64,128]{3,2,1,0:T(8,128)(2,1)}), bf16[64,2,64,128]{3,2,1,0:T(8,128)(2,1)}, u32[]{:S(2)}, u32[]{:S(2)}) %all-to-all-start.2) | async-done | bytes 2097184 | tf_op jit(solution)/shard_map/all_to_all | solution.py:112
  242.8 27.0 %shard_map.83 = bf16[128,128,128]{2,1,0:T(8,128)(2,1)} custom-call(s32[4,5]{1,0:T(4,128)} %reshape.63.order_ref, s32[4,6]{1,0:T(4,128)} %add_convert_fusion.flip_ref, bf16[20,256,256]{2,1,0:T(8,128)(2,1)} %fusion.2.gates_ref, bf16[128,64,128]{2,1,0:T(8,128)(2,1)} %bitcast.7.refs_0_, bf16[128,64,128]{2,1,0:T(8,128)(2,1)} %bitcast.24), custom_call_target="tpu_custom_call" | custom-call | tf_op jit(solution)/shard_map/pallas_call | solution.py:100
  269.8 7.6 %reshape.77 = bf16[4096,512]{1,0:T(8,128)(2,1)} reshape(bf16[128,128,128]{2,1,0:T(8,128)(2,1)} %shard_map.83) | data formatting | bytes 8388608 | tf_op jit(solution)/shard_map/reshape | solution.py:152
  277.4 5.8 %fusion.5 = bf16[512,512]{0,1:T(8,128)(2,1)S(1)} fusion(bf16[4096,512]{1,0:T(8,128)(2,1)} %reshape.77, bf16[4096,512]{1,0:T(8,128)(2,1)} %reshape.78), kind=kOutput, calls=%fused_computation.9 | convolution fusion | flops 2147745792 | bytes 8912896 | tf_op jit(solution)/shard_map/dot_general | solution.py:154
  283.7 21.6 %all_to_all.40 = bf16[128,16,128]{2,1,0:T(8,128)(2,1)S(1)} all-to-all(bf16[128,16,128]{2,1,0:T(8,128)(2,1)S(1)} %convert_element_type.25), channel_id=1, replica_groups=mesh['amp'=64,'grp'=2] {'amp','grp'}, dimensions={0} | all-to-all | bytes 1048576 | tf_op jit(solution)/shard_map/all_to_all | solution.py:119
  305.4 0.9 broadcast_in_dim.16
  306.3 4.9 %all-to-all-start.7 = ((bf16[128,16,128]{2,1,0:T(8,128)(2,1)}), bf16[128,16,128]{2,1,0:T(8,128)(2,1)S(1)}, u32[]{:S(2)}, u32[]{:S(2)}) async-start(bf16[128,16,128]{2,1,0:T(8,128)(2,1)} %broadcast_in_dim.16), calls=%async_computation.7 | async-start | bytes 1048576 | tf_op jit(solution)/shard_map/all_to_all | solution.py:122
  311.2 13.2 %all-to-all-done.7 = bf16[128,16,128]{2,1,0:T(8,128)(2,1)S(1)} async-done(((bf16[128,16,128]{2,1,0:T(8,128)(2,1)}), bf16[128,16,128]{2,1,0:T(8,128)(2,1)S(1)}, u32[]{:S(2)}, u32[]{:S(2)}) %all-to-all-start.7) | async-done | bytes 524320 | tf_op jit(solution)/shard_map/all_to_all | solution.py:122
  324.7 1.1 select_reduce_fusion
  326.5 1.5 fusion.4
  (21 shorter events, 3.5 us)
Async XLA Ops:
  0.6 5.0 %copy-start.4 = (s32[20]{0:T(128)S(1)}, s32[20]{0:T(128)}, u32[]{:S(2)}) copy-start(s32[20]{0:T(128)} %param.9) | copy-start | bytes 244
  19.9 43.0 %all-to-all-start.3 = ((bf16[64,2,64,128]{3,2,1,0:T(8,128)(2,1)}), bf16[64,2,64,128]{3,2,1,0:T(8,128)(2,1)S(1)}, u32[]{:S(2)}, u32[]{:S(2)}) async-start(bf16[64,2,64,128]{3,2,1,0:T(8,128)(2,1)} %bitcast.33), calls=%async_computation.3 | async-start | bytes 4194304 | tf_op jit(solution)/shard_map/all_to_all | solution.py:112
  62.9 1.3 copy-start.3
  64.2 35.4 %all-to-all-start = ((bf16[64,2,64,128]{3,2,1,0:T(8,128)(2,1)}), bf16[64,2,64,128]{3,2,1,0:T(8,128)(2,1)S(1)}, u32[]{:S(2)}, u32[]{:S(2)}) async-start(bf16[64,2,64,128]{3,2,1,0:T(8,128)(2,1)} %bitcast.32), calls=%async_computation | async-start | bytes 4194304 | tf_op jit(solution)/shard_map/all_to_all | solution.py:112
  99.6 5.1 %copy-start.1 = (bf16[64,2,64,128]{3,2,1,0:T(8,128)(2,1)}, bf16[64,2,64,128]{3,2,1,0:T(8,128)(2,1)S(1)}, u32[]{:S(2)}) copy-start(bf16[64,2,64,128]{3,2,1,0:T(8,128)(2,1)S(1)} %all-to-all-done) | copy-start | bytes 6291460
  99.6 35.5 %all-to-all-start.4 = ((bf16[64,2,64,128]{3,2,1,0:T(8,128)(2,1)}), bf16[64,2,64,128]{3,2,1,0:T(8,128)(2,1)}, u32[]{:S(2)}, u32[]{:S(2)}) async-start(bf16[64,2,64,128]{3,2,1,0:T(8,128)(2,1)} %bitcast.28), calls=%async_computation.4 | async-start | bytes 4194304 | tf_op jit(solution)/shard_map/all_to_all | solution.py:112
  135.1 35.4 %all-to-all-start.1 = ((bf16[64,2,64,128]{3,2,1,0:T(8,128)(2,1)}), bf16[64,2,64,128]{3,2,1,0:T(8,128)(2,1)S(1)}, u32[]{:S(2)}, u32[]{:S(2)}) async-start(bf16[64,2,64,128]{3,2,1,0:T(8,128)(2,1)} %bitcast.29), calls=%async_computation.1 | async-start | bytes 4194304 | tf_op jit(solution)/shard_map/all_to_all | solution.py:112
  170.5 1.3 copy-start.2
  171.9 35.4 %all-to-all-start.5 = ((bf16[64,2,64,128]{3,2,1,0:T(8,128)(2,1)}), bf16[64,2,64,128]{3,2,1,0:T(8,128)(2,1)S(1)}, u32[]{:S(2)}, u32[]{:S(2)}) async-start(bf16[64,2,64,128]{3,2,1,0:T(8,128)(2,1)} %bitcast.30), calls=%async_computation.5 | async-start | bytes 4194304 | tf_op jit(solution)/shard_map/all_to_all | solution.py:112
  207.3 12.9 %copy-start = (bf16[64,2,64,128]{3,2,1,0:T(8,128)(2,1)}, bf16[64,2,64,128]{3,2,1,0:T(8,128)(2,1)S(1)}, u32[]{:S(2)}) copy-start(bf16[64,2,64,128]{3,2,1,0:T(8,128)(2,1)S(1)} %all-to-all-done.5) | copy-start | bytes 6291460
  207.3 35.5 %all-to-all-start.2 = ((bf16[64,2,64,128]{3,2,1,0:T(8,128)(2,1)}), bf16[64,2,64,128]{3,2,1,0:T(8,128)(2,1)}, u32[]{:S(2)}, u32[]{:S(2)}) async-start(bf16[64,2,64,128]{3,2,1,0:T(8,128)(2,1)} %bitcast.31), calls=%async_computation.2 | async-start | bytes 4194304 | tf_op jit(solution)/shard_map/all_to_all | solution.py:112
  306.3 18.1 %all-to-all-start.7 = ((bf16[128,16,128]{2,1,0:T(8,128)(2,1)}), bf16[128,16,128]{2,1,0:T(8,128)(2,1)S(1)}, u32[]{:S(2)}, u32[]{:S(2)}) async-start(bf16[128,16,128]{2,1,0:T(8,128)(2,1)} %broadcast_in_dim.16), calls=%async_computation.7 | async-start | bytes 1048576 | tf_op jit(solution)/shard_map/all_to_all | solution.py:122

commit v5 on v4

--- a/solution.py
+++ b/solution.py
@@ -13,7 +13,7 @@
 
 def make_kernel(slab_in, slab_out, sources, blocks_per_source, segment):
     def kernel(order_ref, flip_ref, gates_ref, *refs):
-        x_refs, o_ref, held = refs[:sources], refs[sources], refs[sources + 1]
+        x_refs, o_ref, held = refs[:sources], refs[-2], refs[-1]
         half, wide, pair = held.shape
         lanes = pair // 2
 
@@ -69,7 +69,8 @@
     return jnp.concatenate([top, bottom], axis=1)
 
 
-def run_segment(sources, gates_bd, order, flips, segment, slab_in, slab_out, slabs, offset=0):
+def run_segment(sources, gates_bd, order, flips, segment, slab_in, slab_out, slabs, offset=0,
+                into=None, out_offset=0, out_slabs=None):
     wide = gates_bd.shape[1] // 2
     lanes = sources[0].shape[2]
     blocks = slabs // BLOCK
@@ -84,8 +85,8 @@
         return pl.BlockSpec(shape, pick)
 
     if slab_out:
-        out_spec = pl.BlockSpec((BLOCK, wide, lanes), lambda i, o, f: (i, 0, 0))
-        out_shape = (slabs, wide, lanes)
+        out_spec = pl.BlockSpec((BLOCK, wide, lanes), lambda i, o, f: (i + out_offset, 0, 0))
+        out_shape = (out_slabs or slabs, wide, lanes)
     else:
         out_spec = pl.BlockSpec((wide, BLOCK, lanes), lambda i, o, f: (0, i, 0))
         out_shape = (wide, slabs, lanes)
@@ -93,7 +94,8 @@
         num_scalar_prefetch=2,
         grid=(blocks,),
         in_specs=[pl.BlockSpec(gates_bd.shape, lambda i, o, f: (0, 0, 0))]
-        + [source_spec(index) for index in range(len(sources))],
+        + [source_spec(index) for index in range(len(sources))]
+        + ([] if into is None else [pl.BlockSpec(memory_space=pl.ANY)]),
         out_specs=out_spec,
         scratch_shapes=[pltpu.VMEM((BLOCK // 2, wide, 2 * lanes), jnp.bfloat16)],
     )
@@ -102,7 +104,8 @@
         grid_spec=grid_spec,
         out_shape=jax.ShapeDtypeStruct(out_shape, sources[0].dtype),
         compiler_params=pltpu.CompilerParams(dimension_semantics=("arbitrary",)),
-    )(order, flips, gates_bd, *sources)
+        input_output_aliases={} if into is None else {3 + len(sources): 0},
+    )(order, flips, gates_bd, *sources, *([] if into is None else [into]))
 
 
 def swap_major(values):
@@ -144,7 +147,12 @@
         elif segment < SEGS - 1:
             chunks = [run_segment([part], gates_bd, order, flips, segment, False, False, chunk) for part in chunks]
         else:
-            current = run_segment(chunks, gates_bd, order, flips, segment, False, True, slabs)
+            current = None
+            for c, part in enumerate(chunks):
+                current = run_segment(
+                    [part], gates_bd, order, flips, segment, False, True, chunk,
+                    into=current, out_offset=c * (chunk // BLOCK), out_slabs=slabs,
+                )
         if segment < SEGS - 1:
             chunks = [swap_major(part) for part in chunks]
     order = 4 * amplitudes.shape[2]

time: 327 us -> 315 us (0.963)
  waiting for transfers between devices: 121 us -> 110 us
    all_to_all x6, waiting for transfers between devices: 108 us -> 97.2 us  [swap_major(): lax.all_to_all(split, 'amp', split_axis=0, concat_axis=0, tiled=True)]
    pallas_call x7 -> x8, Pallas kernels: 107 us -> 104 us  [run_segment(): pl.pallas_call(make_kernel(slab_in, slab_out, len(sources), per_source, s...]
  transfers between devices with their start and end apart: 7 -> 7, of which waited for: 7 -> 7; matrix products, arithmetic and copies ran while one was open for 2% -> 2% of each run, Pallas kernels for 20% -> 25%
where the time goes in v5:
time: 315 us; the launch traced here: 314 us
  waiting for transfers between devices  110 us (35%)
  Pallas kernels  104 us (33%)
  starting transfers between devices  42.4 us (13%)
  blocking collectives  21.7 us (7%)
  local copies, waits for them, and re-layouts  21.2 us (7%)
  matrix products  8.36 us (3%)
  other arithmetic  4.98 us (2%)
    pallas_call x8, Pallas kernels, run_segment(): pl.pallas_call(make_kernel(slab_in, slab_out, len(sources), per_source, s...  104 us
    all_to_all x6, waiting for transfers between devices, swap_major(): lax.all_to_all(split, 'amp', split_axis=0, concat_axis=0, tiled=True)  97.2 us
    all_to_all x6, starting transfers between devices, swap_major(): lax.all_to_all(split, 'amp', split_axis=0, concat_axis=0, tiled=True)  37.5 us
    all_to_all x1, blocking collectives, all_sum(): lax.all_to_all(pieces, axes, split_axis=0, concat_axis=0, tiled=True)  21.7 us
    all_to_all x1, waiting for transfers between devices, all_sum(): lax.all_to_all(spread, axes, split_axis=0, concat_axis=0, tiled=True)  13.2 us
    reshape x1, local copies, waits for them, and re-layouts, on_device(): flattened = current.reshape(-1, order)  7.58 us
    reshape x1, local copies, waits for them, and re-layouts, on_device(): adjoint_flat = adjoint.reshape(-1, order)  7.54 us
  transfers between devices with their start and end apart: 7, of which 7 were waited for; matrix products, arithmetic and copies ran while one was open for 2% of the time, Pallas kernels for 25%

profile of v5, /device:TPU:1, one launch (start us, length us, event | category | flops | bytes accessed | tf_op | source)
XLA Modules:
  0.0 313.9 jit_solution(9059350332088400172)
XLA Ops:
  2.4 3.2 %fusion.2.gates_ref = bf16[20,256,256]{2,1,0:T(8,128)(2,1)} fusion(bf16[20,128,128]{2,1,0:T(8,128)(2,1)} %param.8), kind=kLoop, calls=%fused_computation.4 | loop fusion | flops 10485760 | bytes 3276800 | tf_op jit(solution)/shard_map/concatenate | solution.py:69
  7.1 12.1 %shard_map.80 = bf16[128,64,128]{2,1,0:T(8,128)(2,1)} custom-call(s32[4,5]{1,0:T(4,128)} %reshape.63.order_ref, s32[4,6]{1,0:T(4,128)} %add_convert_fusion.flip_ref, bf16[20,256,256]{2,1,0:T(8,128)(2,1)} %fusion.2.gates_ref, bf16[128,128,128]{2,1,0:T(8,128)(2,1)} %refs_0_.3), custom_call_target="tpu_custom_call" | custom-call | tf_op jit(solution)/shard_map/pallas_call | solution.py:102
  19.2 12.4 %all-to-all-start.3 = ((bf16[64,2,64,128]{3,2,1,0:T(8,128)(2,1)}), bf16[64,2,64,128]{3,2,1,0:T(8,128)(2,1)S(1)}, u32[]{:S(2)}, u32[]{:S(2)}) async-start(bf16[64,2,64,128]{3,2,1,0:T(8,128)(2,1)} %bitcast.33), calls=%async_computation.3 | async-start | bytes 4194304 | tf_op jit(solution)/shard_map/all_to_all | solution.py:115
  31.6 12.1 %shard_map.77 = bf16[128,64,128]{2,1,0:T(8,128)(2,1)} custom-call(s32[4,5]{1,0:T(4,128)} %reshape.63.order_ref, s32[4,6]{1,0:T(4,128)} %add_convert_fusion.flip_ref, bf16[20,256,256]{2,1,0:T(8,128)(2,1)} %fusion.2.gates_ref, bf16[128,128,128]{2,1,0:T(8,128)(2,1)} %refs_0_.3), custom_call_target="tpu_custom_call" | custom-call | tf_op jit(solution)/shard_map/pallas_call | solution.py:102
  43.7 18.4 %all-to-all-done.3 = bf16[64,2,64,128]{3,2,1,0:T(8,128)(2,1)S(1)} async-done(((bf16[64,2,64,128]{3,2,1,0:T(8,128)(2,1)}), bf16[64,2,64,128]{3,2,1,0:T(8,128)(2,1)S(1)}, u32[]{:S(2)}, u32[]{:S(2)}) %all-to-all-start.3) | async-done | bytes 2097184 | tf_op jit(solution)/shard_map/all_to_all | solution.py:115
  62.1 1.3 copy-done.2
  63.4 4.9 %all-to-all-start = ((bf16[64,2,64,128]{3,2,1,0:T(8,128)(2,1)}), bf16[64,2,64,128]{3,2,1,0:T(8,128)(2,1)S(1)}, u32[]{:S(2)}, u32[]{:S(2)}) async-start(bf16[64,2,64,128]{3,2,1,0:T(8,128)(2,1)} %bitcast.32), calls=%async_computation | async-start | bytes 4194304 | tf_op jit(solution)/shard_map/all_to_all | solution.py:115
  68.3 12.3 %shard_map.81 = bf16[128,64,128]{2,1,0:T(8,128)(2,1)} custom-call(s32[4,5]{1,0:T(4,128)} %reshape.63.order_ref, s32[4,6]{1,0:T(4,128)} %add_convert_fusion.flip_ref, bf16[20,256,256]{2,1,0:T(8,128)(2,1)} %fusion.2.gates_ref, bf16[128,64,128]{2,1,0:T(8,128)(2,1)} %bitcast.26), custom_call_target="tpu_custom_call" | custom-call | tf_op jit(solution)/shard_map/pallas_call | solution.py:102
  80.7 18.1 %all-to-all-done = bf16[64,2,64,128]{3,2,1,0:T(8,128)(2,1)S(1)} async-done(((bf16[64,2,64,128]{3,2,1,0:T(8,128)(2,1)}), bf16[64,2,64,128]{3,2,1,0:T(8,128)(2,1)S(1)}, u32[]{:S(2)}, u32[]{:S(2)}) %all-to-all-start) | async-done | bytes 2097184 | tf_op jit(solution)/shard_map/all_to_all | solution.py:115
  98.8 5.1 %all-to-all-start.4 = ((bf16[64,2,64,128]{3,2,1,0:T(8,128)(2,1)}), bf16[64,2,64,128]{3,2,1,0:T(8,128)(2,1)}, u32[]{:S(2)}, u32[]{:S(2)}) async-start(bf16[64,2,64,128]{3,2,1,0:T(8,128)(2,1)} %bitcast.28), calls=%async_computation.4 | async-start | bytes 4194304 | tf_op jit(solution)/shard_map/all_to_all | solution.py:115
  104.0 12.4 %shard_map.78 = bf16[128,64,128]{2,1,0:T(8,128)(2,1)} custom-call(s32[4,5]{1,0:T(4,128)} %reshape.63.order_ref, s32[4,6]{1,0:T(4,128)} %add_convert_fusion.flip_ref, bf16[20,256,256]{2,1,0:T(8,128)(2,1)} %fusion.2.gates_ref, bf16[128,64,128]{2,1,0:T(8,128)(2,1)} %bitcast.24), custom_call_target="tpu_custom_call" | custom-call | tf_op jit(solution)/shard_map/pallas_call | solution.py:102
  116.4 18.0 %all-to-all-done.4 = bf16[64,2,64,128]{3,2,1,0:T(8,128)(2,1)} async-done(((bf16[64,2,64,128]{3,2,1,0:T(8,128)(2,1)}), bf16[64,2,64,128]{3,2,1,0:T(8,128)(2,1)}, u32[]{:S(2)}, u32[]{:S(2)}) %all-to-all-start.4) | async-done | bytes 2097184 | tf_op jit(solution)/shard_map/all_to_all | solution.py:115
  134.4 4.9 %all-to-all-start.1 = ((bf16[64,2,64,128]{3,2,1,0:T(8,128)(2,1)}), bf16[64,2,64,128]{3,2,1,0:T(8,128)(2,1)S(1)}, u32[]{:S(2)}, u32[]{:S(2)}) async-start(bf16[64,2,64,128]{3,2,1,0:T(8,128)(2,1)} %bitcast.29), calls=%async_computation.1 | async-start | bytes 4194304 | tf_op jit(solution)/shard_map/all_to_all | solution.py:115
  139.3 13.8 %shard_map.82 = bf16[128,64,128]{2,1,0:T(8,128)(2,1)} custom-call(s32[4,5]{1,0:T(4,128)} %reshape.63.order_ref, s32[4,6]{1,0:T(4,128)} %add_convert_fusion.flip_ref, bf16[20,256,256]{2,1,0:T(8,128)(2,1)} %fusion.2.gates_ref, bf16[128,64,128]{2,1,0:T(8,128)(2,1)} %bitcast.11.refs_0_), custom_call_target="tpu_custom_call" | custom-call | tf_op jit(solution)/shard_map/pallas_call | solution.py:102
  153.1 16.6 %all-to-all-done.1 = bf16[64,2,64,128]{3,2,1,0:T(8,128)(2,1)S(1)} async-done(((bf16[64,2,64,128]{3,2,1,0:T(8,128)(2,1)}), bf16[64,2,64,128]{3,2,1,0:T(8,128)(2,1)S(1)}, u32[]{:S(2)}, u32[]{:S(2)}) %all-to-all-start.1) | async-done | bytes 2097184 | tf_op jit(solution)/shard_map/all_to_all | solution.py:115
  169.8 5.1 %all-to-all-start.5 = ((bf16[64,2,64,128]{3,2,1,0:T(8,128)(2,1)}), bf16[64,2,64,128]{3,2,1,0:T(8,128)(2,1)}, u32[]{:S(2)}, u32[]{:S(2)}) async-start(bf16[64,2,64,128]{3,2,1,0:T(8,128)(2,1)} %bitcast.30), calls=%async_computation.5 | async-start | bytes 4194304 | tf_op jit(solution)/shard_map/all_to_all | solution.py:115
  174.9 13.8 %shard_map.79 = bf16[128,64,128]{2,1,0:T(8,128)(2,1)} custom-call(s32[4,5]{1,0:T(4,128)} %reshape.63.order_ref, s32[4,6]{1,0:T(4,128)} %add_convert_fusion.flip_ref, bf16[20,256,256]{2,1,0:T(8,128)(2,1)} %fusion.2.gates_ref, bf16[128,64,128]{2,1,0:T(8,128)(2,1)} %bitcast.25), custom_call_target="tpu_custom_call" | custom-call | tf_op jit(solution)/shard_map/pallas_call | solution.py:102
  188.7 16.6 %all-to-all-done.5 = bf16[64,2,64,128]{3,2,1,0:T(8,128)(2,1)} async-done(((bf16[64,2,64,128]{3,2,1,0:T(8,128)(2,1)}), bf16[64,2,64,128]{3,2,1,0:T(8,128)(2,1)}, u32[]{:S(2)}, u32[]{:S(2)}) %all-to-all-start.5) | async-done | bytes 2097184 | tf_op jit(solution)/shard_map/all_to_all | solution.py:115
  205.3 4.9 %all-to-all-start.2 = ((bf16[64,2,64,128]{3,2,1,0:T(8,128)(2,1)}), bf16[64,2,64,128]{3,2,1,0:T(8,128)(2,1)S(1)}, u32[]{:S(2)}, u32[]{:S(2)}) async-start(bf16[64,2,64,128]{3,2,1,0:T(8,128)(2,1)} %bitcast.27), calls=%async_computation.2 | async-start | bytes 4194304 | tf_op jit(solution)/shard_map/all_to_all | solution.py:115
  210.2 7.5 %reshape.78 = bf16[4096,512]{1,0:T(8,128)(2,1)} reshape(bf16[128,128,128]{2,1,0:T(8,128)(2,1)} %param.7) | data formatting | bytes 8388608 | tf_op jit(solution)/shard_map/reshape | solution.py:161
  217.8 13.5 %shard_map.83.refs_1_ = bf16[128,128,128]{2,1,0:T(8,128)(2,1)} custom-call(s32[4,5]{1,0:T(4,128)} %reshape.63.order_ref, s32[4,6]{1,0:T(4,128)} %add_convert_fusion.flip_ref, bf16[20,256,256]{2,1,0:T(8,128)(2,1)} %fusion.2.gates_ref, bf16[128,64,128]{2,1,0:T(8,128)(2,1)} %bitcast.13.refs_0_), custom_call_target="tpu_custom_call" | custom-call | tf_op jit(solution)/shard_map/pallas_call | solution.py:102
  231.3 9.4 %all-to-all-done.2 = bf16[64,2,64,128]{3,2,1,0:T(8,128)(2,1)S(1)} async-done(((bf16[64,2,64,128]{3,2,1,0:T(8,128)(2,1)}), bf16[64,2,64,128]{3,2,1,0:T(8,128)(2,1)S(1)}, u32[]{:S(2)}, u32[]{:S(2)}) %all-to-all-start.2) | async-done | bytes 2097184 | tf_op jit(solution)/shard_map/all_to_all | solution.py:115
  240.7 1.4 copy-done.3
  242.1 13.5 %shard_map.84 = bf16[128,128,128]{2,1,0:T(8,128)(2,1)} custom-call(s32[4,5]{1,0:T(4,128)} %reshape.63.order_ref, s32[4,6]{1,0:T(4,128)} %add_convert_fusion.flip_ref, bf16[20,256,256]{2,1,0:T(8,128)(2,1)} %fusion.2.gates_ref, bf16[128,64,128]{2,1,0:T(8,128)(2,1)} %bitcast.31, bf16[128,128,128]{2,1,0:T(8,128)(2,1)} %shard_map.83.refs_1_), custom_call_target="tpu_custom_call", output_to_operand_aliasing={{}: (4, {})} | custom-call | tf_op jit(solution)/shard_map/pallas_call | solution.py:102
  255.6 7.6 %reshape.77 = bf16[4096,512]{1,0:T(8,128)(2,1)} reshape(bf16[128,128,128]{2,1,0:T(8,128)(2,1)} %shard_map.84) | data formatting | bytes 8388608 | tf_op jit(solution)/shard_map/reshape | solution.py:160
  263.2 5.8 %fusion.5 = bf16[512,512]{0,1:T(8,128)(2,1)S(1)} fusion(bf16[4096,512]{1,0:T(8,128)(2,1)} %reshape.77, bf16[4096,512]{1,0:T(8,128)(2,1)} %reshape.78), kind=kOutput, calls=%fused_computation.9 | convolution fusion | flops 2147745792 | bytes 8912896 | tf_op jit(solution)/shard_map/dot_general | solution.py:162
  269.6 21.7 %all_to_all.40 = bf16[128,16,128]{2,1,0:T(8,128)(2,1)S(1)} all-to-all(bf16[128,16,128]{2,1,0:T(8,128)(2,1)S(1)} %convert_element_type.25), channel_id=1, replica_groups=mesh['amp'=64,'grp'=2] {'amp','grp'}, dimensions={0} | all-to-all | bytes 1048576 | tf_op jit(solution)/shard_map/all_to_all | solution.py:122
  291.4 0.9 broadcast_in_dim.16
  292.2 4.9 %all-to-all-start.7 = ((bf16[128,16,128]{2,1,0:T(8,128)(2,1)}), bf16[128,16,128]{2,1,0:T(8,128)(2,1)S(1)}, u32[]{:S(2)}, u32[]{:S(2)}) async-start(bf16[128,16,128]{2,1,0:T(8,128)(2,1)} %broadcast_in_dim.16), calls=%async_computation.7 | async-start | bytes 1048576 | tf_op jit(solution)/shard_map/all_to_all | solution.py:125
  297.2 13.2 %all-to-all-done.7 = bf16[128,16,128]{2,1,0:T(8,128)(2,1)S(1)} async-done(((bf16[128,16,128]{2,1,0:T(8,128)(2,1)}), bf16[128,16,128]{2,1,0:T(8,128)(2,1)S(1)}, u32[]{:S(2)}, u32[]{:S(2)}) %all-to-all-start.7) | async-done | bytes 524320 | tf_op jit(solution)/shard_map/all_to_all | solution.py:125
  310.7 1.1 select_reduce_fusion
  312.4 1.5 fusion.4
  (22 shorter events, 4.2 us)
Async XLA Ops:
  0.6 5.0 %copy-start.4 = (s32[20]{0:T(128)S(1)}, s32[20]{0:T(128)}, u32[]{:S(2)}) copy-start(s32[20]{0:T(128)} %param.9) | copy-start | bytes 244
  19.2 42.9 %all-to-all-start.3 = ((bf16[64,2,64,128]{3,2,1,0:T(8,128)(2,1)}), bf16[64,2,64,128]{3,2,1,0:T(8,128)(2,1)S(1)}, u32[]{:S(2)}, u32[]{:S(2)}) async-start(bf16[64,2,64,128]{3,2,1,0:T(8,128)(2,1)} %bitcast.33), calls=%async_computation.3 | async-start | bytes 4194304 | tf_op jit(solution)/shard_map/all_to_all | solution.py:115
  62.1 1.3 copy-start.2
  63.4 35.4 %all-to-all-start = ((bf16[64,2,64,128]{3,2,1,0:T(8,128)(2,1)}), bf16[64,2,64,128]{3,2,1,0:T(8,128)(2,1)S(1)}, u32[]{:S(2)}, u32[]{:S(2)}) async-start(bf16[64,2,64,128]{3,2,1,0:T(8,128)(2,1)} %bitcast.32), calls=%async_computation | async-start | bytes 4194304 | tf_op jit(solution)/shard_map/all_to_all | solution.py:115
  98.8 5.1 %copy-start = (bf16[64,2,64,128]{3,2,1,0:T(8,128)(2,1)}, bf16[64,2,64,128]{3,2,1,0:T(8,128)(2,1)S(1)}, u32[]{:S(2)}) copy-start(bf16[64,2,64,128]{3,2,1,0:T(8,128)(2,1)S(1)} %all-to-all-done) | copy-start | bytes 6291460
  98.8 35.5 %all-to-all-start.4 = ((bf16[64,2,64,128]{3,2,1,0:T(8,128)(2,1)}), bf16[64,2,64,128]{3,2,1,0:T(8,128)(2,1)}, u32[]{:S(2)}, u32[]{:S(2)}) async-start(bf16[64,2,64,128]{3,2,1,0:T(8,128)(2,1)} %bitcast.28), calls=%async_computation.4 | async-start | bytes 4194304 | tf_op jit(solution)/shard_map/all_to_all | solution.py:115
  134.4 35.4 %all-to-all-start.1 = ((bf16[64,2,64,128]{3,2,1,0:T(8,128)(2,1)}), bf16[64,2,64,128]{3,2,1,0:T(8,128)(2,1)S(1)}, u32[]{:S(2)}, u32[]{:S(2)}) async-start(bf16[64,2,64,128]{3,2,1,0:T(8,128)(2,1)} %bitcast.29), calls=%async_computation.1 | async-start | bytes 4194304 | tf_op jit(solution)/shard_map/all_to_all | solution.py:115
  169.8 5.1 %copy-start.1 = (bf16[64,2,64,128]{3,2,1,0:T(8,128)(2,1)}, bf16[64,2,64,128]{3,2,1,0:T(8,128)(2,1)S(1)}, u32[]{:S(2)}) copy-start(bf16[64,2,64,128]{3,2,1,0:T(8,128)(2,1)S(1)} %all-to-all-done.1) | copy-start | bytes 6291460
  169.8 35.5 %all-to-all-start.5 = ((bf16[64,2,64,128]{3,2,1,0:T(8,128)(2,1)}), bf16[64,2,64,128]{3,2,1,0:T(8,128)(2,1)}, u32[]{:S(2)}, u32[]{:S(2)}) async-start(bf16[64,2,64,128]{3,2,1,0:T(8,128)(2,1)} %bitcast.30), calls=%async_computation.5 | async-start | bytes 4194304 | tf_op jit(solution)/shard_map/all_to_all | solution.py:115
  205.3 35.4 %all-to-all-start.2 = ((bf16[64,2,64,128]{3,2,1,0:T(8,128)(2,1)}), bf16[64,2,64,128]{3,2,1,0:T(8,128)(2,1)S(1)}, u32[]{:S(2)}, u32[]{:S(2)}) async-start(bf16[64,2,64,128]{3,2,1,0:T(8,128)(2,1)} %bitcast.27), calls=%async_computation.2 | async-start | bytes 4194304 | tf_op jit(solution)/shard_map/all_to_all | solution.py:115
  240.7 1.4 copy-start.3
  292.2 18.1 %all-to-all-start.7 = ((bf16[128,16,128]{2,1,0:T(8,128)(2,1)}), bf16[128,16,128]{2,1,0:T(8,128)(2,1)S(1)}, u32[]{:S(2)}, u32[]{:S(2)}) async-start(bf16[128,16,128]{2,1,0:T(8,128)(2,1)} %broadcast_in_dim.16), calls=%async_computation.7 | async-start | bytes 1048576 | tf_op jit(solution)/shard_map/all_to_all | solution.py:125

commit v6 on v5

--- a/solution.py
+++ b/solution.py
@@ -147,21 +147,21 @@
         elif segment < SEGS - 1:
             chunks = [run_segment([part], gates_bd, order, flips, segment, False, False, chunk) for part in chunks]
         else:
-            current = None
-            for c, part in enumerate(chunks):
-                current = run_segment(
-                    [part], gates_bd, order, flips, segment, False, True, chunk,
-                    into=current, out_offset=c * (chunk // BLOCK), out_slabs=slabs,
-                )
+            finals = [run_segment([part], gates_bd, order, flips, segment, False, True, chunk) for part in chunks]
         if segment < SEGS - 1:
             chunks = [swap_major(part) for part in chunks]
     order = 4 * amplitudes.shape[2]
     owned_rows = order // lax.axis_size("grp")
-    flattened = current.reshape(-1, order)
     adjoint_flat = adjoint.reshape(-1, order)
-    partial_correlation = lax.dot_general(
-        adjoint_flat, flattened, (((0,), (0,)), ((), ())), preferred_element_type=jnp.float32
+    rows = adjoint_flat.shape[0] // CHUNKS
+    partial_correlation = sum(
+        lax.dot_general(
+            adjoint_flat[c * rows:(c + 1) * rows], final.reshape(-1, order), (((0,), (0,)), ((), ())),
+            preferred_element_type=jnp.float32,
+        )
+        for c, final in enumerate(finals)
     )
+    current = jnp.concatenate(finals, axis=0)
     summed = all_sum(partial_correlation, ("amp", "grp"))
     owned = lax.dynamic_slice_in_dim(summed, lax.axis_index("grp") * owned_rows, owned_rows, 0)
     gram = lax.dot_general(

time: 315 us -> 317 us (level)
  waiting for transfers between devices: 110 us -> 95.1 us
  Pallas kernels: 104 us -> 110 us
  local copies, waits for them, and re-layouts: 21.2 us -> 27.2 us
  other arithmetic: 4.98 us -> 8.89 us
    all_to_all x6, waiting for transfers between devices: 97.2 us -> 85.9 us  [swap_major(): lax.all_to_all(split, 'amp', split_axis=0, concat_axis=0, tiled=True)]
    slice x0 -> x3, local copies, waits for them, and re-layouts: none -> 9.73 us  [on_device(): adjoint_flat[c * rows:(c + 1) * rows]]
    reshape x2, local copies, waits for them, and re-layouts: 15.1 us -> 8.74 us  [on_device(): final.reshape(-1, order)]
    pallas_call x8, Pallas kernels: 104 us -> 110 us  [run_segment(): pl.pallas_call(make_kernel(slab_in, slab_out, len(sources), per_source, s...]
    all_to_all x1, waiting for transfers between devices: 13.2 us -> 9.21 us  [all_sum(): lax.all_to_all(spread, axes, split_axis=0, concat_axis=0, tiled=True)]
    concatenate x0 -> x1, other arithmetic: none -> 3.97 us  [on_device(): current = jnp.concatenate(finals, axis=0)]
  transfers between devices with their start and end apart: 7 -> 7, of which waited for: 7 -> 7; matrix products, arithmetic and copies ran while one was open for 2% -> 6% of each run, Pallas kernels for 25% -> 26%
where the time goes in v6:
time: 317 us
  Pallas kernels  110 us (35%)
  waiting for transfers between devices  95.1 us (30%)
  starting transfers between devices  42.6 us (13%)
  local copies, waits for them, and re-layouts  27.2 us (9%)
  blocking collectives  24.8 us (8%)
  other arithmetic  8.89 us (3%)
  matrix products  7.47 us (2%)
    pallas_call x8, Pallas kernels, run_segment(): pl.pallas_call(make_kernel(slab_in, slab_out, len(sources), per_source, s...  110 us
    all_to_all x6, waiting for transfers between devices, swap_major(): lax.all_to_all(split, 'amp', split_axis=0, concat_axis=0, tiled=True)  85.9 us
    all_to_all x6, starting transfers between devices, swap_major(): lax.all_to_all(split, 'amp', split_axis=0, concat_axis=0, tiled=True)  37.7 us
    all_to_all x1, blocking collectives, all_sum(): lax.all_to_all(pieces, axes, split_axis=0, concat_axis=0, tiled=True)  24.8 us
    slice x3, local copies, waits for them, and re-layouts, on_device(): adjoint_flat[c * rows:(c + 1) * rows]  9.73 us
    all_to_all x1, waiting for transfers between devices, all_sum(): lax.all_to_all(spread, axes, split_axis=0, concat_axis=0, tiled=True)  9.21 us
    reshape x2, local copies, waits for them, and re-layouts, on_device(): final.reshape(-1, order)  8.74 us
  transfers between devices with their start and end apart: 7, of which 7 were waited for; matrix products, arithmetic and copies ran while one was open for 6% of the time, Pallas kernels for 26%

profile of v6, /device:TPU:1, one launch (start us, length us, event | category | flops | bytes accessed | tf_op | source)
XLA Modules:
  0.0 317.1 jit_solution(1777218937344913750)
XLA Ops:
  2.4 3.2 %fusion.2.gates_ref = bf16[20,256,256]{2,1,0:T(8,128)(2,1)} fusion(bf16[20,128,128]{2,1,0:T(8,128)(2,1)} %param.8), kind=kLoop, calls=%fused_computation.5 | loop fusion | flops 10485760 | bytes 3276800 | tf_op jit(solution)/shard_map/concatenate | solution.py:69
  7.0 12.1 %shard_map.77 = bf16[128,64,128]{2,1,0:T(8,128)(2,1)} custom-call(s32[4,5]{1,0:T(4,128)} %reshape.66.order_ref, s32[4,6]{1,0:T(4,128)} %add_convert_fusion.flip_ref, bf16[20,256,256]{2,1,0:T(8,128)(2,1)} %fusion.2.gates_ref, bf16[128,128,128]{2,1,0:T(8,128)(2,1)} %refs_0_.3), custom_call_target="tpu_custom_call" | custom-call | tf_op jit(solution)/shard_map/pallas_call | solution.py:102
  19.1 12.5 %all-to-all-start = ((bf16[64,2,64,128]{3,2,1,0:T(8,128)(2,1)}), bf16[64,2,64,128]{3,2,1,0:T(8,128)(2,1)S(1)}, u32[]{:S(2)}, u32[]{:S(2)}) async-start(bf16[64,2,64,128]{3,2,1,0:T(8,128)(2,1)} %bitcast.35), calls=%async_computation | async-start | bytes 4194304 | tf_op jit(solution)/shard_map/all_to_all | solution.py:115
  31.6 12.1 %shard_map.81 = bf16[128,64,128]{2,1,0:T(8,128)(2,1)} custom-call(s32[4,5]{1,0:T(4,128)} %reshape.66.order_ref, s32[4,6]{1,0:T(4,128)} %add_convert_fusion.flip_ref, bf16[20,256,256]{2,1,0:T(8,128)(2,1)} %fusion.2.gates_ref, bf16[128,128,128]{2,1,0:T(8,128)(2,1)} %refs_0_.3), custom_call_target="tpu_custom_call" | custom-call | tf_op jit(solution)/shard_map/pallas_call | solution.py:102
  43.7 18.4 %all-to-all-done = bf16[64,2,64,128]{3,2,1,0:T(8,128)(2,1)S(1)} async-done(((bf16[64,2,64,128]{3,2,1,0:T(8,128)(2,1)}), bf16[64,2,64,128]{3,2,1,0:T(8,128)(2,1)S(1)}, u32[]{:S(2)}, u32[]{:S(2)}) %all-to-all-start) | async-done | bytes 2097184 | tf_op jit(solution)/shard_map/all_to_all | solution.py:115
  63.4 4.9 %all-to-all-start.3 = ((bf16[64,2,64,128]{3,2,1,0:T(8,128)(2,1)}), bf16[64,2,64,128]{3,2,1,0:T(8,128)(2,1)S(1)}, u32[]{:S(2)}, u32[]{:S(2)}) async-start(bf16[64,2,64,128]{3,2,1,0:T(8,128)(2,1)} %bitcast.34), calls=%async_computation.3 | async-start | bytes 4194304 | tf_op jit(solution)/shard_map/all_to_all | solution.py:115
  68.4 13.9 %shard_map.78 = bf16[128,64,128]{2,1,0:T(8,128)(2,1)} custom-call(s32[4,5]{1,0:T(4,128)} %reshape.66.order_ref, s32[4,6]{1,0:T(4,128)} %add_convert_fusion.flip_ref, bf16[20,256,256]{2,1,0:T(8,128)(2,1)} %fusion.2.gates_ref, bf16[128,64,128]{2,1,0:T(8,128)(2,1)} %bitcast.30), custom_call_target="tpu_custom_call" | custom-call | tf_op jit(solution)/shard_map/pallas_call | solution.py:102
  82.3 16.6 %all-to-all-done.3 = bf16[64,2,64,128]{3,2,1,0:T(8,128)(2,1)S(1)} async-done(((bf16[64,2,64,128]{3,2,1,0:T(8,128)(2,1)}), bf16[64,2,64,128]{3,2,1,0:T(8,128)(2,1)S(1)}, u32[]{:S(2)}, u32[]{:S(2)}) %all-to-all-start.3) | async-done | bytes 2097184 | tf_op jit(solution)/shard_map/all_to_all | solution.py:115
  100.2 5.1 %all-to-all-start.1 = ((bf16[64,2,64,128]{3,2,1,0:T(8,128)(2,1)}), bf16[64,2,64,128]{3,2,1,0:T(8,128)(2,1)}, u32[]{:S(2)}, u32[]{:S(2)}) async-start(bf16[64,2,64,128]{3,2,1,0:T(8,128)(2,1)} %bitcast.31), calls=%async_computation.1 | async-start | bytes 4194304 | tf_op jit(solution)/shard_map/all_to_all | solution.py:115
  105.3 13.9 %shard_map.82 = bf16[128,64,128]{2,1,0:T(8,128)(2,1)} custom-call(s32[4,5]{1,0:T(4,128)} %reshape.66.order_ref, s32[4,6]{1,0:T(4,128)} %add_convert_fusion.flip_ref, bf16[20,256,256]{2,1,0:T(8,128)(2,1)} %fusion.2.gates_ref, bf16[128,64,128]{2,1,0:T(8,128)(2,1)} %bitcast.28), custom_call_target="tpu_custom_call" | custom-call | tf_op jit(solution)/shard_map/pallas_call | solution.py:102
  119.2 16.5 %all-to-all-done.1 = bf16[64,2,64,128]{3,2,1,0:T(8,128)(2,1)} async-done(((bf16[64,2,64,128]{3,2,1,0:T(8,128)(2,1)}), bf16[64,2,64,128]{3,2,1,0:T(8,128)(2,1)}, u32[]{:S(2)}, u32[]{:S(2)}) %all-to-all-start.1) | async-done | bytes 2097184 | tf_op jit(solution)/shard_map/all_to_all | solution.py:115
  135.7 4.9 %all-to-all-start.4 = ((bf16[64,2,64,128]{3,2,1,0:T(8,128)(2,1)}), bf16[64,2,64,128]{3,2,1,0:T(8,128)(2,1)S(1)}, u32[]{:S(2)}, u32[]{:S(2)}) async-start(bf16[64,2,64,128]{3,2,1,0:T(8,128)(2,1)} %bitcast.32), calls=%async_computation.4 | async-start | bytes 4194304 | tf_op jit(solution)/shard_map/all_to_all | solution.py:115
  140.6 13.8 %shard_map.79 = bf16[128,64,128]{2,1,0:T(8,128)(2,1)} custom-call(s32[4,5]{1,0:T(4,128)} %reshape.66.order_ref, s32[4,6]{1,0:T(4,128)} %add_convert_fusion.flip_ref, bf16[20,256,256]{2,1,0:T(8,128)(2,1)} %fusion.2.gates_ref, bf16[128,64,128]{2,1,0:T(8,128)(2,1)} %bitcast.5.refs_0_), custom_call_target="tpu_custom_call" | custom-call | tf_op jit(solution)/shard_map/pallas_call | solution.py:102
  154.5 16.7 %all-to-all-done.4 = bf16[64,2,64,128]{3,2,1,0:T(8,128)(2,1)S(1)} async-done(((bf16[64,2,64,128]{3,2,1,0:T(8,128)(2,1)}), bf16[64,2,64,128]{3,2,1,0:T(8,128)(2,1)S(1)}, u32[]{:S(2)}, u32[]{:S(2)}) %all-to-all-start.4) | async-done | bytes 2097184 | tf_op jit(solution)/shard_map/all_to_all | solution.py:115
  172.5 4.9 %all-to-all-start.2 = ((bf16[64,2,64,128]{3,2,1,0:T(8,128)(2,1)}), bf16[64,2,64,128]{3,2,1,0:T(8,128)(2,1)S(1)}, u32[]{:S(2)}, u32[]{:S(2)}) async-start(bf16[64,2,64,128]{3,2,1,0:T(8,128)(2,1)} %bitcast.33), calls=%async_computation.2 | async-start | bytes 4194304 | tf_op jit(solution)/shard_map/all_to_all | solution.py:115
  177.4 13.9 %shard_map.83 = bf16[128,64,128]{2,1,0:T(8,128)(2,1)} custom-call(s32[4,5]{1,0:T(4,128)} %reshape.66.order_ref, s32[4,6]{1,0:T(4,128)} %add_convert_fusion.flip_ref, bf16[20,256,256]{2,1,0:T(8,128)(2,1)} %fusion.2.gates_ref, bf16[128,64,128]{2,1,0:T(8,128)(2,1)} %bitcast.29), custom_call_target="tpu_custom_call" | custom-call | tf_op jit(solution)/shard_map/pallas_call | solution.py:102
  191.3 16.6 %all-to-all-done.2 = bf16[64,2,64,128]{3,2,1,0:T(8,128)(2,1)S(1)} async-done(((bf16[64,2,64,128]{3,2,1,0:T(8,128)(2,1)}), bf16[64,2,64,128]{3,2,1,0:T(8,128)(2,1)S(1)}, u32[]{:S(2)}, u32[]{:S(2)}) %all-to-all-start.2) | async-done | bytes 2097184 | tf_op jit(solution)/shard_map/all_to_all | solution.py:115
  207.9 1.4 copy-done.1
  209.3 5.3 %all-to-all-start.5 = ((bf16[64,2,64,128]{3,2,1,0:T(8,128)(2,1)}), bf16[64,2,64,128]{3,2,1,0:T(8,128)(2,1)}, u32[]{:S(2)}, u32[]{:S(2)}) async-start(bf16[64,2,64,128]{3,2,1,0:T(8,128)(2,1)} %bitcast.27), calls=%async_computation.5 | async-start | bytes 4194304 | tf_op jit(solution)/shard_map/all_to_all | solution.py:115
  214.6 4.0 %fusion.10 = (bf16[64,128,128]{2,1,0:T(8,128)(2,1)}, bf16[64,128,128]{2,1,0:T(8,128)(2,1)S(1)}) fusion(bf16[128,128,128]{2,1,0:T(8,128)(2,1)} %param.7), kind=kLoop, calls=%fused_computation.23 | loop fusion | bytes 8388608 | tf_op jit(solution)/shard_map/slice | solution.py:159
  218.7 2.6 slice.21
  221.2 3.1 slice.23
  224.4 15.0 %shard_map.80 = bf16[64,128,128]{2,1,0:T(8,128)(2,1)} custom-call(s32[4,5]{1,0:T(4,128)} %reshape.66.order_ref, s32[4,6]{1,0:T(4,128)} %add_convert_fusion.flip_ref, bf16[20,256,256]{2,1,0:T(8,128)(2,1)} %fusion.2.gates_ref, bf16[128,64,128]{2,1,0:T(8,128)(2,1)} %bitcast.26), custom_call_target="tpu_custom_call" | custom-call | tf_op jit(solution)/shard_map/pallas_call | solution.py:102
  239.4 4.4 %reshape.80 = bf16[2048,512]{1,0:T(8,128)(2,1)} reshape(bf16[64,128,128]{2,1,0:T(8,128)(2,1)} %shard_map.80) | data formatting | bytes 4194304 | tf_op jit(solution)/shard_map/reshape | solution.py:159
  244.8 15.0 %shard_map.84 = bf16[64,128,128]{2,1,0:T(8,128)(2,1)} custom-call(s32[4,5]{1,0:T(4,128)} %reshape.66.order_ref, s32[4,6]{1,0:T(4,128)} %add_convert_fusion.flip_ref, bf16[20,256,256]{2,1,0:T(8,128)(2,1)} %fusion.2.gates_ref, bf16[128,64,128]{2,1,0:T(8,128)(2,1)} %bitcast.13.refs_0_), custom_call_target="tpu_custom_call" | custom-call | tf_op jit(solution)/shard_map/pallas_call | solution.py:102
  259.8 4.3 %reshape.81 = bf16[2048,512]{1,0:T(8,128)(2,1)} reshape(bf16[64,128,128]{2,1,0:T(8,128)(2,1)} %shard_map.84) | data formatting | bytes 4194304 | tf_op jit(solution)/shard_map/reshape | solution.py:159
  264.2 3.6 %fusion.11 = f32[512,512]{1,0:T(8,128)S(1)} fusion(bf16[2048,512]{1,0:T(8,128)(2,1)} %reshape.80, bf16[2048,512]{1,0:T(8,128)(2,1)} %slice.21), kind=kOutput, calls=%fused_computation.24 | convolution fusion | flops 1073741824 | bytes 5242880 | tf_op jit(solution)/shard_map/dot_general | solution.py:158
  269.7 24.8 %all_to_all.40 = bf16[128,16,128]{2,1,0:T(8,128)(2,1)S(1)} all-to-all(bf16[128,16,128]{2,1,0:T(8,128)(2,1)S(1)} %convert_element_type.25), channel_id=1, replica_groups=mesh['amp'=64,'grp'=2] {'amp','grp'}, dimensions={0} | all-to-all | bytes 1048576 | tf_op jit(solution)/shard_map/all_to_all | solution.py:122
  295.5 4.9 %all-to-all-start.7 = ((bf16[128,16,128]{2,1,0:T(8,128)(2,1)}), bf16[128,16,128]{2,1,0:T(8,128)(2,1)S(1)}, u32[]{:S(2)}, u32[]{:S(2)}) async-start(bf16[128,16,128]{2,1,0:T(8,128)(2,1)} %broadcast_in_dim.16), calls=%async_computation.7 | async-start | bytes 1048576 | tf_op jit(solution)/shard_map/all_to_all | solution.py:125
  300.4 4.0 %pad_maximum_fusion = bf16[128,128,128]{2,1,0:T(8,128)(2,1)} fusion(bf16[64,128,128]{2,1,0:T(8,128)(2,1)} %shard_map.84, bf16[64,128,128]{2,1,0:T(8,128)(2,1)S(1)} %copy-done), kind=kLoop, calls=%fused_computation.4 | loop fusion | flops 2097152 | bytes 8388608 | tf_op jit(solution)/shard_map/concatenate | solution.py:164
  304.4 9.2 %all-to-all-done.7 = bf16[128,16,128]{2,1,0:T(8,128)(2,1)S(1)} async-done(((bf16[128,16,128]{2,1,0:T(8,128)(2,1)}), bf16[128,16,128]{2,1,0:T(8,128)(2,1)S(1)}, u32[]{:S(2)}, u32[]{:S(2)}) %all-to-all-start.7) | async-done | bytes 524320 | tf_op jit(solution)/shard_map/all_to_all | solution.py:125
  315.7 1.5 fusion.6
  (31 shorter events, 12.5 us)
Async XLA Ops:
  0.6 4.9 %copy-start.6 = (s32[20]{0:T(128)S(1)}, s32[20]{0:T(128)}, u32[]{:S(2)}) copy-start(s32[20]{0:T(128)} %param.9) | copy-start | bytes 244
  19.1 43.0 %all-to-all-start = ((bf16[64,2,64,128]{3,2,1,0:T(8,128)(2,1)}), bf16[64,2,64,128]{3,2,1,0:T(8,128)(2,1)S(1)}, u32[]{:S(2)}, u32[]{:S(2)}) async-start(bf16[64,2,64,128]{3,2,1,0:T(8,128)(2,1)} %bitcast.35), calls=%async_computation | async-start | bytes 4194304 | tf_op jit(solution)/shard_map/all_to_all | solution.py:115
  62.1 1.4 copy-start.4
  63.4 35.4 %all-to-all-start.3 = ((bf16[64,2,64,128]{3,2,1,0:T(8,128)(2,1)}), bf16[64,2,64,128]{3,2,1,0:T(8,128)(2,1)S(1)}, u32[]{:S(2)}, u32[]{:S(2)}) async-start(bf16[64,2,64,128]{3,2,1,0:T(8,128)(2,1)} %bitcast.34), calls=%async_computation.3 | async-start | bytes 4194304 | tf_op jit(solution)/shard_map/all_to_all | solution.py:115
  98.9 1.3 copy-start.2
  100.2 35.5 %all-to-all-start.1 = ((bf16[64,2,64,128]{3,2,1,0:T(8,128)(2,1)}), bf16[64,2,64,128]{3,2,1,0:T(8,128)(2,1)}, u32[]{:S(2)}, u32[]{:S(2)}) async-start(bf16[64,2,64,128]{3,2,1,0:T(8,128)(2,1)} %bitcast.31), calls=%async_computation.1 | async-start | bytes 4194304 | tf_op jit(solution)/shard_map/all_to_all | solution.py:115
  135.7 35.4 %all-to-all-start.4 = ((bf16[64,2,64,128]{3,2,1,0:T(8,128)(2,1)}), bf16[64,2,64,128]{3,2,1,0:T(8,128)(2,1)S(1)}, u32[]{:S(2)}, u32[]{:S(2)}) async-start(bf16[64,2,64,128]{3,2,1,0:T(8,128)(2,1)} %bitcast.32), calls=%async_computation.4 | async-start | bytes 4194304 | tf_op jit(solution)/shard_map/all_to_all | solution.py:115
  171.1 1.4 copy-start.3
  172.5 35.4 %all-to-all-start.2 = ((bf16[64,2,64,128]{3,2,1,0:T(8,128)(2,1)}), bf16[64,2,64,128]{3,2,1,0:T(8,128)(2,1)S(1)}, u32[]{:S(2)}, u32[]{:S(2)}) async-start(bf16[64,2,64,128]{3,2,1,0:T(8,128)(2,1)} %bitcast.33), calls=%async_computation.2 | async-start | bytes 4194304 | tf_op jit(solution)/shard_map/all_to_all | solution.py:115
  207.9 1.4 copy-start.1
  209.3 35.5 %all-to-all-start.5 = ((bf16[64,2,64,128]{3,2,1,0:T(8,128)(2,1)}), bf16[64,2,64,128]{3,2,1,0:T(8,128)(2,1)}, u32[]{:S(2)}, u32[]{:S(2)}) async-start(bf16[64,2,64,128]{3,2,1,0:T(8,128)(2,1)} %bitcast.27), calls=%async_computation.5 | async-start | bytes 4194304 | tf_op jit(solution)/shard_map/all_to_all | solution.py:115
  264.2 3.6 %copy-start.5 = (bf16[2048,512]{1,0:T(8,128)(2,1)S(1)}, bf16[2048,512]{1,0:T(8,128)(2,1)}, u32[]{:S(2)}) copy-start(bf16[2048,512]{1,0:T(8,128)(2,1)} %reshape.81) | copy-start | bytes 6291460
  269.3 31.1 %copy-start = (bf16[64,128,128]{2,1,0:T(8,128)(2,1)S(1)}, bf16[64,128,128]{2,1,0:T(8,128)(2,1)}, u32[]{:S(2)}) copy-start(bf16[64,128,128]{2,1,0:T(8,128)(2,1)} %shard_map.80) | copy-start | bytes 6291460
  295.5 18.1 %all-to-all-start.7 = ((bf16[128,16,128]{2,1,0:T(8,128)(2,1)}), bf16[128,16,128]{2,1,0:T(8,128)(2,1)S(1)}, u32[]{:S(2)}, u32[]{:S(2)}) async-start(bf16[128,16,128]{2,1,0:T(8,128)(2,1)} %broadcast_in_dim.16), calls=%async_computation.7 | async-start | bytes 1048576 | tf_op jit(solution)/shard_map/all_to_all | solution.py:125

commit v7 on v6

--- a/solution.py
+++ b/solution.py
@@ -13,9 +13,17 @@
 
 def make_kernel(slab_in, slab_out, sources, blocks_per_source, segment):
     def kernel(order_ref, flip_ref, gates_ref, *refs):
-        x_refs, o_ref, held = refs[:sources], refs[-2], refs[-1]
+        x_refs, o_ref, held, diagonal = refs[:sources], refs[-3], refs[-2], refs[-1]
         half, wide, pair = held.shape
         lanes = pair // 2
+
+        @pl.when(pl.program_id(0) == 0)
+        def _():
+            diagonal[...] = jnp.zeros(diagonal.shape, diagonal.dtype)
+            for position in range(GATES):
+                matrix = gates_ref[order_ref[segment, position]]
+                diagonal[position, :lanes, :lanes] = matrix
+                diagonal[position, lanes:, lanes:] = matrix
 
         def load(x_ref):
             if slab_in:
@@ -39,7 +47,7 @@
 
         def one_gate(position, carry):
             pl.when(flip_ref[segment, position] == 1)(flip)
-            matrix = gates_ref[order_ref[segment, position]]
+            matrix = diagonal[position]
             flat = held[...].reshape(half * wide, pair)
             out = lax.dot_general(
                 flat, matrix, (((1,), (1,)), ((), ())), preferred_element_type=jnp.float32
@@ -62,16 +70,9 @@
     return kernel
 
 
-def block_diagonal(gate_mats):
-    zeros = jnp.zeros_like(gate_mats)
-    top = jnp.concatenate([gate_mats, zeros], axis=2)
-    bottom = jnp.concatenate([zeros, gate_mats], axis=2)
-    return jnp.concatenate([top, bottom], axis=1)
-
-
-def run_segment(sources, gates_bd, order, flips, segment, slab_in, slab_out, slabs, offset=0,
+def run_segment(sources, gate_mats, order, flips, segment, slab_in, slab_out, slabs, offset=0,
                 into=None, out_offset=0, out_slabs=None):
-    wide = gates_bd.shape[1] // 2
+    wide = gate_mats.shape[1]
     lanes = sources[0].shape[2]
     blocks = slabs // BLOCK
     per_source = blocks // len(sources)
@@ -93,11 +94,14 @@
     grid_spec = pltpu.PrefetchScalarGridSpec(
         num_scalar_prefetch=2,
         grid=(blocks,),
-        in_specs=[pl.BlockSpec(gates_bd.shape, lambda i, o, f: (0, 0, 0))]
+        in_specs=[pl.BlockSpec(gate_mats.shape, lambda i, o, f: (0, 0, 0))]
         + [source_spec(index) for index in range(len(sources))]
         + ([] if into is None else [pl.BlockSpec(memory_space=pl.ANY)]),
         out_specs=out_spec,
-        scratch_shapes=[pltpu.VMEM((BLOCK // 2, wide, 2 * lanes), jnp.bfloat16)],
+        scratch_shapes=[
+            pltpu.VMEM((BLOCK // 2, wide, 2 * lanes), jnp.bfloat16),
+            pltpu.VMEM((GATES, 2 * wide, 2 * lanes), jnp.bfloat16),
+        ],
     )
     return pl.pallas_call(
         make_kernel(slab_in, slab_out, len(sources), per_source, segment),
@@ -105,7 +109,7 @@
         out_shape=jax.ShapeDtypeStruct(out_shape, sources[0].dtype),
         compiler_params=pltpu.CompilerParams(dimension_semantics=("arbitrary",)),
         input_output_aliases={} if into is None else {3 + len(sources): 0},
-    )(order, flips, gates_bd, *sources, *([] if into is None else [into]))
+    )(order, flips, gate_mats, *sources, *([] if into is None else [into]))
 
 
 def swap_major(values):
@@ -127,7 +131,6 @@
 
 
 def on_device(amplitudes, adjoint, gate_mats, gate_order, gate_window, swap_window):
-    gates_bd = block_diagonal(gate_mats)
     slabs = amplitudes.shape[0]
     chunk = slabs // CHUNKS
     windows = gate_window.reshape(SEGS, GATES)
@@ -141,13 +144,13 @@
     for segment in range(SEGS):
         if segment == 0:
             chunks = [
-                run_segment([amplitudes], gates_bd, order, flips, segment, True, False, chunk, c * (chunk // BLOCK))
+                run_segment([amplitudes], gate_mats, order, flips, segment, True, False, chunk, c * (chunk // BLOCK))
                 for c in range(CHUNKS)
             ]
         elif segment < SEGS - 1:
-            chunks = [run_segment([part], gates_bd, order, flips, segment, False, False, chunk) for part in chunks]
+            chunks = [run_segment([part], gate_mats, order, flips, segment, False, False, chunk) for part in chunks]
         else:
-            finals = [run_segment([part], gates_bd, order, flips, segment, False, True, chunk) for part in chunks]
+            finals = [run_segment([part], gate_mats, order, flips, segment, False, True, chunk) for part in chunks]
         if segment < SEGS - 1:
             chunks = [swap_major(part) for part in chunks]
     order = 4 * amplitudes.shape[2]

time: 317 us -> 314 us (level)
  other arithmetic: 8.89 us -> 5.72 us
    concatenate x1 -> x0, other arithmetic: 3.18 us -> none  [block_diagonal(): return jnp.concatenate([top, bottom], axis=1)]
where the time goes in v7:
time: 314 us; the launch traced here: 313 us
  Pallas kernels  108 us (34%)
  waiting for transfers between devices  97 us (31%)
  starting transfers between devices  42.6 us (14%)
  local copies, waits for them, and re-layouts  27.6 us (9%)
  blocking collectives  23.9 us (8%)
  matrix products  7.48 us (2%)
  other arithmetic  5.72 us (2%)
    pallas_call x8, Pallas kernels, run_segment(): pl.pallas_call(make_kernel(slab_in, slab_out, len(sources), per_source, s...  108 us
    all_to_all x6, waiting for transfers between devices, swap_major(): lax.all_to_all(split, 'amp', split_axis=0, concat_axis=0, tiled=True)  87.8 us
    all_to_all x6, starting transfers between devices, swap_major(): lax.all_to_all(split, 'amp', split_axis=0, concat_axis=0, tiled=True)  37.6 us
    all_to_all x1, blocking collectives, all_sum(): lax.all_to_all(pieces, axes, split_axis=0, concat_axis=0, tiled=True)  23.9 us
    slice x3, local copies, waits for them, and re-layouts, on_device(): adjoint_flat[c * rows:(c + 1) * rows]  9.67 us
    all_to_all x1, waiting for transfers between devices, all_sum(): lax.all_to_all(spread, axes, split_axis=0, concat_axis=0, tiled=True)  9.21 us
    reshape x2, local copies, waits for them, and re-layouts, on_device(): final.reshape(-1, order)  8.69 us
  transfers between devices with their start and end apart: 7, of which 7 were waited for; matrix products, arithmetic and copies ran while one was open for 6% of the time, Pallas kernels for 26%

profile of v7, /device:TPU:1, one launch (start us, length us, event | category | flops | bytes accessed | tf_op | source)
XLA Modules:
  0.0 313.3 jit_solution(7157511515839963264)
XLA Ops:
  4.5 12.2 %shard_map.77 = bf16[128,64,128]{2,1,0:T(8,128)(2,1)} custom-call(s32[4,5]{1,0:T(4,128)} %reshape.66.order_ref, s32[4,6]{1,0:T(4,128)} %add_convert_fusion.flip_ref, bf16[20,128,128]{2,1,0:T(8,128)(2,1)} %gates_ref.15, bf16[128,128,128]{2,1,0:T(8,128)(2,1)} %refs_0_.3), custom_call_target="tpu_custom_call" | custom-call | tf_op jit(solution)/shard_map/pallas_call | solution.py:106
  16.7 12.4 %all-to-all-start = ((bf16[64,2,64,128]{3,2,1,0:T(8,128)(2,1)}), bf16[64,2,64,128]{3,2,1,0:T(8,128)(2,1)S(1)}, u32[]{:S(2)}, u32[]{:S(2)}) async-start(bf16[64,2,64,128]{3,2,1,0:T(8,128)(2,1)} %bitcast.27), calls=%async_computation | async-start | bytes 4194304 | tf_op jit(solution)/shard_map/all_to_all | solution.py:119
  29.2 12.2 %shard_map.81 = bf16[128,64,128]{2,1,0:T(8,128)(2,1)} custom-call(s32[4,5]{1,0:T(4,128)} %reshape.66.order_ref, s32[4,6]{1,0:T(4,128)} %add_convert_fusion.flip_ref, bf16[20,128,128]{2,1,0:T(8,128)(2,1)} %gates_ref.15, bf16[128,128,128]{2,1,0:T(8,128)(2,1)} %refs_0_.3), custom_call_target="tpu_custom_call" | custom-call | tf_op jit(solution)/shard_map/pallas_call | solution.py:106
  41.4 18.3 %all-to-all-done = bf16[64,2,64,128]{3,2,1,0:T(8,128)(2,1)S(1)} async-done(((bf16[64,2,64,128]{3,2,1,0:T(8,128)(2,1)}), bf16[64,2,64,128]{3,2,1,0:T(8,128)(2,1)S(1)}, u32[]{:S(2)}, u32[]{:S(2)}) %all-to-all-start) | async-done | bytes 2097184 | tf_op jit(solution)/shard_map/all_to_all | solution.py:119
  59.7 1.3 copy-done.4
  61.0 4.9 %all-to-all-start.3 = ((bf16[64,2,64,128]{3,2,1,0:T(8,128)(2,1)}), bf16[64,2,64,128]{3,2,1,0:T(8,128)(2,1)S(1)}, u32[]{:S(2)}, u32[]{:S(2)}) async-start(bf16[64,2,64,128]{3,2,1,0:T(8,128)(2,1)} %bitcast.26), calls=%async_computation.3 | async-start | bytes 4194304 | tf_op jit(solution)/shard_map/all_to_all | solution.py:119
  65.9 13.2 %shard_map.78 = bf16[128,64,128]{2,1,0:T(8,128)(2,1)} custom-call(s32[4,5]{1,0:T(4,128)} %reshape.66.order_ref, s32[4,6]{1,0:T(4,128)} %add_convert_fusion.flip_ref, bf16[20,128,128]{2,1,0:T(8,128)(2,1)} %gates_ref.15, bf16[128,64,128]{2,1,0:T(8,128)(2,1)} %bitcast.32), custom_call_target="tpu_custom_call" | custom-call | tf_op jit(solution)/shard_map/pallas_call | solution.py:106
  79.2 17.2 %all-to-all-done.3 = bf16[64,2,64,128]{3,2,1,0:T(8,128)(2,1)S(1)} async-done(((bf16[64,2,64,128]{3,2,1,0:T(8,128)(2,1)}), bf16[64,2,64,128]{3,2,1,0:T(8,128)(2,1)S(1)}, u32[]{:S(2)}, u32[]{:S(2)}) %all-to-all-start.3) | async-done | bytes 2097184 | tf_op jit(solution)/shard_map/all_to_all | solution.py:119
  97.7 5.1 %all-to-all-start.1 = ((bf16[64,2,64,128]{3,2,1,0:T(8,128)(2,1)}), bf16[64,2,64,128]{3,2,1,0:T(8,128)(2,1)}, u32[]{:S(2)}, u32[]{:S(2)}) async-start(bf16[64,2,64,128]{3,2,1,0:T(8,128)(2,1)} %bitcast.33), calls=%async_computation.1 | async-start | bytes 4194304 | tf_op jit(solution)/shard_map/all_to_all | solution.py:119
  102.9 13.2 %shard_map.82 = bf16[128,64,128]{2,1,0:T(8,128)(2,1)} custom-call(s32[4,5]{1,0:T(4,128)} %reshape.66.order_ref, s32[4,6]{1,0:T(4,128)} %add_convert_fusion.flip_ref, bf16[20,128,128]{2,1,0:T(8,128)(2,1)} %gates_ref.15, bf16[128,64,128]{2,1,0:T(8,128)(2,1)} %bitcast.30), custom_call_target="tpu_custom_call" | custom-call | tf_op jit(solution)/shard_map/pallas_call | solution.py:106
  116.0 17.2 %all-to-all-done.1 = bf16[64,2,64,128]{3,2,1,0:T(8,128)(2,1)} async-done(((bf16[64,2,64,128]{3,2,1,0:T(8,128)(2,1)}), bf16[64,2,64,128]{3,2,1,0:T(8,128)(2,1)}, u32[]{:S(2)}, u32[]{:S(2)}) %all-to-all-start.1) | async-done | bytes 2097184 | tf_op jit(solution)/shard_map/all_to_all | solution.py:119
  133.3 4.9 %all-to-all-start.4 = ((bf16[64,2,64,128]{3,2,1,0:T(8,128)(2,1)}), bf16[64,2,64,128]{3,2,1,0:T(8,128)(2,1)S(1)}, u32[]{:S(2)}, u32[]{:S(2)}) async-start(bf16[64,2,64,128]{3,2,1,0:T(8,128)(2,1)} %bitcast.34), calls=%async_computation.4 | async-start | bytes 4194304 | tf_op jit(solution)/shard_map/all_to_all | solution.py:119
  138.2 14.0 %shard_map.79 = bf16[128,64,128]{2,1,0:T(8,128)(2,1)} custom-call(s32[4,5]{1,0:T(4,128)} %reshape.66.order_ref, s32[4,6]{1,0:T(4,128)} %add_convert_fusion.flip_ref, bf16[20,128,128]{2,1,0:T(8,128)(2,1)} %gates_ref.15, bf16[128,64,128]{2,1,0:T(8,128)(2,1)} %bitcast.5.refs_0_), custom_call_target="tpu_custom_call" | custom-call | tf_op jit(solution)/shard_map/pallas_call | solution.py:106
  152.1 16.5 %all-to-all-done.4 = bf16[64,2,64,128]{3,2,1,0:T(8,128)(2,1)S(1)} async-done(((bf16[64,2,64,128]{3,2,1,0:T(8,128)(2,1)}), bf16[64,2,64,128]{3,2,1,0:T(8,128)(2,1)S(1)}, u32[]{:S(2)}, u32[]{:S(2)}) %all-to-all-start.4) | async-done | bytes 2097184 | tf_op jit(solution)/shard_map/all_to_all | solution.py:119
  170.0 4.9 %all-to-all-start.2 = ((bf16[64,2,64,128]{3,2,1,0:T(8,128)(2,1)}), bf16[64,2,64,128]{3,2,1,0:T(8,128)(2,1)S(1)}, u32[]{:S(2)}, u32[]{:S(2)}) async-start(bf16[64,2,64,128]{3,2,1,0:T(8,128)(2,1)} %bitcast.35), calls=%async_computation.2 | async-start | bytes 4194304 | tf_op jit(solution)/shard_map/all_to_all | solution.py:119
  174.9 14.0 %shard_map.83 = bf16[128,64,128]{2,1,0:T(8,128)(2,1)} custom-call(s32[4,5]{1,0:T(4,128)} %reshape.66.order_ref, s32[4,6]{1,0:T(4,128)} %add_convert_fusion.flip_ref, bf16[20,128,128]{2,1,0:T(8,128)(2,1)} %gates_ref.15, bf16[128,64,128]{2,1,0:T(8,128)(2,1)} %bitcast.31), custom_call_target="tpu_custom_call" | custom-call | tf_op jit(solution)/shard_map/pallas_call | solution.py:106
  188.9 16.5 %all-to-all-done.2 = bf16[64,2,64,128]{3,2,1,0:T(8,128)(2,1)S(1)} async-done(((bf16[64,2,64,128]{3,2,1,0:T(8,128)(2,1)}), bf16[64,2,64,128]{3,2,1,0:T(8,128)(2,1)S(1)}, u32[]{:S(2)}, u32[]{:S(2)}) %all-to-all-start.2) | async-done | bytes 2097184 | tf_op jit(solution)/shard_map/all_to_all | solution.py:119
  206.7 5.3 %all-to-all-start.5 = ((bf16[64,2,64,128]{3,2,1,0:T(8,128)(2,1)}), bf16[64,2,64,128]{3,2,1,0:T(8,128)(2,1)}, u32[]{:S(2)}, u32[]{:S(2)}) async-start(bf16[64,2,64,128]{3,2,1,0:T(8,128)(2,1)} %bitcast.29), calls=%async_computation.5 | async-start | bytes 4194304 | tf_op jit(solution)/shard_map/all_to_all | solution.py:119
  212.0 4.0 %fusion.7 = (bf16[64,128,128]{2,1,0:T(8,128)(2,1)}, bf16[64,128,128]{2,1,0:T(8,128)(2,1)S(1)}) fusion(bf16[128,128,128]{2,1,0:T(8,128)(2,1)} %param.7), kind=kLoop, calls=%fused_computation.18 | loop fusion | bytes 8388608 | tf_op jit(solution)/shard_map/slice | solution.py:162
  216.0 2.6 slice.21
  218.6 3.1 slice.23
  221.7 14.4 %shard_map.80 = bf16[64,128,128]{2,1,0:T(8,128)(2,1)} custom-call(s32[4,5]{1,0:T(4,128)} %reshape.66.order_ref, s32[4,6]{1,0:T(4,128)} %add_convert_fusion.flip_ref, bf16[20,128,128]{2,1,0:T(8,128)(2,1)} %gates_ref.15, bf16[128,64,128]{2,1,0:T(8,128)(2,1)} %bitcast.28), custom_call_target="tpu_custom_call" | custom-call | tf_op jit(solution)/shard_map/pallas_call | solution.py:106
  236.1 4.3 %reshape.80 = bf16[2048,512]{1,0:T(8,128)(2,1)} reshape(bf16[64,128,128]{2,1,0:T(8,128)(2,1)} %shard_map.80) | data formatting | bytes 4194304 | tf_op jit(solution)/shard_map/reshape | solution.py:162
  240.4 2.0 all-to-all-done.5
  242.4 14.4 %shard_map.84 = bf16[64,128,128]{2,1,0:T(8,128)(2,1)} custom-call(s32[4,5]{1,0:T(4,128)} %reshape.66.order_ref, s32[4,6]{1,0:T(4,128)} %add_convert_fusion.flip_ref, bf16[20,128,128]{2,1,0:T(8,128)(2,1)} %gates_ref.15, bf16[128,64,128]{2,1,0:T(8,128)(2,1)} %bitcast.13.refs_0_), custom_call_target="tpu_custom_call" | custom-call | tf_op jit(solution)/shard_map/pallas_call | solution.py:106
  256.8 4.4 %reshape.81 = bf16[2048,512]{1,0:T(8,128)(2,1)} reshape(bf16[64,128,128]{2,1,0:T(8,128)(2,1)} %shard_map.84) | data formatting | bytes 4194304 | tf_op jit(solution)/shard_map/reshape | solution.py:162
  261.2 3.6 %fusion.8 = f32[512,512]{1,0:T(8,128)S(1)} fusion(bf16[2048,512]{1,0:T(8,128)(2,1)} %reshape.80, bf16[2048,512]{1,0:T(8,128)(2,1)} %slice.21), kind=kOutput, calls=%fused_computation.19 | convolution fusion | flops 1073741824 | bytes 5242880 | tf_op jit(solution)/shard_map/dot_general | solution.py:161
  266.7 23.9 %all_to_all.40 = bf16[128,16,128]{2,1,0:T(8,128)(2,1)S(1)} all-to-all(bf16[128,16,128]{2,1,0:T(8,128)(2,1)S(1)} %convert_element_type.25), channel_id=1, replica_groups=mesh['amp'=64,'grp'=2] {'amp','grp'}, dimensions={0} | all-to-all | bytes 1048576 | tf_op jit(solution)/shard_map/all_to_all | solution.py:126
  291.6 4.9 %all-to-all-start.7 = ((bf16[128,16,128]{2,1,0:T(8,128)(2,1)}), bf16[128,16,128]{2,1,0:T(8,128)(2,1)S(1)}, u32[]{:S(2)}, u32[]{:S(2)}) async-start(bf16[128,16,128]{2,1,0:T(8,128)(2,1)} %broadcast_in_dim.15), calls=%async_computation.7 | async-start | bytes 1048576 | tf_op jit(solution)/shard_map/all_to_all | solution.py:129
  296.6 4.0 %pad_maximum_fusion = bf16[128,128,128]{2,1,0:T(8,128)(2,1)} fusion(bf16[64,128,128]{2,1,0:T(8,128)(2,1)} %shard_map.84, bf16[64,128,128]{2,1,0:T(8,128)(2,1)S(1)} %copy-done), kind=kLoop, calls=%fused_computation | loop fusion | flops 2097152 | bytes 8388608 | tf_op jit(solution)/shard_map/concatenate | solution.py:167
  300.6 9.2 %all-to-all-done.7 = bf16[128,16,128]{2,1,0:T(8,128)(2,1)S(1)} async-done(((bf16[128,16,128]{2,1,0:T(8,128)(2,1)}), bf16[128,16,128]{2,1,0:T(8,128)(2,1)S(1)}, u32[]{:S(2)}, u32[]{:S(2)}) %all-to-all-start.7) | async-done | bytes 524320 | tf_op jit(solution)/shard_map/all_to_all | solution.py:129
  311.9 1.5 fusion.3
  (28 shorter events, 12.0 us)
Async XLA Ops:
  16.7 42.9 %all-to-all-start = ((bf16[64,2,64,128]{3,2,1,0:T(8,128)(2,1)}), bf16[64,2,64,128]{3,2,1,0:T(8,128)(2,1)S(1)}, u32[]{:S(2)}, u32[]{:S(2)}) async-start(bf16[64,2,64,128]{3,2,1,0:T(8,128)(2,1)} %bitcast.27), calls=%async_computation | async-start | bytes 4194304 | tf_op jit(solution)/shard_map/all_to_all | solution.py:119
  59.7 1.3 copy-start.4
  61.0 35.4 %all-to-all-start.3 = ((bf16[64,2,64,128]{3,2,1,0:T(8,128)(2,1)}), bf16[64,2,64,128]{3,2,1,0:T(8,128)(2,1)S(1)}, u32[]{:S(2)}, u32[]{:S(2)}) async-start(bf16[64,2,64,128]{3,2,1,0:T(8,128)(2,1)} %bitcast.26), calls=%async_computation.3 | async-start | bytes 4194304 | tf_op jit(solution)/shard_map/all_to_all | solution.py:119
  96.4 1.3 copy-start.2
  97.7 35.5 %all-to-all-start.1 = ((bf16[64,2,64,128]{3,2,1,0:T(8,128)(2,1)}), bf16[64,2,64,128]{3,2,1,0:T(8,128)(2,1)}, u32[]{:S(2)}, u32[]{:S(2)}) async-start(bf16[64,2,64,128]{3,2,1,0:T(8,128)(2,1)} %bitcast.33), calls=%async_computation.1 | async-start | bytes 4194304 | tf_op jit(solution)/shard_map/all_to_all | solution.py:119
  133.3 35.4 %all-to-all-start.4 = ((bf16[64,2,64,128]{3,2,1,0:T(8,128)(2,1)}), bf16[64,2,64,128]{3,2,1,0:T(8,128)(2,1)S(1)}, u32[]{:S(2)}, u32[]{:S(2)}) async-start(bf16[64,2,64,128]{3,2,1,0:T(8,128)(2,1)} %bitcast.34), calls=%async_computation.4 | async-start | bytes 4194304 | tf_op jit(solution)/shard_map/all_to_all | solution.py:119
  168.7 1.3 copy-start.3
  170.0 35.4 %all-to-all-start.2 = ((bf16[64,2,64,128]{3,2,1,0:T(8,128)(2,1)}), bf16[64,2,64,128]{3,2,1,0:T(8,128)(2,1)S(1)}, u32[]{:S(2)}, u32[]{:S(2)}) async-start(bf16[64,2,64,128]{3,2,1,0:T(8,128)(2,1)} %bitcast.35), calls=%async_computation.2 | async-start | bytes 4194304 | tf_op jit(solution)/shard_map/all_to_all | solution.py:119
  205.4 1.3 copy-start.1
  206.7 35.7 %all-to-all-start.5 = ((bf16[64,2,64,128]{3,2,1,0:T(8,128)(2,1)}), bf16[64,2,64,128]{3,2,1,0:T(8,128)(2,1)}, u32[]{:S(2)}, u32[]{:S(2)}) async-start(bf16[64,2,64,128]{3,2,1,0:T(8,128)(2,1)} %bitcast.29), calls=%async_computation.5 | async-start | bytes 4194304 | tf_op jit(solution)/shard_map/all_to_all | solution.py:119
  261.2 3.6 %copy-start.5 = (bf16[2048,512]{1,0:T(8,128)(2,1)S(1)}, bf16[2048,512]{1,0:T(8,128)(2,1)}, u32[]{:S(2)}) copy-start(bf16[2048,512]{1,0:T(8,128)(2,1)} %reshape.81) | copy-start | bytes 6291460
  266.4 30.2 %copy-start = (bf16[64,128,128]{2,1,0:T(8,128)(2,1)S(1)}, bf16[64,128,128]{2,1,0:T(8,128)(2,1)}, u32[]{:S(2)}) copy-start(bf16[64,128,128]{2,1,0:T(8,128)(2,1)} %shard_map.80) | copy-start | bytes 6291460
  291.6 18.1 %all-to-all-start.7 = ((bf16[128,16,128]{2,1,0:T(8,128)(2,1)}), bf16[128,16,128]{2,1,0:T(8,128)(2,1)S(1)}, u32[]{:S(2)}, u32[]{:S(2)}) async-start(bf16[128,16,128]{2,1,0:T(8,128)(2,1)} %broadcast_in_dim.15), calls=%async_computation.7 | async-start | bytes 1048576 | tf_op jit(solution)/shard_map/all_to_all | solution.py:129

commit v8 on v7

--- a/solution.py
+++ b/solution.py
@@ -7,7 +7,7 @@
 
 SEGS = 4
 GATES = 5
-BLOCK = 16
+BLOCK = 32
 CHUNKS = 2
 
 

time: 314 us -> 308 us (0.981)
  Pallas kernels: 108 us -> 89 us
  waiting for transfers between devices: 97 us -> 111 us
    pallas_call x8, Pallas kernels: 108 us -> 89 us  [run_segment(): pl.pallas_call(make_kernel(slab_in, slab_out, len(sources), per_source, s...]
    all_to_all x6, waiting for transfers between devices: 87.8 us -> 102 us  [swap_major(): lax.all_to_all(split, 'amp', split_axis=0, concat_axis=0, tiled=True)]
  transfers between devices with their start and end apart: 7 -> 7, of which waited for: 7 -> 7; matrix products, arithmetic and copies ran while one was open for 6% -> 6% of each run, Pallas kernels for 26% -> 22%
where the time goes in v8:
time: 308 us; the launch traced here: 306 us
  waiting for transfers between devices  111 us (36%)
  Pallas kernels  89 us (29%)
  starting transfers between devices  42.4 us (14%)
  local copies, waits for them, and re-layouts  27.6 us (9%)
  blocking collectives  21.7 us (7%)
  matrix products  7.48 us (2%)
  other arithmetic  5.72 us (2%)
    all_to_all x6, waiting for transfers between devices, swap_major(): lax.all_to_all(split, 'amp', split_axis=0, concat_axis=0, tiled=True)  102 us
    pallas_call x8, Pallas kernels, run_segment(): pl.pallas_call(make_kernel(slab_in, slab_out, len(sources), per_source, s...  89 us
    all_to_all x6, starting transfers between devices, swap_major(): lax.all_to_all(split, 'amp', split_axis=0, concat_axis=0, tiled=True)  37.5 us
    all_to_all x1, blocking collectives, all_sum(): lax.all_to_all(pieces, axes, split_axis=0, concat_axis=0, tiled=True)  21.7 us
    slice x3, local copies, waits for them, and re-layouts, on_device(): adjoint_flat[c * rows:(c + 1) * rows]  9.67 us
    all_to_all x1, waiting for transfers between devices, all_sum(): lax.all_to_all(spread, axes, split_axis=0, concat_axis=0, tiled=True)  9.21 us
    reshape x2, local copies, waits for them, and re-layouts, on_device(): final.reshape(-1, order)  8.69 us
  transfers between devices with their start and end apart: 7, of which 7 were waited for; matrix products, arithmetic and copies ran while one was open for 6% of the time, Pallas kernels for 22%

profile of v8, /device:TPU:1, one launch (start us, length us, event | category | flops | bytes accessed | tf_op | source)
XLA Modules:
  0.0 306.2 jit_solution(5526784385592707839)
XLA Ops:
  4.5 11.0 %shard_map.77 = bf16[128,64,128]{2,1,0:T(8,128)(2,1)} custom-call(s32[4,5]{1,0:T(4,128)} %reshape.66.order_ref, s32[4,6]{1,0:T(4,128)} %add_convert_fusion.flip_ref, bf16[20,128,128]{2,1,0:T(8,128)(2,1)} %gates_ref.15, bf16[128,128,128]{2,1,0:T(8,128)(2,1)} %refs_0_.3), custom_call_target="tpu_custom_call" | custom-call | tf_op jit(solution)/shard_map/pallas_call | solution.py:106
  15.5 12.5 %all-to-all-start = ((bf16[64,2,64,128]{3,2,1,0:T(8,128)(2,1)}), bf16[64,2,64,128]{3,2,1,0:T(8,128)(2,1)S(1)}, u32[]{:S(2)}, u32[]{:S(2)}) async-start(bf16[64,2,64,128]{3,2,1,0:T(8,128)(2,1)} %bitcast.27), calls=%async_computation | async-start | bytes 4194304 | tf_op jit(solution)/shard_map/all_to_all | solution.py:119
  27.9 10.9 %shard_map.81 = bf16[128,64,128]{2,1,0:T(8,128)(2,1)} custom-call(s32[4,5]{1,0:T(4,128)} %reshape.66.order_ref, s32[4,6]{1,0:T(4,128)} %add_convert_fusion.flip_ref, bf16[20,128,128]{2,1,0:T(8,128)(2,1)} %gates_ref.15, bf16[128,128,128]{2,1,0:T(8,128)(2,1)} %refs_0_.3), custom_call_target="tpu_custom_call" | custom-call | tf_op jit(solution)/shard_map/pallas_call | solution.py:106
  38.8 19.6 %all-to-all-done = bf16[64,2,64,128]{3,2,1,0:T(8,128)(2,1)S(1)} async-done(((bf16[64,2,64,128]{3,2,1,0:T(8,128)(2,1)}), bf16[64,2,64,128]{3,2,1,0:T(8,128)(2,1)S(1)}, u32[]{:S(2)}, u32[]{:S(2)}) %all-to-all-start) | async-done | bytes 2097184 | tf_op jit(solution)/shard_map/all_to_all | solution.py:119
  58.4 1.3 copy-done.4
  59.8 4.9 %all-to-all-start.3 = ((bf16[64,2,64,128]{3,2,1,0:T(8,128)(2,1)}), bf16[64,2,64,128]{3,2,1,0:T(8,128)(2,1)S(1)}, u32[]{:S(2)}, u32[]{:S(2)}) async-start(bf16[64,2,64,128]{3,2,1,0:T(8,128)(2,1)} %bitcast.26), calls=%async_computation.3 | async-start | bytes 4194304 | tf_op jit(solution)/shard_map/all_to_all | solution.py:119
  64.7 10.0 %shard_map.78 = bf16[128,64,128]{2,1,0:T(8,128)(2,1)} custom-call(s32[4,5]{1,0:T(4,128)} %reshape.66.order_ref, s32[4,6]{1,0:T(4,128)} %add_convert_fusion.flip_ref, bf16[20,128,128]{2,1,0:T(8,128)(2,1)} %gates_ref.15, bf16[128,64,128]{2,1,0:T(8,128)(2,1)} %bitcast.32), custom_call_target="tpu_custom_call" | custom-call | tf_op jit(solution)/shard_map/pallas_call | solution.py:106
  74.7 20.4 %all-to-all-done.3 = bf16[64,2,64,128]{3,2,1,0:T(8,128)(2,1)S(1)} async-done(((bf16[64,2,64,128]{3,2,1,0:T(8,128)(2,1)}), bf16[64,2,64,128]{3,2,1,0:T(8,128)(2,1)S(1)}, u32[]{:S(2)}, u32[]{:S(2)}) %all-to-all-start.3) | async-done | bytes 2097184 | tf_op jit(solution)/shard_map/all_to_all | solution.py:119
  96.5 5.1 %all-to-all-start.1 = ((bf16[64,2,64,128]{3,2,1,0:T(8,128)(2,1)}), bf16[64,2,64,128]{3,2,1,0:T(8,128)(2,1)}, u32[]{:S(2)}, u32[]{:S(2)}) async-start(bf16[64,2,64,128]{3,2,1,0:T(8,128)(2,1)} %bitcast.33), calls=%async_computation.1 | async-start | bytes 4194304 | tf_op jit(solution)/shard_map/all_to_all | solution.py:119
  101.6 10.0 %shard_map.82 = bf16[128,64,128]{2,1,0:T(8,128)(2,1)} custom-call(s32[4,5]{1,0:T(4,128)} %reshape.66.order_ref, s32[4,6]{1,0:T(4,128)} %add_convert_fusion.flip_ref, bf16[20,128,128]{2,1,0:T(8,128)(2,1)} %gates_ref.15, bf16[128,64,128]{2,1,0:T(8,128)(2,1)} %bitcast.30), custom_call_target="tpu_custom_call" | custom-call | tf_op jit(solution)/shard_map/pallas_call | solution.py:106
  111.6 20.4 %all-to-all-done.1 = bf16[64,2,64,128]{3,2,1,0:T(8,128)(2,1)} async-done(((bf16[64,2,64,128]{3,2,1,0:T(8,128)(2,1)}), bf16[64,2,64,128]{3,2,1,0:T(8,128)(2,1)}, u32[]{:S(2)}, u32[]{:S(2)}) %all-to-all-start.1) | async-done | bytes 2097184 | tf_op jit(solution)/shard_map/all_to_all | solution.py:119
  132.0 4.9 %all-to-all-start.4 = ((bf16[64,2,64,128]{3,2,1,0:T(8,128)(2,1)}), bf16[64,2,64,128]{3,2,1,0:T(8,128)(2,1)S(1)}, u32[]{:S(2)}, u32[]{:S(2)}) async-start(bf16[64,2,64,128]{3,2,1,0:T(8,128)(2,1)} %bitcast.34), calls=%async_computation.4 | async-start | bytes 4194304 | tf_op jit(solution)/shard_map/all_to_all | solution.py:119
  137.0 12.6 %shard_map.79 = bf16[128,64,128]{2,1,0:T(8,128)(2,1)} custom-call(s32[4,5]{1,0:T(4,128)} %reshape.66.order_ref, s32[4,6]{1,0:T(4,128)} %add_convert_fusion.flip_ref, bf16[20,128,128]{2,1,0:T(8,128)(2,1)} %gates_ref.15, bf16[128,64,128]{2,1,0:T(8,128)(2,1)} %bitcast.5.refs_0_), custom_call_target="tpu_custom_call" | custom-call | tf_op jit(solution)/shard_map/pallas_call | solution.py:106
  149.6 17.8 %all-to-all-done.4 = bf16[64,2,64,128]{3,2,1,0:T(8,128)(2,1)S(1)} async-done(((bf16[64,2,64,128]{3,2,1,0:T(8,128)(2,1)}), bf16[64,2,64,128]{3,2,1,0:T(8,128)(2,1)S(1)}, u32[]{:S(2)}, u32[]{:S(2)}) %all-to-all-start.4) | async-done | bytes 2097184 | tf_op jit(solution)/shard_map/all_to_all | solution.py:119
  168.8 4.9 %all-to-all-start.2 = ((bf16[64,2,64,128]{3,2,1,0:T(8,128)(2,1)}), bf16[64,2,64,128]{3,2,1,0:T(8,128)(2,1)S(1)}, u32[]{:S(2)}, u32[]{:S(2)}) async-start(bf16[64,2,64,128]{3,2,1,0:T(8,128)(2,1)} %bitcast.35), calls=%async_computation.2 | async-start | bytes 4194304 | tf_op jit(solution)/shard_map/all_to_all | solution.py:119
  173.7 12.6 %shard_map.83 = bf16[128,64,128]{2,1,0:T(8,128)(2,1)} custom-call(s32[4,5]{1,0:T(4,128)} %reshape.66.order_ref, s32[4,6]{1,0:T(4,128)} %add_convert_fusion.flip_ref, bf16[20,128,128]{2,1,0:T(8,128)(2,1)} %gates_ref.15, bf16[128,64,128]{2,1,0:T(8,128)(2,1)} %bitcast.31), custom_call_target="tpu_custom_call" | custom-call | tf_op jit(solution)/shard_map/pallas_call | solution.py:106
  186.3 17.9 %all-to-all-done.2 = bf16[64,2,64,128]{3,2,1,0:T(8,128)(2,1)S(1)} async-done(((bf16[64,2,64,128]{3,2,1,0:T(8,128)(2,1)}), bf16[64,2,64,128]{3,2,1,0:T(8,128)(2,1)S(1)}, u32[]{:S(2)}, u32[]{:S(2)}) %all-to-all-start.2) | async-done | bytes 2097184 | tf_op jit(solution)/shard_map/all_to_all | solution.py:119
  205.5 5.1 %all-to-all-start.5 = ((bf16[64,2,64,128]{3,2,1,0:T(8,128)(2,1)}), bf16[64,2,64,128]{3,2,1,0:T(8,128)(2,1)}, u32[]{:S(2)}, u32[]{:S(2)}) async-start(bf16[64,2,64,128]{3,2,1,0:T(8,128)(2,1)} %bitcast.29), calls=%async_computation.5 | async-start | bytes 4194304 | tf_op jit(solution)/shard_map/all_to_all | solution.py:119
  210.6 4.0 %fusion.7 = (bf16[64,128,128]{2,1,0:T(8,128)(2,1)}, bf16[64,128,128]{2,1,0:T(8,128)(2,1)S(1)}) fusion(bf16[128,128,128]{2,1,0:T(8,128)(2,1)} %param.7), kind=kLoop, calls=%fused_computation.18 | loop fusion | bytes 8388608 | tf_op jit(solution)/shard_map/slice | solution.py:162
  214.6 2.6 slice.21
  217.2 3.1 %slice.23 = bf16[2048,512]{1,0:T(8,128)(2,1)S(1)} reshape(bf16[64,128,128]{2,1,0:T(8,128)(2,1)} %get-tuple-element.2) | data formatting | bytes 4194304 | tf_op jit(solution)/shard_map/slice | solution.py:162
  220.3 11.0 %shard_map.80 = bf16[64,128,128]{2,1,0:T(8,128)(2,1)} custom-call(s32[4,5]{1,0:T(4,128)} %reshape.66.order_ref, s32[4,6]{1,0:T(4,128)} %add_convert_fusion.flip_ref, bf16[20,128,128]{2,1,0:T(8,128)(2,1)} %gates_ref.15, bf16[128,64,128]{2,1,0:T(8,128)(2,1)} %bitcast.28), custom_call_target="tpu_custom_call" | custom-call | tf_op jit(solution)/shard_map/pallas_call | solution.py:106
  231.3 4.3 %reshape.80 = bf16[2048,512]{1,0:T(8,128)(2,1)} reshape(bf16[64,128,128]{2,1,0:T(8,128)(2,1)} %shard_map.80) | data formatting | bytes 4194304 | tf_op jit(solution)/shard_map/reshape | solution.py:162
  235.6 5.4 %all-to-all-done.5 = bf16[64,2,64,128]{3,2,1,0:T(8,128)(2,1)} async-done(((bf16[64,2,64,128]{3,2,1,0:T(8,128)(2,1)}), bf16[64,2,64,128]{3,2,1,0:T(8,128)(2,1)}, u32[]{:S(2)}, u32[]{:S(2)}) %all-to-all-start.5) | async-done | bytes 2097184 | tf_op jit(solution)/shard_map/all_to_all | solution.py:119
  241.0 11.0 %shard_map.84 = bf16[64,128,128]{2,1,0:T(8,128)(2,1)} custom-call(s32[4,5]{1,0:T(4,128)} %reshape.66.order_ref, s32[4,6]{1,0:T(4,128)} %add_convert_fusion.flip_ref, bf16[20,128,128]{2,1,0:T(8,128)(2,1)} %gates_ref.15, bf16[128,64,128]{2,1,0:T(8,128)(2,1)} %bitcast.13.refs_0_), custom_call_target="tpu_custom_call" | custom-call | tf_op jit(solution)/shard_map/pallas_call | solution.py:106
  252.0 4.4 %reshape.81 = bf16[2048,512]{1,0:T(8,128)(2,1)} reshape(bf16[64,128,128]{2,1,0:T(8,128)(2,1)} %shard_map.84) | data formatting | bytes 4194304 | tf_op jit(solution)/shard_map/reshape | solution.py:162
  256.4 3.6 %fusion.8 = f32[512,512]{1,0:T(8,128)S(1)} fusion(bf16[2048,512]{1,0:T(8,128)(2,1)} %reshape.80, bf16[2048,512]{1,0:T(8,128)(2,1)} %slice.21), kind=kOutput, calls=%fused_computation.19 | convolution fusion | flops 1073741824 | bytes 5242880 | tf_op jit(solution)/shard_map/dot_general | solution.py:161
  261.8 21.7 %all_to_all.40 = bf16[128,16,128]{2,1,0:T(8,128)(2,1)S(1)} all-to-all(bf16[128,16,128]{2,1,0:T(8,128)(2,1)S(1)} %convert_element_type.25), channel_id=1, replica_groups=mesh['amp'=64,'grp'=2] {'amp','grp'}, dimensions={0} | all-to-all | bytes 1048576 | tf_op jit(solution)/shard_map/all_to_all | solution.py:126
  284.6 4.9 %all-to-all-start.7 = ((bf16[128,16,128]{2,1,0:T(8,128)(2,1)}), bf16[128,16,128]{2,1,0:T(8,128)(2,1)S(1)}, u32[]{:S(2)}, u32[]{:S(2)}) async-start(bf16[128,16,128]{2,1,0:T(8,128)(2,1)} %broadcast_in_dim.15), calls=%async_computation.7 | async-start | bytes 1048576 | tf_op jit(solution)/shard_map/all_to_all | solution.py:129
  289.5 4.0 %pad_maximum_fusion = bf16[128,128,128]{2,1,0:T(8,128)(2,1)} fusion(bf16[64,128,128]{2,1,0:T(8,128)(2,1)} %shard_map.84, bf16[64,128,128]{2,1,0:T(8,128)(2,1)S(1)} %copy-done), kind=kLoop, calls=%fused_computation | loop fusion | flops 2097152 | bytes 8388608 | tf_op jit(solution)/shard_map/concatenate | solution.py:167
  293.5 9.2 %all-to-all-done.7 = bf16[128,16,128]{2,1,0:T(8,128)(2,1)S(1)} async-done(((bf16[128,16,128]{2,1,0:T(8,128)(2,1)}), bf16[128,16,128]{2,1,0:T(8,128)(2,1)S(1)}, u32[]{:S(2)}, u32[]{:S(2)}) %all-to-all-start.7) | async-done | bytes 524320 | tf_op jit(solution)/shard_map/all_to_all | solution.py:129
  304.8 1.5 fusion.3
  (28 shorter events, 12.0 us)
Async XLA Ops:
  15.5 43.0 %all-to-all-start = ((bf16[64,2,64,128]{3,2,1,0:T(8,128)(2,1)}), bf16[64,2,64,128]{3,2,1,0:T(8,128)(2,1)S(1)}, u32[]{:S(2)}, u32[]{:S(2)}) async-start(bf16[64,2,64,128]{3,2,1,0:T(8,128)(2,1)} %bitcast.27), calls=%async_computation | async-start | bytes 4194304 | tf_op jit(solution)/shard_map/all_to_all | solution.py:119
  58.4 1.3 copy-start.4
  59.8 35.4 %all-to-all-start.3 = ((bf16[64,2,64,128]{3,2,1,0:T(8,128)(2,1)}), bf16[64,2,64,128]{3,2,1,0:T(8,128)(2,1)S(1)}, u32[]{:S(2)}, u32[]{:S(2)}) async-start(bf16[64,2,64,128]{3,2,1,0:T(8,128)(2,1)} %bitcast.26), calls=%async_computation.3 | async-start | bytes 4194304 | tf_op jit(solution)/shard_map/all_to_all | solution.py:119
  95.2 1.3 copy-start.2
  96.5 35.5 %all-to-all-start.1 = ((bf16[64,2,64,128]{3,2,1,0:T(8,128)(2,1)}), bf16[64,2,64,128]{3,2,1,0:T(8,128)(2,1)}, u32[]{:S(2)}, u32[]{:S(2)}) async-start(bf16[64,2,64,128]{3,2,1,0:T(8,128)(2,1)} %bitcast.33), calls=%async_computation.1 | async-start | bytes 4194304 | tf_op jit(solution)/shard_map/all_to_all | solution.py:119
  132.0 35.4 %all-to-all-start.4 = ((bf16[64,2,64,128]{3,2,1,0:T(8,128)(2,1)}), bf16[64,2,64,128]{3,2,1,0:T(8,128)(2,1)S(1)}, u32[]{:S(2)}, u32[]{:S(2)}) async-start(bf16[64,2,64,128]{3,2,1,0:T(8,128)(2,1)} %bitcast.34), calls=%async_computation.4 | async-start | bytes 4194304 | tf_op jit(solution)/shard_map/all_to_all | solution.py:119
  167.4 1.3 copy-start.3
  168.8 35.4 %all-to-all-start.2 = ((bf16[64,2,64,128]{3,2,1,0:T(8,128)(2,1)}), bf16[64,2,64,128]{3,2,1,0:T(8,128)(2,1)S(1)}, u32[]{:S(2)}, u32[]{:S(2)}) async-start(bf16[64,2,64,128]{3,2,1,0:T(8,128)(2,1)} %bitcast.35), calls=%async_computation.2 | async-start | bytes 4194304 | tf_op jit(solution)/shard_map/all_to_all | solution.py:119
  204.2 1.3 copy-start.1
  205.5 35.5 %all-to-all-start.5 = ((bf16[64,2,64,128]{3,2,1,0:T(8,128)(2,1)}), bf16[64,2,64,128]{3,2,1,0:T(8,128)(2,1)}, u32[]{:S(2)}, u32[]{:S(2)}) async-start(bf16[64,2,64,128]{3,2,1,0:T(8,128)(2,1)} %bitcast.29), calls=%async_computation.5 | async-start | bytes 4194304 | tf_op jit(solution)/shard_map/all_to_all | solution.py:119
  256.3 3.6 %copy-start.5 = (bf16[2048,512]{1,0:T(8,128)(2,1)S(1)}, bf16[2048,512]{1,0:T(8,128)(2,1)}, u32[]{:S(2)}) copy-start(bf16[2048,512]{1,0:T(8,128)(2,1)} %reshape.81) | copy-start | bytes 6291460
  261.5 28.0 %copy-start = (bf16[64,128,128]{2,1,0:T(8,128)(2,1)S(1)}, bf16[64,128,128]{2,1,0:T(8,128)(2,1)}, u32[]{:S(2)}) copy-start(bf16[64,128,128]{2,1,0:T(8,128)(2,1)} %shard_map.80) | copy-start | bytes 6291460
  284.6 18.1 %all-to-all-start.7 = ((bf16[128,16,128]{2,1,0:T(8,128)(2,1)}), bf16[128,16,128]{2,1,0:T(8,128)(2,1)S(1)}, u32[]{:S(2)}, u32[]{:S(2)}) async-start(bf16[128,16,128]{2,1,0:T(8,128)(2,1)} %broadcast_in_dim.15), calls=%async_computation.7 | async-start | bytes 1048576 | tf_op jit(solution)/shard_map/all_to_all | solution.py:129

commit v9 on v8

--- a/solution.py
+++ b/solution.py
@@ -13,7 +13,11 @@
 
 def make_kernel(slab_in, slab_out, sources, blocks_per_source, segment):
     def kernel(order_ref, flip_ref, gates_ref, *refs):
-        x_refs, o_ref, held, diagonal = refs[:sources], refs[-3], refs[-2], refs[-1]
+        held, diagonal = refs[-2], refs[-1]
+        if slab_out:
+            x_refs, o_ref, flat_ref = refs[:sources], refs[-4], refs[-3]
+        else:
+            x_refs, o_ref = refs[:sources], refs[-3]
         half, wide, pair = held.shape
         lanes = pair // 2
 
@@ -63,6 +67,7 @@
         if slab_out:
             o_ref[:half] = first
             o_ref[half:] = second
+            flat_ref[...] = o_ref[...].reshape(flat_ref.shape)
         else:
             o_ref[:, :half, :] = jnp.swapaxes(first, 0, 1)
             o_ref[:, half:, :] = jnp.swapaxes(second, 0, 1)
@@ -85,12 +90,20 @@
         shape = (BLOCK, wide, lanes) if slab_in else (wide, BLOCK, lanes)
         return pl.BlockSpec(shape, pick)
 
+    dtype = sources[0].dtype
     if slab_out:
-        out_spec = pl.BlockSpec((BLOCK, wide, lanes), lambda i, o, f: (i + out_offset, 0, 0))
-        out_shape = (out_slabs or slabs, wide, lanes)
+        rows_per_slab = wide // 4
+        out_spec = [
+            pl.BlockSpec((BLOCK, wide, lanes), lambda i, o, f: (i, 0, 0)),
+            pl.BlockSpec((BLOCK * rows_per_slab, 4 * lanes), lambda i, o, f: (i, 0)),
+        ]
+        out_shape = [
+            jax.ShapeDtypeStruct((slabs, wide, lanes), dtype),
+            jax.ShapeDtypeStruct((slabs * rows_per_slab, 4 * lanes), dtype),
+        ]
     else:
         out_spec = pl.BlockSpec((wide, BLOCK, lanes), lambda i, o, f: (0, i, 0))
-        out_shape = (wide, slabs, lanes)
+        out_shape = jax.ShapeDtypeStruct((wide, slabs, lanes), dtype)
     grid_spec = pltpu.PrefetchScalarGridSpec(
         num_scalar_prefetch=2,
         grid=(blocks,),
@@ -106,7 +119,7 @@
     return pl.pallas_call(
         make_kernel(slab_in, slab_out, len(sources), per_source, segment),
         grid_spec=grid_spec,
-        out_shape=jax.ShapeDtypeStruct(out_shape, sources[0].dtype),
+        out_shape=out_shape,
         compiler_params=pltpu.CompilerParams(dimension_semantics=("arbitrary",)),
         input_output_aliases={} if into is None else {3 + len(sources): 0},
     )(order, flips, gate_mats, *sources, *([] if into is None else [into]))
@@ -159,12 +172,12 @@
     rows = adjoint_flat.shape[0] // CHUNKS
     partial_correlation = sum(
         lax.dot_general(
-            adjoint_flat[c * rows:(c + 1) * rows], final.reshape(-1, order), (((0,), (0,)), ((), ())),
+            adjoint_flat[c * rows:(c + 1) * rows], flat, (((0,), (0,)), ((), ())),
             preferred_element_type=jnp.float32,
         )
-        for c, final in enumerate(finals)
-    )
-    current = jnp.concatenate(finals, axis=0)
+        for c, (_, flat) in enumerate(finals)
+    )
+    current = jnp.concatenate([final for final, _ in finals], axis=0)
     summed = all_sum(partial_correlation, ("amp", "grp"))
     owned = lax.dynamic_slice_in_dim(summed, lax.axis_index("grp") * owned_rows, owned_rows, 0)
     gram = lax.dot_general(

time: 308 us -> 304 us (0.987)
  local copies, waits for them, and re-layouts: 27.6 us -> 18.9 us
  Pallas kernels: 89 us -> 92.5 us
    reshape x2 -> x0, local copies, waits for them, and re-layouts: 8.69 us -> none  [on_device(): final.reshape(-1, order)]
    pallas_call x8, Pallas kernels: 89 us -> 92.5 us  [run_segment(): pl.pallas_call(make_kernel(slab_in, slab_out, len(sources), per_source, s...]
  transfers between devices with their start and end apart: 7 -> 7, of which waited for: 7 -> 7; matrix products, arithmetic and copies ran while one was open for 6% -> 5% of each run, Pallas kernels for 22% -> 23%
where the time goes in v9:
time: 304 us; the launch traced here: 302 us
  waiting for transfers between devices  112 us (37%)
  Pallas kernels  92.5 us (30%)
  starting transfers between devices  42.4 us (14%)
  blocking collectives  21.7 us (7%)
  local copies, waits for them, and re-layouts  18.9 us (6%)
  matrix products  7.47 us (2%)
  other arithmetic  5.72 us (2%)
    all_to_all x6, waiting for transfers between devices, swap_major(): lax.all_to_all(split, 'amp', split_axis=0, concat_axis=0, tiled=True)  103 us
    pallas_call x8, Pallas kernels, run_segment(): pl.pallas_call(make_kernel(slab_in, slab_out, len(sources), per_source, s...  92.5 us
    all_to_all x6, starting transfers between devices, swap_major(): lax.all_to_all(split, 'amp', split_axis=0, concat_axis=0, tiled=True)  37.5 us
    all_to_all x1, blocking collectives, all_sum(): lax.all_to_all(pieces, axes, split_axis=0, concat_axis=0, tiled=True)  21.7 us
    slice x3, local copies, waits for them, and re-layouts, on_device(): adjoint_flat[c * rows:(c + 1) * rows]  9.69 us
    all_to_all x1, waiting for transfers between devices, all_sum(): lax.all_to_all(spread, axes, split_axis=0, concat_axis=0, tiled=True)  9.21 us
  transfers between devices with their start and end apart: 7, of which 7 were waited for; matrix products, arithmetic and copies ran while one was open for 5% of the time, Pallas kernels for 23%

profile of v9, /device:TPU:1, one launch (start us, length us, event | category | flops | bytes accessed | tf_op | source)
XLA Modules:
  0.0 302.3 jit_solution(12611646060296001188)
XLA Ops:
  4.5 11.6 %shard_map.77 = bf16[128,64,128]{2,1,0:T(8,128)(2,1)} custom-call(s32[4,5]{1,0:T(4,128)} %reshape.60.order_ref, s32[4,6]{1,0:T(4,128)} %add_convert_fusion.flip_ref, bf16[20,128,128]{2,1,0:T(8,128)(2,1)} %gates_ref.15, bf16[128,128,128]{2,1,0:T(8,128)(2,1)} %refs_0_.3), custom_call_target="tpu_custom_call" | custom-call | tf_op jit(solution)/shard_map/pallas_call | solution.py:119
  16.1 12.5 %all-to-all-start = ((bf16[64,2,64,128]{3,2,1,0:T(8,128)(2,1)}), bf16[64,2,64,128]{3,2,1,0:T(8,128)(2,1)S(1)}, u32[]{:S(2)}, u32[]{:S(2)}) async-start(bf16[64,2,64,128]{3,2,1,0:T(8,128)(2,1)} %bitcast.27), calls=%async_computation | async-start | bytes 4194304 | tf_op jit(solution)/shard_map/all_to_all | solution.py:132
  28.6 11.5 %shard_map.81 = bf16[128,64,128]{2,1,0:T(8,128)(2,1)} custom-call(s32[4,5]{1,0:T(4,128)} %reshape.60.order_ref, s32[4,6]{1,0:T(4,128)} %add_convert_fusion.flip_ref, bf16[20,128,128]{2,1,0:T(8,128)(2,1)} %gates_ref.15, bf16[128,128,128]{2,1,0:T(8,128)(2,1)} %refs_0_.3), custom_call_target="tpu_custom_call" | custom-call | tf_op jit(solution)/shard_map/pallas_call | solution.py:119
  40.1 19.0 %all-to-all-done = bf16[64,2,64,128]{3,2,1,0:T(8,128)(2,1)S(1)} async-done(((bf16[64,2,64,128]{3,2,1,0:T(8,128)(2,1)}), bf16[64,2,64,128]{3,2,1,0:T(8,128)(2,1)S(1)}, u32[]{:S(2)}, u32[]{:S(2)}) %all-to-all-start) | async-done | bytes 2097184 | tf_op jit(solution)/shard_map/all_to_all | solution.py:132
  59.0 1.3 copy-done.3
  60.4 4.9 %all-to-all-start.3 = ((bf16[64,2,64,128]{3,2,1,0:T(8,128)(2,1)}), bf16[64,2,64,128]{3,2,1,0:T(8,128)(2,1)S(1)}, u32[]{:S(2)}, u32[]{:S(2)}) async-start(bf16[64,2,64,128]{3,2,1,0:T(8,128)(2,1)} %bitcast.26), calls=%async_computation.3 | async-start | bytes 4194304 | tf_op jit(solution)/shard_map/all_to_all | solution.py:132
  65.3 12.6 %shard_map.78 = bf16[128,64,128]{2,1,0:T(8,128)(2,1)} custom-call(s32[4,5]{1,0:T(4,128)} %reshape.60.order_ref, s32[4,6]{1,0:T(4,128)} %add_convert_fusion.flip_ref, bf16[20,128,128]{2,1,0:T(8,128)(2,1)} %gates_ref.15, bf16[128,64,128]{2,1,0:T(8,128)(2,1)} %bitcast.32), custom_call_target="tpu_custom_call" | custom-call | tf_op jit(solution)/shard_map/pallas_call | solution.py:119
  77.9 17.9 %all-to-all-done.3 = bf16[64,2,64,128]{3,2,1,0:T(8,128)(2,1)S(1)} async-done(((bf16[64,2,64,128]{3,2,1,0:T(8,128)(2,1)}), bf16[64,2,64,128]{3,2,1,0:T(8,128)(2,1)S(1)}, u32[]{:S(2)}, u32[]{:S(2)}) %all-to-all-start.3) | async-done | bytes 2097184 | tf_op jit(solution)/shard_map/all_to_all | solution.py:132
  95.8 1.3 copy-done.1
  97.1 5.1 %all-to-all-start.1 = ((bf16[64,2,64,128]{3,2,1,0:T(8,128)(2,1)}), bf16[64,2,64,128]{3,2,1,0:T(8,128)(2,1)}, u32[]{:S(2)}, u32[]{:S(2)}) async-start(bf16[64,2,64,128]{3,2,1,0:T(8,128)(2,1)} %bitcast.33), calls=%async_computation.1 | async-start | bytes 4194304 | tf_op jit(solution)/shard_map/all_to_all | solution.py:132
  102.3 12.5 %shard_map.82 = bf16[128,64,128]{2,1,0:T(8,128)(2,1)} custom-call(s32[4,5]{1,0:T(4,128)} %reshape.60.order_ref, s32[4,6]{1,0:T(4,128)} %add_convert_fusion.flip_ref, bf16[20,128,128]{2,1,0:T(8,128)(2,1)} %gates_ref.15, bf16[128,64,128]{2,1,0:T(8,128)(2,1)} %bitcast.30), custom_call_target="tpu_custom_call" | custom-call | tf_op jit(solution)/shard_map/pallas_call | solution.py:119
  114.8 17.9 %all-to-all-done.1 = bf16[64,2,64,128]{3,2,1,0:T(8,128)(2,1)} async-done(((bf16[64,2,64,128]{3,2,1,0:T(8,128)(2,1)}), bf16[64,2,64,128]{3,2,1,0:T(8,128)(2,1)}, u32[]{:S(2)}, u32[]{:S(2)}) %all-to-all-start.1) | async-done | bytes 2097184 | tf_op jit(solution)/shard_map/all_to_all | solution.py:132
  132.7 4.9 %all-to-all-start.4 = ((bf16[64,2,64,128]{3,2,1,0:T(8,128)(2,1)}), bf16[64,2,64,128]{3,2,1,0:T(8,128)(2,1)S(1)}, u32[]{:S(2)}, u32[]{:S(2)}) async-start(bf16[64,2,64,128]{3,2,1,0:T(8,128)(2,1)} %bitcast.34), calls=%async_computation.4 | async-start | bytes 4194304 | tf_op jit(solution)/shard_map/all_to_all | solution.py:132
  137.6 11.3 %shard_map.79 = bf16[128,64,128]{2,1,0:T(8,128)(2,1)} custom-call(s32[4,5]{1,0:T(4,128)} %reshape.60.order_ref, s32[4,6]{1,0:T(4,128)} %add_convert_fusion.flip_ref, bf16[20,128,128]{2,1,0:T(8,128)(2,1)} %gates_ref.15, bf16[128,64,128]{2,1,0:T(8,128)(2,1)} %bitcast.5.refs_0_), custom_call_target="tpu_custom_call" | custom-call | tf_op jit(solution)/shard_map/pallas_call | solution.py:119
  148.9 19.1 %all-to-all-done.4 = bf16[64,2,64,128]{3,2,1,0:T(8,128)(2,1)S(1)} async-done(((bf16[64,2,64,128]{3,2,1,0:T(8,128)(2,1)}), bf16[64,2,64,128]{3,2,1,0:T(8,128)(2,1)S(1)}, u32[]{:S(2)}, u32[]{:S(2)}) %all-to-all-start.4) | async-done | bytes 2097184 | tf_op jit(solution)/shard_map/all_to_all | solution.py:132
  168.1 1.3 copy-done.2
  169.4 4.9 %all-to-all-start.2 = ((bf16[64,2,64,128]{3,2,1,0:T(8,128)(2,1)}), bf16[64,2,64,128]{3,2,1,0:T(8,128)(2,1)S(1)}, u32[]{:S(2)}, u32[]{:S(2)}) async-start(bf16[64,2,64,128]{3,2,1,0:T(8,128)(2,1)} %bitcast.35), calls=%async_computation.2 | async-start | bytes 4194304 | tf_op jit(solution)/shard_map/all_to_all | solution.py:132
  174.3 11.2 %shard_map.83 = bf16[128,64,128]{2,1,0:T(8,128)(2,1)} custom-call(s32[4,5]{1,0:T(4,128)} %reshape.60.order_ref, s32[4,6]{1,0:T(4,128)} %add_convert_fusion.flip_ref, bf16[20,128,128]{2,1,0:T(8,128)(2,1)} %gates_ref.15, bf16[128,64,128]{2,1,0:T(8,128)(2,1)} %bitcast.31), custom_call_target="tpu_custom_call" | custom-call | tf_op jit(solution)/shard_map/pallas_call | solution.py:119
  185.5 19.2 %all-to-all-done.2 = bf16[64,2,64,128]{3,2,1,0:T(8,128)(2,1)S(1)} async-done(((bf16[64,2,64,128]{3,2,1,0:T(8,128)(2,1)}), bf16[64,2,64,128]{3,2,1,0:T(8,128)(2,1)S(1)}, u32[]{:S(2)}, u32[]{:S(2)}) %all-to-all-start.2) | async-done | bytes 2097184 | tf_op jit(solution)/shard_map/all_to_all | solution.py:132
  206.1 5.1 %all-to-all-start.5 = ((bf16[64,2,64,128]{3,2,1,0:T(8,128)(2,1)}), bf16[64,2,64,128]{3,2,1,0:T(8,128)(2,1)}, u32[]{:S(2)}, u32[]{:S(2)}) async-start(bf16[64,2,64,128]{3,2,1,0:T(8,128)(2,1)} %bitcast.29), calls=%async_computation.5 | async-start | bytes 4194304 | tf_op jit(solution)/shard_map/all_to_all | solution.py:132
  211.2 4.0 %fusion.7 = (bf16[64,128,128]{2,1,0:T(8,128)(2,1)}, bf16[64,128,128]{2,1,0:T(8,128)(2,1)S(1)}) fusion(bf16[128,128,128]{2,1,0:T(8,128)(2,1)} %param.7), kind=kLoop, calls=%fused_computation.18 | loop fusion | bytes 8388608 | tf_op jit(solution)/shard_map/slice | solution.py:175
  215.3 2.6 slice.21
  217.8 3.1 %slice.23 = bf16[2048,512]{1,0:T(8,128)(2,1)S(1)} reshape(bf16[64,128,128]{2,1,0:T(8,128)(2,1)} %get-tuple-element.10) | data formatting | bytes 4194304 | tf_op jit(solution)/shard_map/slice | solution.py:175
  220.9 10.8 %shard_map.80 = (bf16[64,128,128]{2,1,0:T(8,128)(2,1)}, bf16[2048,512]{1,0:T(8,128)(2,1)}) custom-call(s32[4,5]{1,0:T(4,128)} %reshape.60.order_ref, s32[4,6]{1,0:T(4,128)} %add_convert_fusion.flip_ref, bf16[20,128,128]{2,1,0:T(8,128)(2,1)} %gates_ref.15, bf16[128,64,128]{2,1,0:T(8,128)(2,1)} %bitcast.28), custom_call_target="tpu_custom_call" | custom-call | tf_op jit(solution)/shard_map/pallas_call | solution.py:119
  231.8 9.9 %all-to-all-done.5 = bf16[64,2,64,128]{3,2,1,0:T(8,128)(2,1)} async-done(((bf16[64,2,64,128]{3,2,1,0:T(8,128)(2,1)}), bf16[64,2,64,128]{3,2,1,0:T(8,128)(2,1)}, u32[]{:S(2)}, u32[]{:S(2)}) %all-to-all-start.5) | async-done | bytes 2097184 | tf_op jit(solution)/shard_map/all_to_all | solution.py:132
  241.6 10.8 %shard_map.84 = (bf16[64,128,128]{2,1,0:T(8,128)(2,1)}, bf16[2048,512]{1,0:T(8,128)(2,1)}) custom-call(s32[4,5]{1,0:T(4,128)} %reshape.60.order_ref, s32[4,6]{1,0:T(4,128)} %add_convert_fusion.flip_ref, bf16[20,128,128]{2,1,0:T(8,128)(2,1)} %gates_ref.15, bf16[128,64,128]{2,1,0:T(8,128)(2,1)} %bitcast.13.refs_0_), custom_call_target="tpu_custom_call" | custom-call | tf_op jit(solution)/shard_map/pallas_call | solution.py:119
  252.4 3.6 %fusion.8 = f32[512,512]{1,0:T(8,128)S(1)} fusion(bf16[2048,512]{1,0:T(8,128)(2,1)} %get-tuple-element.8, bf16[2048,512]{1,0:T(8,128)(2,1)} %slice.21), kind=kOutput, calls=%fused_computation.19 | convolution fusion | flops 1073741824 | bytes 5242880 | tf_op jit(solution)/shard_map/dot_general | solution.py:174
  257.9 21.7 %all_to_all.40 = bf16[128,16,128]{2,1,0:T(8,128)(2,1)S(1)} all-to-all(bf16[128,16,128]{2,1,0:T(8,128)(2,1)S(1)} %convert_element_type.25), channel_id=1, replica_groups=mesh['amp'=64,'grp'=2] {'amp','grp'}, dimensions={0} | all-to-all | bytes 1048576 | tf_op jit(solution)/shard_map/all_to_all | solution.py:139
  280.6 4.9 %all-to-all-start.7 = ((bf16[128,16,128]{2,1,0:T(8,128)(2,1)}), bf16[128,16,128]{2,1,0:T(8,128)(2,1)S(1)}, u32[]{:S(2)}, u32[]{:S(2)}) async-start(bf16[128,16,128]{2,1,0:T(8,128)(2,1)} %broadcast_in_dim.15), calls=%async_computation.7 | async-start | bytes 1048576 | tf_op jit(solution)/shard_map/all_to_all | solution.py:142
  285.6 4.0 %pad_maximum_fusion = bf16[128,128,128]{2,1,0:T(8,128)(2,1)} fusion(bf16[64,128,128]{2,1,0:T(8,128)(2,1)} %get-tuple-element.7, bf16[64,128,128]{2,1,0:T(8,128)(2,1)S(1)} %copy-done.4), kind=kLoop, calls=%fused_computation | loop fusion | flops 2097152 | bytes 8388608 | tf_op jit(solution)/shard_map/concatenate | solution.py:180
  289.5 9.2 %all-to-all-done.7 = bf16[128,16,128]{2,1,0:T(8,128)(2,1)S(1)} async-done(((bf16[128,16,128]{2,1,0:T(8,128)(2,1)}), bf16[128,16,128]{2,1,0:T(8,128)(2,1)S(1)}, u32[]{:S(2)}, u32[]{:S(2)}) %all-to-all-start.7) | async-done | bytes 524320 | tf_op jit(solution)/shard_map/all_to_all | solution.py:142
  300.8 1.5 fusion.3
  (26 shorter events, 9.4 us)
Async XLA Ops:
  16.1 42.9 %all-to-all-start = ((bf16[64,2,64,128]{3,2,1,0:T(8,128)(2,1)}), bf16[64,2,64,128]{3,2,1,0:T(8,128)(2,1)S(1)}, u32[]{:S(2)}, u32[]{:S(2)}) async-start(bf16[64,2,64,128]{3,2,1,0:T(8,128)(2,1)} %bitcast.27), calls=%async_computation | async-start | bytes 4194304 | tf_op jit(solution)/shard_map/all_to_all | solution.py:132
  59.0 1.3 copy-start.3
  60.4 35.4 %all-to-all-start.3 = ((bf16[64,2,64,128]{3,2,1,0:T(8,128)(2,1)}), bf16[64,2,64,128]{3,2,1,0:T(8,128)(2,1)S(1)}, u32[]{:S(2)}, u32[]{:S(2)}) async-start(bf16[64,2,64,128]{3,2,1,0:T(8,128)(2,1)} %bitcast.26), calls=%async_computation.3 | async-start | bytes 4194304 | tf_op jit(solution)/shard_map/all_to_all | solution.py:132
  95.8 1.3 copy-start.1
  97.1 35.5 %all-to-all-start.1 = ((bf16[64,2,64,128]{3,2,1,0:T(8,128)(2,1)}), bf16[64,2,64,128]{3,2,1,0:T(8,128)(2,1)}, u32[]{:S(2)}, u32[]{:S(2)}) async-start(bf16[64,2,64,128]{3,2,1,0:T(8,128)(2,1)} %bitcast.33), calls=%async_computation.1 | async-start | bytes 4194304 | tf_op jit(solution)/shard_map/all_to_all | solution.py:132
  132.7 35.4 %all-to-all-start.4 = ((bf16[64,2,64,128]{3,2,1,0:T(8,128)(2,1)}), bf16[64,2,64,128]{3,2,1,0:T(8,128)(2,1)S(1)}, u32[]{:S(2)}, u32[]{:S(2)}) async-start(bf16[64,2,64,128]{3,2,1,0:T(8,128)(2,1)} %bitcast.34), calls=%async_computation.4 | async-start | bytes 4194304 | tf_op jit(solution)/shard_map/all_to_all | solution.py:132
  168.1 1.3 copy-start.2
  169.4 35.4 %all-to-all-start.2 = ((bf16[64,2,64,128]{3,2,1,0:T(8,128)(2,1)}), bf16[64,2,64,128]{3,2,1,0:T(8,128)(2,1)S(1)}, u32[]{:S(2)}, u32[]{:S(2)}) async-start(bf16[64,2,64,128]{3,2,1,0:T(8,128)(2,1)} %bitcast.35), calls=%async_computation.2 | async-start | bytes 4194304 | tf_op jit(solution)/shard_map/all_to_all | solution.py:132
  204.8 1.3 copy-start
  206.1 35.5 %all-to-all-start.5 = ((bf16[64,2,64,128]{3,2,1,0:T(8,128)(2,1)}), bf16[64,2,64,128]{3,2,1,0:T(8,128)(2,1)}, u32[]{:S(2)}, u32[]{:S(2)}) async-start(bf16[64,2,64,128]{3,2,1,0:T(8,128)(2,1)} %bitcast.29), calls=%async_computation.5 | async-start | bytes 4194304 | tf_op jit(solution)/shard_map/all_to_all | solution.py:132
  252.4 3.6 %copy-start.5 = (bf16[2048,512]{1,0:T(8,128)(2,1)S(1)}, bf16[2048,512]{1,0:T(8,128)(2,1)}, u32[]{:S(2)}) copy-start(bf16[2048,512]{1,0:T(8,128)(2,1)} %get-tuple-element.9) | copy-start | bytes 6291460
  257.6 28.0 %copy-start.4 = (bf16[64,128,128]{2,1,0:T(8,128)(2,1)S(1)}, bf16[64,128,128]{2,1,0:T(8,128)(2,1)}, u32[]{:S(2)}) copy-start(bf16[64,128,128]{2,1,0:T(8,128)(2,1)} %get-tuple-element.6) | copy-start | bytes 6291460
  280.6 18.1 %all-to-all-start.7 = ((bf16[128,16,128]{2,1,0:T(8,128)(2,1)}), bf16[128,16,128]{2,1,0:T(8,128)(2,1)S(1)}, u32[]{:S(2)}, u32[]{:S(2)}) async-start(bf16[128,16,128]{2,1,0:T(8,128)(2,1)} %broadcast_in_dim.15), calls=%async_computation.7 | async-start | bytes 1048576 | tf_op jit(solution)/shard_map/all_to_all | solution.py:142

commit v10 on v9

--- a/solution.py
+++ b/solution.py
@@ -15,7 +15,7 @@
     def kernel(order_ref, flip_ref, gates_ref, *refs):
         held, diagonal = refs[-2], refs[-1]
         if slab_out:
-            x_refs, o_ref, flat_ref = refs[:sources], refs[-4], refs[-3]
+            x_refs, adjoint_ref, o_ref, corr_ref = refs[:sources], refs[-5], refs[-4], refs[-3]
         else:
             x_refs, o_ref = refs[:sources], refs[-3]
         half, wide, pair = held.shape
@@ -67,7 +67,16 @@
         if slab_out:
             o_ref[:half] = first
             o_ref[half:] = second
-            flat_ref[...] = o_ref[...].reshape(flat_ref.shape)
+            flat = o_ref[...].reshape(adjoint_ref.shape)
+            part = jnp.dot(adjoint_ref[...].T, flat, preferred_element_type=jnp.float32)
+
+            @pl.when(pl.program_id(0) == 0)
+            def _():
+                corr_ref[...] = part
+
+            @pl.when(pl.program_id(0) > 0)
+            def _():
+                corr_ref[...] += part
         else:
             o_ref[:, :half, :] = jnp.swapaxes(first, 0, 1)
             o_ref[:, half:, :] = jnp.swapaxes(second, 0, 1)
@@ -76,7 +85,7 @@
 
 
 def run_segment(sources, gate_mats, order, flips, segment, slab_in, slab_out, slabs, offset=0,
-                into=None, out_offset=0, out_slabs=None):
+                adjoint=None, adjoint_offset=0):
     wide = gate_mats.shape[1]
     lanes = sources[0].shape[2]
     blocks = slabs // BLOCK
@@ -95,13 +104,16 @@
         rows_per_slab = wide // 4
         out_spec = [
             pl.BlockSpec((BLOCK, wide, lanes), lambda i, o, f: (i, 0, 0)),
-            pl.BlockSpec((BLOCK * rows_per_slab, 4 * lanes), lambda i, o, f: (i, 0)),
+            pl.BlockSpec((4 * lanes, 4 * lanes), lambda i, o, f: (0, 0)),
         ]
         out_shape = [
             jax.ShapeDtypeStruct((slabs, wide, lanes), dtype),
-            jax.ShapeDtypeStruct((slabs * rows_per_slab, 4 * lanes), dtype),
+            jax.ShapeDtypeStruct((4 * lanes, 4 * lanes), jnp.float32),
         ]
+        adjoint_spec = [pl.BlockSpec((BLOCK * rows_per_slab, 4 * lanes), lambda i, o, f: (i + adjoint_offset, 0))]
     else:
+        adjoint_spec = []
+    if not slab_out:
         out_spec = pl.BlockSpec((wide, BLOCK, lanes), lambda i, o, f: (0, i, 0))
         out_shape = jax.ShapeDtypeStruct((wide, slabs, lanes), dtype)
     grid_spec = pltpu.PrefetchScalarGridSpec(
@@ -109,7 +121,7 @@
         grid=(blocks,),
         in_specs=[pl.BlockSpec(gate_mats.shape, lambda i, o, f: (0, 0, 0))]
         + [source_spec(index) for index in range(len(sources))]
-        + ([] if into is None else [pl.BlockSpec(memory_space=pl.ANY)]),
+        + adjoint_spec,
         out_specs=out_spec,
         scratch_shapes=[
             pltpu.VMEM((BLOCK // 2, wide, 2 * lanes), jnp.bfloat16),
@@ -121,8 +133,7 @@
         grid_spec=grid_spec,
         out_shape=out_shape,
         compiler_params=pltpu.CompilerParams(dimension_semantics=("arbitrary",)),
-        input_output_aliases={} if into is None else {3 + len(sources): 0},
-    )(order, flips, gate_mats, *sources, *([] if into is None else [into]))
+    )(order, flips, gate_mats, *sources, *([] if adjoint is None else [adjoint]))
 
 
 def swap_major(values):
@@ -163,20 +174,17 @@
         elif segment < SEGS - 1:
             chunks = [run_segment([part], gate_mats, order, flips, segment, False, False, chunk) for part in chunks]
         else:
-            finals = [run_segment([part], gate_mats, order, flips, segment, False, True, chunk) for part in chunks]
+            adjoint_flat = adjoint.reshape(-1, 4 * adjoint.shape[2])
+            finals = [
+                run_segment([part], gate_mats, order, flips, segment, False, True, chunk,
+                            adjoint=adjoint_flat, adjoint_offset=c * (chunk // BLOCK))
+                for c, part in enumerate(chunks)
+            ]
         if segment < SEGS - 1:
             chunks = [swap_major(part) for part in chunks]
     order = 4 * amplitudes.shape[2]
     owned_rows = order // lax.axis_size("grp")
-    adjoint_flat = adjoint.reshape(-1, order)
-    rows = adjoint_flat.shape[0] // CHUNKS
-    partial_correlation = sum(
-        lax.dot_general(
-            adjoint_flat[c * rows:(c + 1) * rows], flat, (((0,), (0,)), ((), ())),
-            preferred_element_type=jnp.float32,
-        )
-        for c, (_, flat) in enumerate(finals)
-    )
+    partial_correlation = sum(corr for _, corr in finals)
     current = jnp.concatenate([final for final, _ in finals], axis=0)
     summed = all_sum(partial_correlation, ("amp", "grp"))
     owned = lax.dynamic_slice_in_dim(summed, lax.axis_index("grp") * owned_rows, owned_rows, 0)

time: 304 us -> 301 us (level)
  matrix products: 7.47 us -> 2.55 us
  waiting for transfers between devices: 112 us -> 116 us
    slice x3 -> x0, local copies, waits for them, and re-layouts: 9.69 us -> none  [on_device(): adjoint_flat[c * rows:(c + 1) * rows]]
    reshape x0 -> x1, local copies, waits for them, and re-layouts: none -> 7.52 us  [on_device(): adjoint_flat = adjoint.reshape(-1, 4 * adjoint.shape[2])]
    dot_general x2 -> x0, matrix products: 4.92 us -> none  [on_device(): lax.dot_general(adjoint_flat[c * rows:(c + 1) * rows], flat, (((0,), (0,)...]
    all_to_all x6, waiting for transfers between devices: 103 us -> 107 us  [swap_major(): lax.all_to_all(split, 'amp', split_axis=0, concat_axis=0, tiled=True)]
  transfers between devices with their start and end apart: 7 -> 7, of which waited for: 7 -> 7; matrix products, arithmetic and copies ran while one was open for 5% -> 4% of each run, Pallas kernels for 23% -> 23%
where the time goes in v10:
time: 301 us; the launch traced here: 299 us
  waiting for transfers between devices  116 us (39%)
  Pallas kernels  90.8 us (30%)
  starting transfers between devices  42.4 us (14%)
  blocking collectives  21.7 us (7%)
  local copies, waits for them, and re-layouts  16.6 us (6%)
  other arithmetic  7.09 us (2%)
    all_to_all x6, waiting for transfers between devices, swap_major(): lax.all_to_all(split, 'amp', split_axis=0, concat_axis=0, tiled=True)  107 us
    pallas_call x8, Pallas kernels, run_segment(): pl.pallas_call(make_kernel(slab_in, slab_out, len(sources), per_source, s...  90.8 us
    all_to_all x6, starting transfers between devices, swap_major(): lax.all_to_all(split, 'amp', split_axis=0, concat_axis=0, tiled=True)  37.5 us
    all_to_all x1, blocking collectives, all_sum(): lax.all_to_all(pieces, axes, split_axis=0, concat_axis=0, tiled=True)  21.7 us
    all_to_all x1, waiting for transfers between devices, all_sum(): lax.all_to_all(spread, axes, split_axis=0, concat_axis=0, tiled=True)  9.21 us
    reshape x1, local copies, waits for them, and re-layouts, on_device(): adjoint_flat = adjoint.reshape(-1, 4 * adjoint.shape[2])  7.52 us
  transfers between devices with their start and end apart: 7, of which 7 were waited for; matrix products, arithmetic and copies ran while one was open for 4% of the time, Pallas kernels for 23%

profile of v10, /device:TPU:1, one launch (start us, length us, event | category | flops | bytes accessed | tf_op | source)
XLA Modules:
  0.0 299.1 jit_solution(8347572431758653502)
XLA Ops:
  2.4 1.3 reshape.60.order_ref
  4.5 11.0 %shard_map.77 = bf16[128,64,128]{2,1,0:T(8,128)(2,1)} custom-call(s32[4,5]{1,0:T(4,128)} %reshape.60.order_ref, s32[4,6]{1,0:T(4,128)} %add_convert_fusion.1.flip_ref, bf16[20,128,128]{2,1,0:T(8,128)(2,1)} %gates_ref.15, bf16[128,128,128]{2,1,0:T(8,128)(2,1)} %refs_0_.3), custom_call_target="tpu_custom_call" | custom-call | tf_op jit(solution)/shard_map/pallas_call | solution.py:131
  15.5 12.5 %all-to-all-start = ((bf16[64,2,64,128]{3,2,1,0:T(8,128)(2,1)}), bf16[64,2,64,128]{3,2,1,0:T(8,128)(2,1)S(1)}, u32[]{:S(2)}, u32[]{:S(2)}) async-start(bf16[64,2,64,128]{3,2,1,0:T(8,128)(2,1)} %bitcast.22), calls=%async_computation | async-start | bytes 4194304 | tf_op jit(solution)/shard_map/all_to_all | solution.py:143
  27.9 10.9 %shard_map.81 = bf16[128,64,128]{2,1,0:T(8,128)(2,1)} custom-call(s32[4,5]{1,0:T(4,128)} %reshape.60.order_ref, s32[4,6]{1,0:T(4,128)} %add_convert_fusion.1.flip_ref, bf16[20,128,128]{2,1,0:T(8,128)(2,1)} %gates_ref.15, bf16[128,128,128]{2,1,0:T(8,128)(2,1)} %refs_0_.3), custom_call_target="tpu_custom_call" | custom-call | tf_op jit(solution)/shard_map/pallas_call | solution.py:131
  38.8 19.6 %all-to-all-done = bf16[64,2,64,128]{3,2,1,0:T(8,128)(2,1)S(1)} async-done(((bf16[64,2,64,128]{3,2,1,0:T(8,128)(2,1)}), bf16[64,2,64,128]{3,2,1,0:T(8,128)(2,1)S(1)}, u32[]{:S(2)}, u32[]{:S(2)}) %all-to-all-start) | async-done | bytes 2097184 | tf_op jit(solution)/shard_map/all_to_all | solution.py:143
  58.4 1.3 copy-done.3
  59.8 4.9 %all-to-all-start.3 = ((bf16[64,2,64,128]{3,2,1,0:T(8,128)(2,1)}), bf16[64,2,64,128]{3,2,1,0:T(8,128)(2,1)S(1)}, u32[]{:S(2)}, u32[]{:S(2)}) async-start(bf16[64,2,64,128]{3,2,1,0:T(8,128)(2,1)} %bitcast.21), calls=%async_computation.3 | async-start | bytes 4194304 | tf_op jit(solution)/shard_map/all_to_all | solution.py:143
  64.7 12.0 %shard_map.78 = bf16[128,64,128]{2,1,0:T(8,128)(2,1)} custom-call(s32[4,5]{1,0:T(4,128)} %reshape.60.order_ref, s32[4,6]{1,0:T(4,128)} %add_convert_fusion.1.flip_ref, bf16[20,128,128]{2,1,0:T(8,128)(2,1)} %gates_ref.15, bf16[128,64,128]{2,1,0:T(8,128)(2,1)} %bitcast.25), custom_call_target="tpu_custom_call" | custom-call | tf_op jit(solution)/shard_map/pallas_call | solution.py:131
  76.7 18.5 %all-to-all-done.3 = bf16[64,2,64,128]{3,2,1,0:T(8,128)(2,1)S(1)} async-done(((bf16[64,2,64,128]{3,2,1,0:T(8,128)(2,1)}), bf16[64,2,64,128]{3,2,1,0:T(8,128)(2,1)S(1)}, u32[]{:S(2)}, u32[]{:S(2)}) %all-to-all-start.3) | async-done | bytes 2097184 | tf_op jit(solution)/shard_map/all_to_all | solution.py:143
  95.2 1.3 copy-done.1
  96.5 5.1 %all-to-all-start.1 = ((bf16[64,2,64,128]{3,2,1,0:T(8,128)(2,1)}), bf16[64,2,64,128]{3,2,1,0:T(8,128)(2,1)}, u32[]{:S(2)}, u32[]{:S(2)}) async-start(bf16[64,2,64,128]{3,2,1,0:T(8,128)(2,1)} %bitcast.27), calls=%async_computation.1 | async-start | bytes 4194304 | tf_op jit(solution)/shard_map/all_to_all | solution.py:143
  101.6 11.9 %shard_map.82 = bf16[128,64,128]{2,1,0:T(8,128)(2,1)} custom-call(s32[4,5]{1,0:T(4,128)} %reshape.60.order_ref, s32[4,6]{1,0:T(4,128)} %add_convert_fusion.1.flip_ref, bf16[20,128,128]{2,1,0:T(8,128)(2,1)} %gates_ref.15, bf16[128,64,128]{2,1,0:T(8,128)(2,1)} %bitcast.23), custom_call_target="tpu_custom_call" | custom-call | tf_op jit(solution)/shard_map/pallas_call | solution.py:131
  113.5 18.5 %all-to-all-done.1 = bf16[64,2,64,128]{3,2,1,0:T(8,128)(2,1)} async-done(((bf16[64,2,64,128]{3,2,1,0:T(8,128)(2,1)}), bf16[64,2,64,128]{3,2,1,0:T(8,128)(2,1)}, u32[]{:S(2)}, u32[]{:S(2)}) %all-to-all-start.1) | async-done | bytes 2097184 | tf_op jit(solution)/shard_map/all_to_all | solution.py:143
  132.0 4.9 %all-to-all-start.4 = ((bf16[64,2,64,128]{3,2,1,0:T(8,128)(2,1)}), bf16[64,2,64,128]{3,2,1,0:T(8,128)(2,1)S(1)}, u32[]{:S(2)}, u32[]{:S(2)}) async-start(bf16[64,2,64,128]{3,2,1,0:T(8,128)(2,1)} %bitcast.28), calls=%async_computation.4 | async-start | bytes 4194304 | tf_op jit(solution)/shard_map/all_to_all | solution.py:143
  137.0 10.6 %shard_map.79 = bf16[128,64,128]{2,1,0:T(8,128)(2,1)} custom-call(s32[4,5]{1,0:T(4,128)} %reshape.60.order_ref, s32[4,6]{1,0:T(4,128)} %add_convert_fusion.1.flip_ref, bf16[20,128,128]{2,1,0:T(8,128)(2,1)} %gates_ref.15, bf16[128,64,128]{2,1,0:T(8,128)(2,1)} %bitcast.5.refs_0_), custom_call_target="tpu_custom_call" | custom-call | tf_op jit(solution)/shard_map/pallas_call | solution.py:131
  147.6 19.8 %all-to-all-done.4 = bf16[64,2,64,128]{3,2,1,0:T(8,128)(2,1)S(1)} async-done(((bf16[64,2,64,128]{3,2,1,0:T(8,128)(2,1)}), bf16[64,2,64,128]{3,2,1,0:T(8,128)(2,1)S(1)}, u32[]{:S(2)}, u32[]{:S(2)}) %all-to-all-start.4) | async-done | bytes 2097184 | tf_op jit(solution)/shard_map/all_to_all | solution.py:143
  167.4 1.3 copy-done.2
  168.8 4.9 %all-to-all-start.2 = ((bf16[64,2,64,128]{3,2,1,0:T(8,128)(2,1)}), bf16[64,2,64,128]{3,2,1,0:T(8,128)(2,1)S(1)}, u32[]{:S(2)}, u32[]{:S(2)}) async-start(bf16[64,2,64,128]{3,2,1,0:T(8,128)(2,1)} %bitcast.29), calls=%async_computation.2 | async-start | bytes 4194304 | tf_op jit(solution)/shard_map/all_to_all | solution.py:143
  173.7 10.7 %shard_map.83 = bf16[128,64,128]{2,1,0:T(8,128)(2,1)} custom-call(s32[4,5]{1,0:T(4,128)} %reshape.60.order_ref, s32[4,6]{1,0:T(4,128)} %add_convert_fusion.1.flip_ref, bf16[20,128,128]{2,1,0:T(8,128)(2,1)} %gates_ref.15, bf16[128,64,128]{2,1,0:T(8,128)(2,1)} %bitcast.24), custom_call_target="tpu_custom_call" | custom-call | tf_op jit(solution)/shard_map/pallas_call | solution.py:131
  184.4 19.8 %all-to-all-done.2 = bf16[64,2,64,128]{3,2,1,0:T(8,128)(2,1)S(1)} async-done(((bf16[64,2,64,128]{3,2,1,0:T(8,128)(2,1)}), bf16[64,2,64,128]{3,2,1,0:T(8,128)(2,1)S(1)}, u32[]{:S(2)}, u32[]{:S(2)}) %all-to-all-start.2) | async-done | bytes 2097184 | tf_op jit(solution)/shard_map/all_to_all | solution.py:143
  204.2 1.4 copy-done
  205.5 5.1 %all-to-all-start.5 = ((bf16[64,2,64,128]{3,2,1,0:T(8,128)(2,1)}), bf16[64,2,64,128]{3,2,1,0:T(8,128)(2,1)}, u32[]{:S(2)}, u32[]{:S(2)}) async-start(bf16[64,2,64,128]{3,2,1,0:T(8,128)(2,1)} %bitcast.26), calls=%async_computation.5 | async-start | bytes 4194304 | tf_op jit(solution)/shard_map/all_to_all | solution.py:143
  210.7 7.5 %reshape.68.refs_1_ = bf16[4096,512]{1,0:T(8,128)(2,1)} reshape(bf16[128,128,128]{2,1,0:T(8,128)(2,1)} %param.7) | data formatting | bytes 8388608 | tf_op jit(solution)/shard_map/reshape | solution.py:177
  218.2 11.8 %shard_map.80 = (bf16[64,128,128]{2,1,0:T(8,128)(2,1)}, f32[512,512]{1,0:T(8,128)}) custom-call(s32[4,5]{1,0:T(4,128)} %reshape.60.order_ref, s32[4,6]{1,0:T(4,128)} %add_convert_fusion.1.flip_ref, bf16[20,128,128]{2,1,0:T(8,128)(2,1)} %gates_ref.15, bf16[128,64,128]{2,1,0:T(8,128)(2,1)} %bitcast.20, bf16[4096,512]{1,0:T(8,128)(2,1)} %reshape.68.refs_1_), custom_call_target="tpu_custom_call" | custom-call | tf_op jit(solution)/shard_map/pallas_call | solution.py:131
  230.0 11.1 %all-to-all-done.5 = bf16[64,2,64,128]{3,2,1,0:T(8,128)(2,1)} async-done(((bf16[64,2,64,128]{3,2,1,0:T(8,128)(2,1)}), bf16[64,2,64,128]{3,2,1,0:T(8,128)(2,1)}, u32[]{:S(2)}, u32[]{:S(2)}) %all-to-all-start.5) | async-done | bytes 2097184 | tf_op jit(solution)/shard_map/all_to_all | solution.py:143
  241.1 11.9 %shard_map.84 = (bf16[64,128,128]{2,1,0:T(8,128)(2,1)}, f32[512,512]{1,0:T(8,128)}) custom-call(s32[4,5]{1,0:T(4,128)} %reshape.60.order_ref, s32[4,6]{1,0:T(4,128)} %add_convert_fusion.1.flip_ref, bf16[20,128,128]{2,1,0:T(8,128)(2,1)} %gates_ref.15, bf16[128,64,128]{2,1,0:T(8,128)(2,1)} %bitcast.13.refs_0_, bf16[4096,512]{1,0:T(8,128)(2,1)} %reshape.68.refs_1_), custom_call_target="tpu_custom_call" | custom-call | tf_op jit(solution)/shard_map/pallas_call | solution.py:131
  253.0 1.4 add_convert_fusion
  254.7 21.7 %all_to_all.40 = bf16[128,16,128]{2,1,0:T(8,128)(2,1)S(1)} all-to-all(bf16[128,16,128]{2,1,0:T(8,128)(2,1)S(1)} %convert_element_type.21), channel_id=1, replica_groups=mesh['amp'=64,'grp'=2] {'amp','grp'}, dimensions={0} | all-to-all | bytes 1048576 | tf_op jit(solution)/shard_map/all_to_all | solution.py:150
  277.4 4.9 %all-to-all-start.7 = ((bf16[128,16,128]{2,1,0:T(8,128)(2,1)}), bf16[128,16,128]{2,1,0:T(8,128)(2,1)S(1)}, u32[]{:S(2)}, u32[]{:S(2)}) async-start(bf16[128,16,128]{2,1,0:T(8,128)(2,1)} %broadcast_in_dim.15), calls=%async_computation.7 | async-start | bytes 1048576 | tf_op jit(solution)/shard_map/all_to_all | solution.py:153
  282.3 4.0 %pad_maximum_fusion = bf16[128,128,128]{2,1,0:T(8,128)(2,1)} fusion(bf16[64,128,128]{2,1,0:T(8,128)(2,1)} %get-tuple-element.7, bf16[64,128,128]{2,1,0:T(8,128)(2,1)S(1)} %copy-done.4), kind=kLoop, calls=%fused_computation | loop fusion | flops 2097152 | bytes 8388608 | tf_op jit(solution)/shard_map/concatenate | solution.py:188
  286.3 9.2 %all-to-all-done.7 = bf16[128,16,128]{2,1,0:T(8,128)(2,1)S(1)} async-done(((bf16[128,16,128]{2,1,0:T(8,128)(2,1)}), bf16[128,16,128]{2,1,0:T(8,128)(2,1)S(1)}, u32[]{:S(2)}, u32[]{:S(2)}) %all-to-all-start.7) | async-done | bytes 524320 | tf_op jit(solution)/shard_map/all_to_all | solution.py:153
  297.6 1.5 fusion.1
  (22 shorter events, 5.3 us)
Async XLA Ops:
  15.5 42.9 %all-to-all-start = ((bf16[64,2,64,128]{3,2,1,0:T(8,128)(2,1)}), bf16[64,2,64,128]{3,2,1,0:T(8,128)(2,1)S(1)}, u32[]{:S(2)}, u32[]{:S(2)}) async-start(bf16[64,2,64,128]{3,2,1,0:T(8,128)(2,1)} %bitcast.22), calls=%async_computation | async-start | bytes 4194304 | tf_op jit(solution)/shard_map/all_to_all | solution.py:143
  58.4 1.3 copy-start.3
  59.8 35.4 %all-to-all-start.3 = ((bf16[64,2,64,128]{3,2,1,0:T(8,128)(2,1)}), bf16[64,2,64,128]{3,2,1,0:T(8,128)(2,1)S(1)}, u32[]{:S(2)}, u32[]{:S(2)}) async-start(bf16[64,2,64,128]{3,2,1,0:T(8,128)(2,1)} %bitcast.21), calls=%async_computation.3 | async-start | bytes 4194304 | tf_op jit(solution)/shard_map/all_to_all | solution.py:143
  95.2 1.3 copy-start.1
  96.5 35.5 %all-to-all-start.1 = ((bf16[64,2,64,128]{3,2,1,0:T(8,128)(2,1)}), bf16[64,2,64,128]{3,2,1,0:T(8,128)(2,1)}, u32[]{:S(2)}, u32[]{:S(2)}) async-start(bf16[64,2,64,128]{3,2,1,0:T(8,128)(2,1)} %bitcast.27), calls=%async_computation.1 | async-start | bytes 4194304 | tf_op jit(solution)/shard_map/all_to_all | solution.py:143
  132.0 35.4 %all-to-all-start.4 = ((bf16[64,2,64,128]{3,2,1,0:T(8,128)(2,1)}), bf16[64,2,64,128]{3,2,1,0:T(8,128)(2,1)S(1)}, u32[]{:S(2)}, u32[]{:S(2)}) async-start(bf16[64,2,64,128]{3,2,1,0:T(8,128)(2,1)} %bitcast.28), calls=%async_computation.4 | async-start | bytes 4194304 | tf_op jit(solution)/shard_map/all_to_all | solution.py:143
  167.4 1.3 copy-start.2
  168.8 35.4 %all-to-all-start.2 = ((bf16[64,2,64,128]{3,2,1,0:T(8,128)(2,1)}), bf16[64,2,64,128]{3,2,1,0:T(8,128)(2,1)S(1)}, u32[]{:S(2)}, u32[]{:S(2)}) async-start(bf16[64,2,64,128]{3,2,1,0:T(8,128)(2,1)} %bitcast.29), calls=%async_computation.2 | async-start | bytes 4194304 | tf_op jit(solution)/shard_map/all_to_all | solution.py:143
  204.2 1.4 copy-start
  205.5 35.5 %all-to-all-start.5 = ((bf16[64,2,64,128]{3,2,1,0:T(8,128)(2,1)}), bf16[64,2,64,128]{3,2,1,0:T(8,128)(2,1)}, u32[]{:S(2)}, u32[]{:S(2)}) async-start(bf16[64,2,64,128]{3,2,1,0:T(8,128)(2,1)} %bitcast.26), calls=%async_computation.5 | async-start | bytes 4194304 | tf_op jit(solution)/shard_map/all_to_all | solution.py:143
  241.1 11.9 %copy-start.5 = (f32[512,512]{1,0:T(8,128)S(1)}, f32[512,512]{1,0:T(8,128)}, u32[]{:S(2)}) copy-start(f32[512,512]{1,0:T(8,128)} %get-tuple-element.8) | copy-start | bytes 3145732
  254.4 28.0 %copy-start.4 = (bf16[64,128,128]{2,1,0:T(8,128)(2,1)S(1)}, bf16[64,128,128]{2,1,0:T(8,128)(2,1)}, u32[]{:S(2)}) copy-start(bf16[64,128,128]{2,1,0:T(8,128)(2,1)} %get-tuple-element.6) | copy-start | bytes 6291460
  277.4 18.1 %all-to-all-start.7 = ((bf16[128,16,128]{2,1,0:T(8,128)(2,1)}), bf16[128,16,128]{2,1,0:T(8,128)(2,1)S(1)}, u32[]{:S(2)}, u32[]{:S(2)}) async-start(bf16[128,16,128]{2,1,0:T(8,128)(2,1)} %broadcast_in_dim.15), calls=%async_computation.7 | async-start | bytes 1048576 | tf_op jit(solution)/shard_map/all_to_all | solution.py:153

commit v11 on v10

--- a/solution.py
+++ b/solution.py
@@ -12,7 +12,7 @@
 
 
 def make_kernel(slab_in, slab_out, sources, blocks_per_source, segment):
-    def kernel(order_ref, flip_ref, gates_ref, *refs):
+    def kernel(order_ref, window_ref, swap_ref, gates_ref, *refs):
         held, diagonal = refs[-2], refs[-1]
         if slab_out:
             x_refs, adjoint_ref, o_ref, corr_ref = refs[:sources], refs[-5], refs[-4], refs[-3]
@@ -25,7 +25,7 @@
         def _():
             diagonal[...] = jnp.zeros(diagonal.shape, diagonal.dtype)
             for position in range(GATES):
-                matrix = gates_ref[order_ref[segment, position]]
+                matrix = gates_ref[order_ref[segment * GATES + position]]
                 diagonal[position, :lanes, :lanes] = matrix
                 diagonal[position, lanes:, lanes:] = matrix
 
@@ -49,8 +49,14 @@
             held[:, :, :lanes] = jnp.swapaxes(held[:, :, :lanes], 1, 2)
             held[:, :, lanes:] = jnp.swapaxes(held[:, :, lanes:], 1, 2)
 
+        starting = 0 if segment == 0 else 1 - swap_ref[segment - 1]
+        wanted = 1 - swap_ref[segment] if segment < SEGS - 1 else 0
+
         def one_gate(position, carry):
-            pl.when(flip_ref[segment, position] == 1)(flip)
+            base = segment * GATES
+            previous = window_ref[base + jnp.maximum(position - 1, 0)]
+            lanes_now = jnp.where(position == 0, starting, previous)
+            pl.when(window_ref[base + position] != lanes_now)(flip)
             matrix = diagonal[position]
             flat = held[...].reshape(half * wide, pair)
             out = lax.dot_general(
@@ -60,7 +66,7 @@
             return carry
 
         lax.fori_loop(0, GATES, one_gate, 0)
-        pl.when(flip_ref[segment, GATES] == 1)(flip)
+        pl.when(window_ref[segment * GATES + GATES - 1] != wanted)(flip)
 
         first = held[:, :, :lanes]
         second = held[:, :, lanes:]
@@ -84,7 +90,7 @@
     return kernel
 
 
-def run_segment(sources, gate_mats, order, flips, segment, slab_in, slab_out, slabs, offset=0,
+def run_segment(sources, gate_mats, order, window, swaps, segment, slab_in, slab_out, slabs, offset=0,
                 adjoint=None, adjoint_offset=0):
     wide = gate_mats.shape[1]
     lanes = sources[0].shape[2]
@@ -92,7 +98,7 @@
     per_source = blocks // len(sources)
 
     def source_spec(index):
-        def pick(i, o, f):
+        def pick(i, o, w, s):
             local = jnp.clip(i - index * per_source, 0, per_source - 1) + offset
             return (local, 0, 0) if slab_in else (0, local, 0)
 
@@ -103,23 +109,23 @@
     if slab_out:
         rows_per_slab = wide // 4
         out_spec = [
-            pl.BlockSpec((BLOCK, wide, lanes), lambda i, o, f: (i, 0, 0)),
-            pl.BlockSpec((4 * lanes, 4 * lanes), lambda i, o, f: (0, 0)),
+            pl.BlockSpec((BLOCK, wide, lanes), lambda i, o, w, s: (i, 0, 0)),
+            pl.BlockSpec((4 * lanes, 4 * lanes), lambda i, o, w, s: (0, 0)),
         ]
         out_shape = [
             jax.ShapeDtypeStruct((slabs, wide, lanes), dtype),
             jax.ShapeDtypeStruct((4 * lanes, 4 * lanes), jnp.float32),
         ]
-        adjoint_spec = [pl.BlockSpec((BLOCK * rows_per_slab, 4 * lanes), lambda i, o, f: (i + adjoint_offset, 0))]
+        adjoint_spec = [pl.BlockSpec((BLOCK * rows_per_slab, 4 * lanes), lambda i, o, w, s: (i + adjoint_offset, 0))]
     else:
         adjoint_spec = []
     if not slab_out:
-        out_spec = pl.BlockSpec((wide, BLOCK, lanes), lambda i, o, f: (0, i, 0))
+        out_spec = pl.BlockSpec((wide, BLOCK, lanes), lambda i, o, w, s: (0, i, 0))
         out_shape = jax.ShapeDtypeStruct((wide, slabs, lanes), dtype)
     grid_spec = pltpu.PrefetchScalarGridSpec(
-        num_scalar_prefetch=2,
+        num_scalar_prefetch=3,
         grid=(blocks,),
-        in_specs=[pl.BlockSpec(gate_mats.shape, lambda i, o, f: (0, 0, 0))]
+        in_specs=[pl.BlockSpec(gate_mats.shape, lambda i, o, w, s: (0, 0, 0))]
         + [source_spec(index) for index in range(len(sources))]
         + adjoint_spec,
         out_specs=out_spec,
@@ -133,7 +139,7 @@
         grid_spec=grid_spec,
         out_shape=out_shape,
         compiler_params=pltpu.CompilerParams(dimension_semantics=("arbitrary",)),
-    )(order, flips, gate_mats, *sources, *([] if adjoint is None else [adjoint]))
+    )(order, window, swaps, gate_mats, *sources, *([] if adjoint is None else [adjoint]))
 
 
 def swap_major(values):
@@ -157,26 +163,20 @@
 def on_device(amplitudes, adjoint, gate_mats, gate_order, gate_window, swap_window):
     slabs = amplitudes.shape[0]
     chunk = slabs // CHUNKS
-    windows = gate_window.reshape(SEGS, GATES)
-    starting = jnp.concatenate([jnp.zeros((1,), jnp.int32), 1 - swap_window])
-    wanted = jnp.concatenate([1 - swap_window, jnp.zeros((1,), jnp.int32)])
-    before = jnp.concatenate([starting[:, None], windows[:, :-1]], axis=1)
-    flips = jnp.concatenate([windows != before, (windows[:, -1] != wanted)[:, None]], axis=1)
-    flips = flips.astype(jnp.int32)
-    order = gate_order.reshape(SEGS, GATES)
+    order, window, swaps = gate_order, gate_window, swap_window
     chunks = None
     for segment in range(SEGS):
         if segment == 0:
             chunks = [
-                run_segment([amplitudes], gate_mats, order, flips, segment, True, False, chunk, c * (chunk // BLOCK))
+                run_segment([amplitudes], gate_mats, order, window, swaps, segment, True, False, chunk, c * (chunk // BLOCK))
                 for c in range(CHUNKS)
             ]
         elif segment < SEGS - 1:
-            chunks = [run_segment([part], gate_mats, order, flips, segment, False, False, chunk) for part in chunks]
+            chunks = [run_segment([part], gate_mats, order, window, swaps, segment, False, False, chunk) for part in chunks]
         else:
             adjoint_flat = adjoint.reshape(-1, 4 * adjoint.shape[2])
             finals = [
-                run_segment([part], gate_mats, order, flips, segment, False, True, chunk,
+                run_segment([part], gate_mats, order, window, swaps, segment, False, True, chunk,
                             adjoint=adjoint_flat, adjoint_offset=c * (chunk // BLOCK))
                 for c, part in enumerate(chunks)
             ]

time: 301 us -> 299 us (level)
  no operation moved by 1% of the time
where the time goes in v11:
time: 299 us; the launch traced here: 296 us
  waiting for transfers between devices  115 us (38%)
  Pallas kernels  93.2 us (31%)
  starting transfers between devices  42.4 us (14%)
  blocking collectives  21.7 us (7%)
  local copies, waits for them, and re-layouts  14.4 us (5%)
  other arithmetic  5.49 us (2%)
    all_to_all x6, waiting for transfers between devices, swap_major(): lax.all_to_all(split, 'amp', split_axis=0, concat_axis=0, tiled=True)  106 us
    pallas_call x8, Pallas kernels, run_segment(): pl.pallas_call(make_kernel(slab_in, slab_out, len(sources), per_source, s...  93.2 us
    all_to_all x6, starting transfers between devices, swap_major(): lax.all_to_all(split, 'amp', split_axis=0, concat_axis=0, tiled=True)  37.5 us
    all_to_all x1, blocking collectives, all_sum(): lax.all_to_all(pieces, axes, split_axis=0, concat_axis=0, tiled=True)  21.7 us
    all_to_all x1, waiting for transfers between devices, all_sum(): lax.all_to_all(spread, axes, split_axis=0, concat_axis=0, tiled=True)  9.21 us
    reshape x1, local copies, waits for them, and re-layouts, on_device(): adjoint_flat = adjoint.reshape(-1, 4 * adjoint.shape[2])  7.52 us
  transfers between devices with their start and end apart: 7, of which 7 were waited for; matrix products, arithmetic and copies ran while one was open for 4% of the time, Pallas kernels for 23%

profile of v11, /device:TPU:1, one launch (start us, length us, event | category | flops | bytes accessed | tf_op | source)
XLA Modules:
  0.0 296.5 jit_solution(7207169981500051823)
XLA Ops:
  0.6 11.0 %shard_map.77 = bf16[128,64,128]{2,1,0:T(8,128)(2,1)} custom-call(s32[20]{0:T(128)} %order_ref.15, s32[20]{0:T(128)} %window_ref.15, s32[3]{0:T(128)} %swap_ref.15, bf16[20,128,128]{2,1,0:T(8,128)(2,1)} %gates_ref.15, bf16[128,128,128]{2,1,0:T(8,128)(2,1)} %refs_0_.3), custom_call_target="tpu_custom_call" | custom-call | tf_op jit(solution)/shard_map/pallas_call | solution.py:137
  11.6 12.5 %all-to-all-start = ((bf16[64,2,64,128]{3,2,1,0:T(8,128)(2,1)}), bf16[64,2,64,128]{3,2,1,0:T(8,128)(2,1)S(1)}, u32[]{:S(2)}, u32[]{:S(2)}) async-start(bf16[64,2,64,128]{3,2,1,0:T(8,128)(2,1)} %bitcast.24), calls=%async_computation | async-start | bytes 4194304 | tf_op jit(solution)/shard_map/all_to_all | solution.py:149
  24.0 10.9 %shard_map.81 = bf16[128,64,128]{2,1,0:T(8,128)(2,1)} custom-call(s32[20]{0:T(128)} %order_ref.15, s32[20]{0:T(128)} %window_ref.15, s32[3]{0:T(128)} %swap_ref.15, bf16[20,128,128]{2,1,0:T(8,128)(2,1)} %gates_ref.15, bf16[128,128,128]{2,1,0:T(8,128)(2,1)} %refs_0_.3), custom_call_target="tpu_custom_call" | custom-call | tf_op jit(solution)/shard_map/pallas_call | solution.py:137
  34.9 19.6 %all-to-all-done = bf16[64,2,64,128]{3,2,1,0:T(8,128)(2,1)S(1)} async-done(((bf16[64,2,64,128]{3,2,1,0:T(8,128)(2,1)}), bf16[64,2,64,128]{3,2,1,0:T(8,128)(2,1)S(1)}, u32[]{:S(2)}, u32[]{:S(2)}) %all-to-all-start) | async-done | bytes 2097184 | tf_op jit(solution)/shard_map/all_to_all | solution.py:149
  54.5 1.3 copy-done.3
  55.9 4.9 %all-to-all-start.3 = ((bf16[64,2,64,128]{3,2,1,0:T(8,128)(2,1)}), bf16[64,2,64,128]{3,2,1,0:T(8,128)(2,1)S(1)}, u32[]{:S(2)}, u32[]{:S(2)}) async-start(bf16[64,2,64,128]{3,2,1,0:T(8,128)(2,1)} %bitcast.23), calls=%async_computation.3 | async-start | bytes 4194304 | tf_op jit(solution)/shard_map/all_to_all | solution.py:149
  60.8 11.3 %shard_map.78 = bf16[128,64,128]{2,1,0:T(8,128)(2,1)} custom-call(s32[20]{0:T(128)} %order_ref.15, s32[20]{0:T(128)} %window_ref.15, s32[3]{0:T(128)} %swap_ref.15, bf16[20,128,128]{2,1,0:T(8,128)(2,1)} %gates_ref.15, bf16[128,64,128]{2,1,0:T(8,128)(2,1)} %bitcast.18), custom_call_target="tpu_custom_call" | custom-call | tf_op jit(solution)/shard_map/pallas_call | solution.py:137
  72.1 19.2 %all-to-all-done.3 = bf16[64,2,64,128]{3,2,1,0:T(8,128)(2,1)S(1)} async-done(((bf16[64,2,64,128]{3,2,1,0:T(8,128)(2,1)}), bf16[64,2,64,128]{3,2,1,0:T(8,128)(2,1)S(1)}, u32[]{:S(2)}, u32[]{:S(2)}) %all-to-all-start.3) | async-done | bytes 2097184 | tf_op jit(solution)/shard_map/all_to_all | solution.py:149
  91.3 1.3 copy-done.1
  92.6 5.1 %all-to-all-start.1 = ((bf16[64,2,64,128]{3,2,1,0:T(8,128)(2,1)}), bf16[64,2,64,128]{3,2,1,0:T(8,128)(2,1)}, u32[]{:S(2)}, u32[]{:S(2)}) async-start(bf16[64,2,64,128]{3,2,1,0:T(8,128)(2,1)} %bitcast.20), calls=%async_computation.1 | async-start | bytes 4194304 | tf_op jit(solution)/shard_map/all_to_all | solution.py:149
  97.7 11.2 %shard_map.82 = bf16[128,64,128]{2,1,0:T(8,128)(2,1)} custom-call(s32[20]{0:T(128)} %order_ref.15, s32[20]{0:T(128)} %window_ref.15, s32[3]{0:T(128)} %swap_ref.15, bf16[20,128,128]{2,1,0:T(8,128)(2,1)} %gates_ref.15, bf16[128,64,128]{2,1,0:T(8,128)(2,1)} %bitcast.16), custom_call_target="tpu_custom_call" | custom-call | tf_op jit(solution)/shard_map/pallas_call | solution.py:137
  108.9 19.2 %all-to-all-done.1 = bf16[64,2,64,128]{3,2,1,0:T(8,128)(2,1)} async-done(((bf16[64,2,64,128]{3,2,1,0:T(8,128)(2,1)}), bf16[64,2,64,128]{3,2,1,0:T(8,128)(2,1)}, u32[]{:S(2)}, u32[]{:S(2)}) %all-to-all-start.1) | async-done | bytes 2097184 | tf_op jit(solution)/shard_map/all_to_all | solution.py:149
  128.1 4.9 %all-to-all-start.4 = ((bf16[64,2,64,128]{3,2,1,0:T(8,128)(2,1)}), bf16[64,2,64,128]{3,2,1,0:T(8,128)(2,1)S(1)}, u32[]{:S(2)}, u32[]{:S(2)}) async-start(bf16[64,2,64,128]{3,2,1,0:T(8,128)(2,1)} %bitcast.21), calls=%async_computation.4 | async-start | bytes 4194304 | tf_op jit(solution)/shard_map/all_to_all | solution.py:149
  133.1 11.3 %shard_map.79 = bf16[128,64,128]{2,1,0:T(8,128)(2,1)} custom-call(s32[20]{0:T(128)} %order_ref.15, s32[20]{0:T(128)} %window_ref.15, s32[3]{0:T(128)} %swap_ref.15, bf16[20,128,128]{2,1,0:T(8,128)(2,1)} %gates_ref.15, bf16[128,64,128]{2,1,0:T(8,128)(2,1)} %bitcast.3.refs_0_), custom_call_target="tpu_custom_call" | custom-call | tf_op jit(solution)/shard_map/pallas_call | solution.py:137
  144.3 19.2 %all-to-all-done.4 = bf16[64,2,64,128]{3,2,1,0:T(8,128)(2,1)S(1)} async-done(((bf16[64,2,64,128]{3,2,1,0:T(8,128)(2,1)}), bf16[64,2,64,128]{3,2,1,0:T(8,128)(2,1)S(1)}, u32[]{:S(2)}, u32[]{:S(2)}) %all-to-all-start.4) | async-done | bytes 2097184 | tf_op jit(solution)/shard_map/all_to_all | solution.py:149
  163.5 1.3 copy-done.2
  164.9 4.9 %all-to-all-start.2 = ((bf16[64,2,64,128]{3,2,1,0:T(8,128)(2,1)}), bf16[64,2,64,128]{3,2,1,0:T(8,128)(2,1)S(1)}, u32[]{:S(2)}, u32[]{:S(2)}) async-start(bf16[64,2,64,128]{3,2,1,0:T(8,128)(2,1)} %bitcast.22), calls=%async_computation.2 | async-start | bytes 4194304 | tf_op jit(solution)/shard_map/all_to_all | solution.py:149
  169.8 11.3 %shard_map.83 = bf16[128,64,128]{2,1,0:T(8,128)(2,1)} custom-call(s32[20]{0:T(128)} %order_ref.15, s32[20]{0:T(128)} %window_ref.15, s32[3]{0:T(128)} %swap_ref.15, bf16[20,128,128]{2,1,0:T(8,128)(2,1)} %gates_ref.15, bf16[128,64,128]{2,1,0:T(8,128)(2,1)} %bitcast.17), custom_call_target="tpu_custom_call" | custom-call | tf_op jit(solution)/shard_map/pallas_call | solution.py:137
  181.1 19.2 %all-to-all-done.2 = bf16[64,2,64,128]{3,2,1,0:T(8,128)(2,1)S(1)} async-done(((bf16[64,2,64,128]{3,2,1,0:T(8,128)(2,1)}), bf16[64,2,64,128]{3,2,1,0:T(8,128)(2,1)S(1)}, u32[]{:S(2)}, u32[]{:S(2)}) %all-to-all-start.2) | async-done | bytes 2097184 | tf_op jit(solution)/shard_map/all_to_all | solution.py:149
  200.3 1.3 copy-done
  201.6 5.1 %all-to-all-start.5 = ((bf16[64,2,64,128]{3,2,1,0:T(8,128)(2,1)}), bf16[64,2,64,128]{3,2,1,0:T(8,128)(2,1)}, u32[]{:S(2)}, u32[]{:S(2)}) async-start(bf16[64,2,64,128]{3,2,1,0:T(8,128)(2,1)} %bitcast.19), calls=%async_computation.5 | async-start | bytes 4194304 | tf_op jit(solution)/shard_map/all_to_all | solution.py:149
  206.7 7.5 %reshape.58.refs_1_ = bf16[4096,512]{1,0:T(8,128)(2,1)} reshape(bf16[128,128,128]{2,1,0:T(8,128)(2,1)} %param.7) | data formatting | bytes 8388608 | tf_op jit(solution)/shard_map/reshape | solution.py:177
  214.3 13.1 %shard_map.80 = (bf16[64,128,128]{2,1,0:T(8,128)(2,1)}, f32[512,512]{1,0:T(8,128)}) custom-call(s32[20]{0:T(128)} %order_ref.15, s32[20]{0:T(128)} %window_ref.15, s32[3]{0:T(128)} %swap_ref.15, bf16[20,128,128]{2,1,0:T(8,128)(2,1)} %gates_ref.15, bf16[128,64,128]{2,1,0:T(8,128)(2,1)} %bitcast.15, bf16[4096,512]{1,0:T(8,128)(2,1)} %reshape.58.refs_1_), custom_call_target="tpu_custom_call" | custom-call | tf_op jit(solution)/shard_map/pallas_call | solution.py:137
  227.3 9.8 %all-to-all-done.5 = bf16[64,2,64,128]{3,2,1,0:T(8,128)(2,1)} async-done(((bf16[64,2,64,128]{3,2,1,0:T(8,128)(2,1)}), bf16[64,2,64,128]{3,2,1,0:T(8,128)(2,1)}, u32[]{:S(2)}, u32[]{:S(2)}) %all-to-all-start.5) | async-done | bytes 2097184 | tf_op jit(solution)/shard_map/all_to_all | solution.py:149
  237.2 13.2 %shard_map.84 = (bf16[64,128,128]{2,1,0:T(8,128)(2,1)}, f32[512,512]{1,0:T(8,128)}) custom-call(s32[20]{0:T(128)} %order_ref.15, s32[20]{0:T(128)} %window_ref.15, s32[3]{0:T(128)} %swap_ref.15, bf16[20,128,128]{2,1,0:T(8,128)(2,1)} %gates_ref.15, bf16[128,64,128]{2,1,0:T(8,128)(2,1)} %bitcast.11.refs_0_, bf16[4096,512]{1,0:T(8,128)(2,1)} %reshape.58.refs_1_), custom_call_target="tpu_custom_call" | custom-call | tf_op jit(solution)/shard_map/pallas_call | solution.py:137
  250.3 1.4 add_convert_fusion
  252.1 21.7 %all_to_all.40 = bf16[128,16,128]{2,1,0:T(8,128)(2,1)S(1)} all-to-all(bf16[128,16,128]{2,1,0:T(8,128)(2,1)S(1)} %convert_element_type.17), channel_id=1, replica_groups=mesh['amp'=64,'grp'=2] {'amp','grp'}, dimensions={0} | all-to-all | bytes 1048576 | tf_op jit(solution)/shard_map/all_to_all | solution.py:156
  274.8 4.9 %all-to-all-start.7 = ((bf16[128,16,128]{2,1,0:T(8,128)(2,1)}), bf16[128,16,128]{2,1,0:T(8,128)(2,1)S(1)}, u32[]{:S(2)}, u32[]{:S(2)}) async-start(bf16[128,16,128]{2,1,0:T(8,128)(2,1)} %broadcast_in_dim.10), calls=%async_computation.7 | async-start | bytes 1048576 | tf_op jit(solution)/shard_map/all_to_all | solution.py:159
  279.7 4.0 %pad_maximum_fusion = bf16[128,128,128]{2,1,0:T(8,128)(2,1)} fusion(bf16[64,128,128]{2,1,0:T(8,128)(2,1)} %get-tuple-element.7, bf16[64,128,128]{2,1,0:T(8,128)(2,1)S(1)} %copy-done.4), kind=kLoop, calls=%fused_computation | loop fusion | flops 2097152 | bytes 8388608 | tf_op jit(solution)/shard_map/concatenate | solution.py:188
  283.7 9.2 %all-to-all-done.7 = bf16[128,16,128]{2,1,0:T(8,128)(2,1)S(1)} async-done(((bf16[128,16,128]{2,1,0:T(8,128)(2,1)}), bf16[128,16,128]{2,1,0:T(8,128)(2,1)S(1)}, u32[]{:S(2)}, u32[]{:S(2)}) %all-to-all-start.7) | async-done | bytes 524320 | tf_op jit(solution)/shard_map/all_to_all | solution.py:159
  293.2 1.1 select_reduce_fusion
  295.0 1.5 fusion.1
  (12 shorter events, 1.7 us)
Async XLA Ops:
  11.6 42.9 %all-to-all-start = ((bf16[64,2,64,128]{3,2,1,0:T(8,128)(2,1)}), bf16[64,2,64,128]{3,2,1,0:T(8,128)(2,1)S(1)}, u32[]{:S(2)}, u32[]{:S(2)}) async-start(bf16[64,2,64,128]{3,2,1,0:T(8,128)(2,1)} %bitcast.24), calls=%async_computation | async-start | bytes 4194304 | tf_op jit(solution)/shard_map/all_to_all | solution.py:149
  54.5 1.3 copy-start.3
  55.9 35.4 %all-to-all-start.3 = ((bf16[64,2,64,128]{3,2,1,0:T(8,128)(2,1)}), bf16[64,2,64,128]{3,2,1,0:T(8,128)(2,1)S(1)}, u32[]{:S(2)}, u32[]{:S(2)}) async-start(bf16[64,2,64,128]{3,2,1,0:T(8,128)(2,1)} %bitcast.23), calls=%async_computation.3 | async-start | bytes 4194304 | tf_op jit(solution)/shard_map/all_to_all | solution.py:149
  91.3 1.3 copy-start.1
  92.6 35.5 %all-to-all-start.1 = ((bf16[64,2,64,128]{3,2,1,0:T(8,128)(2,1)}), bf16[64,2,64,128]{3,2,1,0:T(8,128)(2,1)}, u32[]{:S(2)}, u32[]{:S(2)}) async-start(bf16[64,2,64,128]{3,2,1,0:T(8,128)(2,1)} %bitcast.20), calls=%async_computation.1 | async-start | bytes 4194304 | tf_op jit(solution)/shard_map/all_to_all | solution.py:149
  128.1 35.4 %all-to-all-start.4 = ((bf16[64,2,64,128]{3,2,1,0:T(8,128)(2,1)}), bf16[64,2,64,128]{3,2,1,0:T(8,128)(2,1)S(1)}, u32[]{:S(2)}, u32[]{:S(2)}) async-start(bf16[64,2,64,128]{3,2,1,0:T(8,128)(2,1)} %bitcast.21), calls=%async_computation.4 | async-start | bytes 4194304 | tf_op jit(solution)/shard_map/all_to_all | solution.py:149
  163.5 1.3 copy-start.2
  164.9 35.4 %all-to-all-start.2 = ((bf16[64,2,64,128]{3,2,1,0:T(8,128)(2,1)}), bf16[64,2,64,128]{3,2,1,0:T(8,128)(2,1)S(1)}, u32[]{:S(2)}, u32[]{:S(2)}) async-start(bf16[64,2,64,128]{3,2,1,0:T(8,128)(2,1)} %bitcast.22), calls=%async_computation.2 | async-start | bytes 4194304 | tf_op jit(solution)/shard_map/all_to_all | solution.py:149
  200.3 1.4 copy-start
  201.6 35.5 %all-to-all-start.5 = ((bf16[64,2,64,128]{3,2,1,0:T(8,128)(2,1)}), bf16[64,2,64,128]{3,2,1,0:T(8,128)(2,1)}, u32[]{:S(2)}, u32[]{:S(2)}) async-start(bf16[64,2,64,128]{3,2,1,0:T(8,128)(2,1)} %bitcast.19), calls=%async_computation.5 | async-start | bytes 4194304 | tf_op jit(solution)/shard_map/all_to_all | solution.py:149
  237.1 13.2 %copy-start.5 = (f32[512,512]{1,0:T(8,128)S(1)}, f32[512,512]{1,0:T(8,128)}, u32[]{:S(2)}) copy-start(f32[512,512]{1,0:T(8,128)} %get-tuple-element.8) | copy-start | bytes 3145732
  251.7 28.0 %copy-start.4 = (bf16[64,128,128]{2,1,0:T(8,128)(2,1)S(1)}, bf16[64,128,128]{2,1,0:T(8,128)(2,1)}, u32[]{:S(2)}) copy-start(bf16[64,128,128]{2,1,0:T(8,128)(2,1)} %get-tuple-element.6) | copy-start | bytes 6291460
  274.8 18.1 %all-to-all-start.7 = ((bf16[128,16,128]{2,1,0:T(8,128)(2,1)}), bf16[128,16,128]{2,1,0:T(8,128)(2,1)S(1)}, u32[]{:S(2)}, u32[]{:S(2)}) async-start(bf16[128,16,128]{2,1,0:T(8,128)(2,1)} %broadcast_in_dim.10), calls=%async_computation.7 | async-start | bytes 1048576 | tf_op jit(solution)/shard_map/all_to_all | solution.py:159

commit v12 on v11

--- a/solution.py
+++ b/solution.py
@@ -8,6 +8,7 @@
 SEGS = 4
 GATES = 5
 BLOCK = 32
+LAST_BLOCK = 16
 CHUNKS = 2
 
 
@@ -92,6 +93,7 @@
 
 def run_segment(sources, gate_mats, order, window, swaps, segment, slab_in, slab_out, slabs, offset=0,
                 adjoint=None, adjoint_offset=0):
+    BLOCK = LAST_BLOCK if slab_out else globals()["BLOCK"]
     wide = gate_mats.shape[1]
     lanes = sources[0].shape[2]
     blocks = slabs // BLOCK
@@ -177,7 +179,7 @@
             adjoint_flat = adjoint.reshape(-1, 4 * adjoint.shape[2])
             finals = [
                 run_segment([part], gate_mats, order, window, swaps, segment, False, True, chunk,
-                            adjoint=adjoint_flat, adjoint_offset=c * (chunk // BLOCK))
+                            adjoint=adjoint_flat, adjoint_offset=c * (chunk // LAST_BLOCK))
                 for c, part in enumerate(chunks)
             ]
         if segment < SEGS - 1:

time: 299 us -> 301 us (level)
  Pallas kernels: 93.2 us -> 97.6 us
    pallas_call x8, Pallas kernels: 93.2 us -> 97.6 us  [run_segment(): pl.pallas_call(make_kernel(slab_in, slab_out, len(sources), per_source, s...]
  transfers between devices with their start and end apart: 7 -> 7, of which waited for: 7 -> 7; matrix products, arithmetic and copies ran while one was open for 4% -> 4% of each run, Pallas kernels for 23% -> 24%
where the time goes in v12:
time: 301 us; the launch traced here: 299 us
  waiting for transfers between devices  113 us (38%)
  Pallas kernels  97.6 us (32%)
  starting transfers between devices  42.4 us (14%)
  blocking collectives  21.7 us (7%)
  local copies, waits for them, and re-layouts  14.4 us (5%)
  other arithmetic  5.49 us (2%)
    all_to_all x6, waiting for transfers between devices, swap_major(): lax.all_to_all(split, 'amp', split_axis=0, concat_axis=0, tiled=True)  104 us
    pallas_call x8, Pallas kernels, run_segment(): pl.pallas_call(make_kernel(slab_in, slab_out, len(sources), per_source, s...  97.6 us
    all_to_all x6, starting transfers between devices, swap_major(): lax.all_to_all(split, 'amp', split_axis=0, concat_axis=0, tiled=True)  37.5 us
    all_to_all x1, blocking collectives, all_sum(): lax.all_to_all(pieces, axes, split_axis=0, concat_axis=0, tiled=True)  21.7 us
    all_to_all x1, waiting for transfers between devices, all_sum(): lax.all_to_all(spread, axes, split_axis=0, concat_axis=0, tiled=True)  9.21 us
    reshape x1, local copies, waits for them, and re-layouts, on_device(): adjoint_flat = adjoint.reshape(-1, 4 * adjoint.shape[2])  7.52 us
  transfers between devices with their start and end apart: 7, of which 7 were waited for; matrix products, arithmetic and copies ran while one was open for 4% of the time, Pallas kernels for 24%

profile of v12, /device:TPU:1, one launch (start us, length us, event | category | flops | bytes accessed | tf_op | source)
XLA Modules:
  0.0 298.7 jit_solution(16222721926561351589)
XLA Ops:
  0.6 11.6 %shard_map.77 = bf16[128,64,128]{2,1,0:T(8,128)(2,1)} custom-call(s32[20]{0:T(128)} %order_ref.15, s32[20]{0:T(128)} %window_ref.15, s32[3]{0:T(128)} %swap_ref.15, bf16[20,128,128]{2,1,0:T(8,128)(2,1)} %gates_ref.15, bf16[128,128,128]{2,1,0:T(8,128)(2,1)} %refs_0_.3), custom_call_target="tpu_custom_call" | custom-call | tf_op jit(solution)/shard_map/pallas_call | solution.py:139
  12.2 12.5 %all-to-all-start = ((bf16[64,2,64,128]{3,2,1,0:T(8,128)(2,1)}), bf16[64,2,64,128]{3,2,1,0:T(8,128)(2,1)S(1)}, u32[]{:S(2)}, u32[]{:S(2)}) async-start(bf16[64,2,64,128]{3,2,1,0:T(8,128)(2,1)} %bitcast.24), calls=%async_computation | async-start | bytes 4194304 | tf_op jit(solution)/shard_map/all_to_all | solution.py:151
  24.7 11.5 %shard_map.81 = bf16[128,64,128]{2,1,0:T(8,128)(2,1)} custom-call(s32[20]{0:T(128)} %order_ref.15, s32[20]{0:T(128)} %window_ref.15, s32[3]{0:T(128)} %swap_ref.15, bf16[20,128,128]{2,1,0:T(8,128)(2,1)} %gates_ref.15, bf16[128,128,128]{2,1,0:T(8,128)(2,1)} %refs_0_.3), custom_call_target="tpu_custom_call" | custom-call | tf_op jit(solution)/shard_map/pallas_call | solution.py:139
  36.2 19.0 %all-to-all-done = bf16[64,2,64,128]{3,2,1,0:T(8,128)(2,1)S(1)} async-done(((bf16[64,2,64,128]{3,2,1,0:T(8,128)(2,1)}), bf16[64,2,64,128]{3,2,1,0:T(8,128)(2,1)S(1)}, u32[]{:S(2)}, u32[]{:S(2)}) %all-to-all-start) | async-done | bytes 2097184 | tf_op jit(solution)/shard_map/all_to_all | solution.py:151
  55.2 1.3 copy-done.3
  56.5 4.9 %all-to-all-start.3 = ((bf16[64,2,64,128]{3,2,1,0:T(8,128)(2,1)}), bf16[64,2,64,128]{3,2,1,0:T(8,128)(2,1)S(1)}, u32[]{:S(2)}, u32[]{:S(2)}) async-start(bf16[64,2,64,128]{3,2,1,0:T(8,128)(2,1)} %bitcast.23), calls=%async_computation.3 | async-start | bytes 4194304 | tf_op jit(solution)/shard_map/all_to_all | solution.py:151
  61.4 11.3 %shard_map.78 = bf16[128,64,128]{2,1,0:T(8,128)(2,1)} custom-call(s32[20]{0:T(128)} %order_ref.15, s32[20]{0:T(128)} %window_ref.15, s32[3]{0:T(128)} %swap_ref.15, bf16[20,128,128]{2,1,0:T(8,128)(2,1)} %gates_ref.15, bf16[128,64,128]{2,1,0:T(8,128)(2,1)} %bitcast.18), custom_call_target="tpu_custom_call" | custom-call | tf_op jit(solution)/shard_map/pallas_call | solution.py:139
  72.7 19.2 %all-to-all-done.3 = bf16[64,2,64,128]{3,2,1,0:T(8,128)(2,1)S(1)} async-done(((bf16[64,2,64,128]{3,2,1,0:T(8,128)(2,1)}), bf16[64,2,64,128]{3,2,1,0:T(8,128)(2,1)S(1)}, u32[]{:S(2)}, u32[]{:S(2)}) %all-to-all-start.3) | async-done | bytes 2097184 | tf_op jit(solution)/shard_map/all_to_all | solution.py:151
  91.9 1.3 copy-done.1
  93.2 5.1 %all-to-all-start.1 = ((bf16[64,2,64,128]{3,2,1,0:T(8,128)(2,1)}), bf16[64,2,64,128]{3,2,1,0:T(8,128)(2,1)}, u32[]{:S(2)}, u32[]{:S(2)}) async-start(bf16[64,2,64,128]{3,2,1,0:T(8,128)(2,1)} %bitcast.20), calls=%async_computation.1 | async-start | bytes 4194304 | tf_op jit(solution)/shard_map/all_to_all | solution.py:151
  98.4 11.2 %shard_map.82 = bf16[128,64,128]{2,1,0:T(8,128)(2,1)} custom-call(s32[20]{0:T(128)} %order_ref.15, s32[20]{0:T(128)} %window_ref.15, s32[3]{0:T(128)} %swap_ref.15, bf16[20,128,128]{2,1,0:T(8,128)(2,1)} %gates_ref.15, bf16[128,64,128]{2,1,0:T(8,128)(2,1)} %bitcast.16), custom_call_target="tpu_custom_call" | custom-call | tf_op jit(solution)/shard_map/pallas_call | solution.py:139
  109.6 19.2 %all-to-all-done.1 = bf16[64,2,64,128]{3,2,1,0:T(8,128)(2,1)} async-done(((bf16[64,2,64,128]{3,2,1,0:T(8,128)(2,1)}), bf16[64,2,64,128]{3,2,1,0:T(8,128)(2,1)}, u32[]{:S(2)}, u32[]{:S(2)}) %all-to-all-start.1) | async-done | bytes 2097184 | tf_op jit(solution)/shard_map/all_to_all | solution.py:151
  128.8 4.9 %all-to-all-start.4 = ((bf16[64,2,64,128]{3,2,1,0:T(8,128)(2,1)}), bf16[64,2,64,128]{3,2,1,0:T(8,128)(2,1)S(1)}, u32[]{:S(2)}, u32[]{:S(2)}) async-start(bf16[64,2,64,128]{3,2,1,0:T(8,128)(2,1)} %bitcast.21), calls=%async_computation.4 | async-start | bytes 4194304 | tf_op jit(solution)/shard_map/all_to_all | solution.py:151
  133.7 11.3 %shard_map.79 = bf16[128,64,128]{2,1,0:T(8,128)(2,1)} custom-call(s32[20]{0:T(128)} %order_ref.15, s32[20]{0:T(128)} %window_ref.15, s32[3]{0:T(128)} %swap_ref.15, bf16[20,128,128]{2,1,0:T(8,128)(2,1)} %gates_ref.15, bf16[128,64,128]{2,1,0:T(8,128)(2,1)} %bitcast.3.refs_0_), custom_call_target="tpu_custom_call" | custom-call | tf_op jit(solution)/shard_map/pallas_call | solution.py:139
  144.9 19.2 %all-to-all-done.4 = bf16[64,2,64,128]{3,2,1,0:T(8,128)(2,1)S(1)} async-done(((bf16[64,2,64,128]{3,2,1,0:T(8,128)(2,1)}), bf16[64,2,64,128]{3,2,1,0:T(8,128)(2,1)S(1)}, u32[]{:S(2)}, u32[]{:S(2)}) %all-to-all-start.4) | async-done | bytes 2097184 | tf_op jit(solution)/shard_map/all_to_all | solution.py:151
  164.2 1.3 copy-done.2
  165.5 4.9 %all-to-all-start.2 = ((bf16[64,2,64,128]{3,2,1,0:T(8,128)(2,1)}), bf16[64,2,64,128]{3,2,1,0:T(8,128)(2,1)S(1)}, u32[]{:S(2)}, u32[]{:S(2)}) async-start(bf16[64,2,64,128]{3,2,1,0:T(8,128)(2,1)} %bitcast.22), calls=%async_computation.2 | async-start | bytes 4194304 | tf_op jit(solution)/shard_map/all_to_all | solution.py:151
  170.4 11.3 %shard_map.83 = bf16[128,64,128]{2,1,0:T(8,128)(2,1)} custom-call(s32[20]{0:T(128)} %order_ref.15, s32[20]{0:T(128)} %window_ref.15, s32[3]{0:T(128)} %swap_ref.15, bf16[20,128,128]{2,1,0:T(8,128)(2,1)} %gates_ref.15, bf16[128,64,128]{2,1,0:T(8,128)(2,1)} %bitcast.17), custom_call_target="tpu_custom_call" | custom-call | tf_op jit(solution)/shard_map/pallas_call | solution.py:139
  181.7 19.2 %all-to-all-done.2 = bf16[64,2,64,128]{3,2,1,0:T(8,128)(2,1)S(1)} async-done(((bf16[64,2,64,128]{3,2,1,0:T(8,128)(2,1)}), bf16[64,2,64,128]{3,2,1,0:T(8,128)(2,1)S(1)}, u32[]{:S(2)}, u32[]{:S(2)}) %all-to-all-start.2) | async-done | bytes 2097184 | tf_op jit(solution)/shard_map/all_to_all | solution.py:151
  200.9 1.3 copy-done
  202.2 5.1 %all-to-all-start.5 = ((bf16[64,2,64,128]{3,2,1,0:T(8,128)(2,1)}), bf16[64,2,64,128]{3,2,1,0:T(8,128)(2,1)}, u32[]{:S(2)}, u32[]{:S(2)}) async-start(bf16[64,2,64,128]{3,2,1,0:T(8,128)(2,1)} %bitcast.19), calls=%async_computation.5 | async-start | bytes 4194304 | tf_op jit(solution)/shard_map/all_to_all | solution.py:151
  207.4 7.5 %reshape.58.refs_1_ = bf16[4096,512]{1,0:T(8,128)(2,1)} reshape(bf16[128,128,128]{2,1,0:T(8,128)(2,1)} %param.7) | data formatting | bytes 8388608 | tf_op jit(solution)/shard_map/reshape | solution.py:179
  214.9 14.7 %shard_map.80 = (bf16[64,128,128]{2,1,0:T(8,128)(2,1)}, f32[512,512]{1,0:T(8,128)}) custom-call(s32[20]{0:T(128)} %order_ref.15, s32[20]{0:T(128)} %window_ref.15, s32[3]{0:T(128)} %swap_ref.15, bf16[20,128,128]{2,1,0:T(8,128)(2,1)} %gates_ref.15, bf16[128,64,128]{2,1,0:T(8,128)(2,1)} %bitcast.15, bf16[4096,512]{1,0:T(8,128)(2,1)} %reshape.58.refs_1_), custom_call_target="tpu_custom_call" | custom-call | tf_op jit(solution)/shard_map/pallas_call | solution.py:139
  229.6 8.2 %all-to-all-done.5 = bf16[64,2,64,128]{3,2,1,0:T(8,128)(2,1)} async-done(((bf16[64,2,64,128]{3,2,1,0:T(8,128)(2,1)}), bf16[64,2,64,128]{3,2,1,0:T(8,128)(2,1)}, u32[]{:S(2)}, u32[]{:S(2)}) %all-to-all-start.5) | async-done | bytes 2097184 | tf_op jit(solution)/shard_map/all_to_all | solution.py:151
  237.8 14.8 %shard_map.84 = (bf16[64,128,128]{2,1,0:T(8,128)(2,1)}, f32[512,512]{1,0:T(8,128)}) custom-call(s32[20]{0:T(128)} %order_ref.15, s32[20]{0:T(128)} %window_ref.15, s32[3]{0:T(128)} %swap_ref.15, bf16[20,128,128]{2,1,0:T(8,128)(2,1)} %gates_ref.15, bf16[128,64,128]{2,1,0:T(8,128)(2,1)} %bitcast.11.refs_0_, bf16[4096,512]{1,0:T(8,128)(2,1)} %reshape.58.refs_1_), custom_call_target="tpu_custom_call" | custom-call | tf_op jit(solution)/shard_map/pallas_call | solution.py:139
  252.6 1.4 add_convert_fusion
  254.3 21.7 %all_to_all.40 = bf16[128,16,128]{2,1,0:T(8,128)(2,1)S(1)} all-to-all(bf16[128,16,128]{2,1,0:T(8,128)(2,1)S(1)} %convert_element_type.17), channel_id=1, replica_groups=mesh['amp'=64,'grp'=2] {'amp','grp'}, dimensions={0} | all-to-all | bytes 1048576 | tf_op jit(solution)/shard_map/all_to_all | solution.py:158
  277.0 4.9 %all-to-all-start.7 = ((bf16[128,16,128]{2,1,0:T(8,128)(2,1)}), bf16[128,16,128]{2,1,0:T(8,128)(2,1)S(1)}, u32[]{:S(2)}, u32[]{:S(2)}) async-start(bf16[128,16,128]{2,1,0:T(8,128)(2,1)} %broadcast_in_dim.10), calls=%async_computation.7 | async-start | bytes 1048576 | tf_op jit(solution)/shard_map/all_to_all | solution.py:161
  281.9 4.0 %pad_maximum_fusion = bf16[128,128,128]{2,1,0:T(8,128)(2,1)} fusion(bf16[64,128,128]{2,1,0:T(8,128)(2,1)} %get-tuple-element.7, bf16[64,128,128]{2,1,0:T(8,128)(2,1)S(1)} %copy-done.4), kind=kLoop, calls=%fused_computation | loop fusion | flops 2097152 | bytes 8388608 | tf_op jit(solution)/shard_map/concatenate | solution.py:190
  285.9 9.2 %all-to-all-done.7 = bf16[128,16,128]{2,1,0:T(8,128)(2,1)S(1)} async-done(((bf16[128,16,128]{2,1,0:T(8,128)(2,1)}), bf16[128,16,128]{2,1,0:T(8,128)(2,1)S(1)}, u32[]{:S(2)}, u32[]{:S(2)}) %all-to-all-start.7) | async-done | bytes 524320 | tf_op jit(solution)/shard_map/all_to_all | solution.py:161
  295.4 1.1 select_reduce_fusion
  297.2 1.5 fusion.1
  (12 shorter events, 1.7 us)
Async XLA Ops:
  12.2 42.9 %all-to-all-start = ((bf16[64,2,64,128]{3,2,1,0:T(8,128)(2,1)}), bf16[64,2,64,128]{3,2,1,0:T(8,128)(2,1)S(1)}, u32[]{:S(2)}, u32[]{:S(2)}) async-start(bf16[64,2,64,128]{3,2,1,0:T(8,128)(2,1)} %bitcast.24), calls=%async_computation | async-start | bytes 4194304 | tf_op jit(solution)/shard_map/all_to_all | solution.py:151
  55.2 1.3 copy-start.3
  56.5 35.4 %all-to-all-start.3 = ((bf16[64,2,64,128]{3,2,1,0:T(8,128)(2,1)}), bf16[64,2,64,128]{3,2,1,0:T(8,128)(2,1)S(1)}, u32[]{:S(2)}, u32[]{:S(2)}) async-start(bf16[64,2,64,128]{3,2,1,0:T(8,128)(2,1)} %bitcast.23), calls=%async_computation.3 | async-start | bytes 4194304 | tf_op jit(solution)/shard_map/all_to_all | solution.py:151
  91.9 1.3 copy-start.1
  93.2 35.5 %all-to-all-start.1 = ((bf16[64,2,64,128]{3,2,1,0:T(8,128)(2,1)}), bf16[64,2,64,128]{3,2,1,0:T(8,128)(2,1)}, u32[]{:S(2)}, u32[]{:S(2)}) async-start(bf16[64,2,64,128]{3,2,1,0:T(8,128)(2,1)} %bitcast.20), calls=%async_computation.1 | async-start | bytes 4194304 | tf_op jit(solution)/shard_map/all_to_all | solution.py:151
  128.8 35.4 %all-to-all-start.4 = ((bf16[64,2,64,128]{3,2,1,0:T(8,128)(2,1)}), bf16[64,2,64,128]{3,2,1,0:T(8,128)(2,1)S(1)}, u32[]{:S(2)}, u32[]{:S(2)}) async-start(bf16[64,2,64,128]{3,2,1,0:T(8,128)(2,1)} %bitcast.21), calls=%async_computation.4 | async-start | bytes 4194304 | tf_op jit(solution)/shard_map/all_to_all | solution.py:151
  164.2 1.3 copy-start.2
  165.5 35.4 %all-to-all-start.2 = ((bf16[64,2,64,128]{3,2,1,0:T(8,128)(2,1)}), bf16[64,2,64,128]{3,2,1,0:T(8,128)(2,1)S(1)}, u32[]{:S(2)}, u32[]{:S(2)}) async-start(bf16[64,2,64,128]{3,2,1,0:T(8,128)(2,1)} %bitcast.22), calls=%async_computation.2 | async-start | bytes 4194304 | tf_op jit(solution)/shard_map/all_to_all | solution.py:151
  200.9 1.4 copy-start
  202.2 35.5 %all-to-all-start.5 = ((bf16[64,2,64,128]{3,2,1,0:T(8,128)(2,1)}), bf16[64,2,64,128]{3,2,1,0:T(8,128)(2,1)}, u32[]{:S(2)}, u32[]{:S(2)}) async-start(bf16[64,2,64,128]{3,2,1,0:T(8,128)(2,1)} %bitcast.19), calls=%async_computation.5 | async-start | bytes 4194304 | tf_op jit(solution)/shard_map/all_to_all | solution.py:151
  237.8 14.8 %copy-start.5 = (f32[512,512]{1,0:T(8,128)S(1)}, f32[512,512]{1,0:T(8,128)}, u32[]{:S(2)}) copy-start(f32[512,512]{1,0:T(8,128)} %get-tuple-element.8) | copy-start | bytes 3145732
  254.0 28.0 %copy-start.4 = (bf16[64,128,128]{2,1,0:T(8,128)(2,1)S(1)}, bf16[64,128,128]{2,1,0:T(8,128)(2,1)}, u32[]{:S(2)}) copy-start(bf16[64,128,128]{2,1,0:T(8,128)(2,1)} %get-tuple-element.6) | copy-start | bytes 6291460
  277.0 18.1 %all-to-all-start.7 = ((bf16[128,16,128]{2,1,0:T(8,128)(2,1)}), bf16[128,16,128]{2,1,0:T(8,128)(2,1)S(1)}, u32[]{:S(2)}, u32[]{:S(2)}) async-start(bf16[128,16,128]{2,1,0:T(8,128)(2,1)} %broadcast_in_dim.10), calls=%async_computation.7 | async-start | bytes 1048576 | tf_op jit(solution)/shard_map/all_to_all | solution.py:161

commit v13 on v11

--- a/solution.py
+++ b/solution.py
@@ -192,11 +192,11 @@
         summed,
         summed,
         (((0,), (0,)), ((), ())),
-        precision=lax.Precision.HIGHEST,
+        precision=lax.Precision.HIGH,
         preferred_element_type=jnp.float32,
     )
     scale = 1.0 / jnp.sqrt(jnp.trace(gram) / order + 1e-06)
-    product = jnp.dot(owned, gram, precision=lax.Precision.HIGHEST)
+    product = jnp.dot(owned, gram, precision=lax.Precision.HIGH)
     environment = jnp.sqrt(jnp.float32(order)) * (
         1.5 * scale * owned - 0.5 * scale * scale * scale * product
     )

time: 299 us -> 298 us (level)
  no operation moved by 1% of the time
where the time goes in v13:
time: 298 us; the launch traced here: 297 us
  waiting for transfers between devices  116 us (39%)
  Pallas kernels  93.2 us (31%)
  starting transfers between devices  42.4 us (14%)
  blocking collectives  21.7 us (7%)
  local copies, waits for them, and re-layouts  14.4 us (5%)
  other arithmetic  5.49 us (2%)
    all_to_all x6, waiting for transfers between devices, swap_major(): lax.all_to_all(split, 'amp', split_axis=0, concat_axis=0, tiled=True)  107 us
    pallas_call x8, Pallas kernels, run_segment(): pl.pallas_call(make_kernel(slab_in, slab_out, len(sources), per_source, s...  93.2 us
    all_to_all x6, starting transfers between devices, swap_major(): lax.all_to_all(split, 'amp', split_axis=0, concat_axis=0, tiled=True)  37.5 us
    all_to_all x1, blocking collectives, all_sum(): lax.all_to_all(pieces, axes, split_axis=0, concat_axis=0, tiled=True)  21.7 us
    all_to_all x1, waiting for transfers between devices, all_sum(): lax.all_to_all(spread, axes, split_axis=0, concat_axis=0, tiled=True)  9.21 us
    reshape x1, local copies, waits for them, and re-layouts, on_device(): adjoint_flat = adjoint.reshape(-1, 4 * adjoint.shape[2])  7.52 us
  transfers between devices with their start and end apart: 7, of which 7 were waited for; matrix products, arithmetic and copies ran while one was open for 4% of the time, Pallas kernels for 23%

profile of v13, /device:TPU:1, one launch (start us, length us, event | category | flops | bytes accessed | tf_op | source)
XLA Modules:
  0.0 296.9 jit_solution(386773758383859070)
XLA Ops:
  0.6 12.2 %shard_map.77 = bf16[128,64,128]{2,1,0:T(8,128)(2,1)} custom-call(s32[20]{0:T(128)} %order_ref.15, s32[20]{0:T(128)} %window_ref.15, s32[3]{0:T(128)} %swap_ref.15, bf16[20,128,128]{2,1,0:T(8,128)(2,1)} %gates_ref.15, bf16[128,128,128]{2,1,0:T(8,128)(2,1)} %refs_0_.3), custom_call_target="tpu_custom_call" | custom-call | tf_op jit(solution)/shard_map/pallas_call | solution.py:137
  12.9 12.5 %all-to-all-start = ((bf16[64,2,64,128]{3,2,1,0:T(8,128)(2,1)}), bf16[64,2,64,128]{3,2,1,0:T(8,128)(2,1)S(1)}, u32[]{:S(2)}, u32[]{:S(2)}) async-start(bf16[64,2,64,128]{3,2,1,0:T(8,128)(2,1)} %bitcast.24), calls=%async_computation | async-start | bytes 4194304 | tf_op jit(solution)/shard_map/all_to_all | solution.py:149
  25.3 12.1 %shard_map.81 = bf16[128,64,128]{2,1,0:T(8,128)(2,1)} custom-call(s32[20]{0:T(128)} %order_ref.15, s32[20]{0:T(128)} %window_ref.15, s32[3]{0:T(128)} %swap_ref.15, bf16[20,128,128]{2,1,0:T(8,128)(2,1)} %gates_ref.15, bf16[128,128,128]{2,1,0:T(8,128)(2,1)} %refs_0_.3), custom_call_target="tpu_custom_call" | custom-call | tf_op jit(solution)/shard_map/pallas_call | solution.py:137
  37.5 18.3 %all-to-all-done = bf16[64,2,64,128]{3,2,1,0:T(8,128)(2,1)S(1)} async-done(((bf16[64,2,64,128]{3,2,1,0:T(8,128)(2,1)}), bf16[64,2,64,128]{3,2,1,0:T(8,128)(2,1)S(1)}, u32[]{:S(2)}, u32[]{:S(2)}) %all-to-all-start) | async-done | bytes 2097184 | tf_op jit(solution)/shard_map/all_to_all | solution.py:149
  55.8 1.3 copy-done.3
  57.2 4.9 %all-to-all-start.3 = ((bf16[64,2,64,128]{3,2,1,0:T(8,128)(2,1)}), bf16[64,2,64,128]{3,2,1,0:T(8,128)(2,1)S(1)}, u32[]{:S(2)}, u32[]{:S(2)}) async-start(bf16[64,2,64,128]{3,2,1,0:T(8,128)(2,1)} %bitcast.23), calls=%async_computation.3 | async-start | bytes 4194304 | tf_op jit(solution)/shard_map/all_to_all | solution.py:149
  62.1 10.7 %shard_map.78 = bf16[128,64,128]{2,1,0:T(8,128)(2,1)} custom-call(s32[20]{0:T(128)} %order_ref.15, s32[20]{0:T(128)} %window_ref.15, s32[3]{0:T(128)} %swap_ref.15, bf16[20,128,128]{2,1,0:T(8,128)(2,1)} %gates_ref.15, bf16[128,64,128]{2,1,0:T(8,128)(2,1)} %bitcast.18), custom_call_target="tpu_custom_call" | custom-call | tf_op jit(solution)/shard_map/pallas_call | solution.py:137
  72.7 19.8 %all-to-all-done.3 = bf16[64,2,64,128]{3,2,1,0:T(8,128)(2,1)S(1)} async-done(((bf16[64,2,64,128]{3,2,1,0:T(8,128)(2,1)}), bf16[64,2,64,128]{3,2,1,0:T(8,128)(2,1)S(1)}, u32[]{:S(2)}, u32[]{:S(2)}) %all-to-all-start.3) | async-done | bytes 2097184 | tf_op jit(solution)/shard_map/all_to_all | solution.py:149
  92.6 1.3 copy-done.1
  93.9 5.1 %all-to-all-start.1 = ((bf16[64,2,64,128]{3,2,1,0:T(8,128)(2,1)}), bf16[64,2,64,128]{3,2,1,0:T(8,128)(2,1)}, u32[]{:S(2)}, u32[]{:S(2)}) async-start(bf16[64,2,64,128]{3,2,1,0:T(8,128)(2,1)} %bitcast.20), calls=%async_computation.1 | async-start | bytes 4194304 | tf_op jit(solution)/shard_map/all_to_all | solution.py:149
  99.0 10.6 %shard_map.82 = bf16[128,64,128]{2,1,0:T(8,128)(2,1)} custom-call(s32[20]{0:T(128)} %order_ref.15, s32[20]{0:T(128)} %window_ref.15, s32[3]{0:T(128)} %swap_ref.15, bf16[20,128,128]{2,1,0:T(8,128)(2,1)} %gates_ref.15, bf16[128,64,128]{2,1,0:T(8,128)(2,1)} %bitcast.16), custom_call_target="tpu_custom_call" | custom-call | tf_op jit(solution)/shard_map/pallas_call | solution.py:137
  109.6 19.8 %all-to-all-done.1 = bf16[64,2,64,128]{3,2,1,0:T(8,128)(2,1)} async-done(((bf16[64,2,64,128]{3,2,1,0:T(8,128)(2,1)}), bf16[64,2,64,128]{3,2,1,0:T(8,128)(2,1)}, u32[]{:S(2)}, u32[]{:S(2)}) %all-to-all-start.1) | async-done | bytes 2097184 | tf_op jit(solution)/shard_map/all_to_all | solution.py:149
  129.4 4.9 %all-to-all-start.4 = ((bf16[64,2,64,128]{3,2,1,0:T(8,128)(2,1)}), bf16[64,2,64,128]{3,2,1,0:T(8,128)(2,1)S(1)}, u32[]{:S(2)}, u32[]{:S(2)}) async-start(bf16[64,2,64,128]{3,2,1,0:T(8,128)(2,1)} %bitcast.21), calls=%async_computation.4 | async-start | bytes 4194304 | tf_op jit(solution)/shard_map/all_to_all | solution.py:149
  134.3 11.3 %shard_map.79 = bf16[128,64,128]{2,1,0:T(8,128)(2,1)} custom-call(s32[20]{0:T(128)} %order_ref.15, s32[20]{0:T(128)} %window_ref.15, s32[3]{0:T(128)} %swap_ref.15, bf16[20,128,128]{2,1,0:T(8,128)(2,1)} %gates_ref.15, bf16[128,64,128]{2,1,0:T(8,128)(2,1)} %bitcast.3.refs_0_), custom_call_target="tpu_custom_call" | custom-call | tf_op jit(solution)/shard_map/pallas_call | solution.py:137
  145.6 19.2 %all-to-all-done.4 = bf16[64,2,64,128]{3,2,1,0:T(8,128)(2,1)S(1)} async-done(((bf16[64,2,64,128]{3,2,1,0:T(8,128)(2,1)}), bf16[64,2,64,128]{3,2,1,0:T(8,128)(2,1)S(1)}, u32[]{:S(2)}, u32[]{:S(2)}) %all-to-all-start.4) | async-done | bytes 2097184 | tf_op jit(solution)/shard_map/all_to_all | solution.py:149
  164.8 1.3 copy-done.2
  166.1 4.9 %all-to-all-start.2 = ((bf16[64,2,64,128]{3,2,1,0:T(8,128)(2,1)}), bf16[64,2,64,128]{3,2,1,0:T(8,128)(2,1)S(1)}, u32[]{:S(2)}, u32[]{:S(2)}) async-start(bf16[64,2,64,128]{3,2,1,0:T(8,128)(2,1)} %bitcast.22), calls=%async_computation.2 | async-start | bytes 4194304 | tf_op jit(solution)/shard_map/all_to_all | solution.py:149
  171.1 11.3 %shard_map.83 = bf16[128,64,128]{2,1,0:T(8,128)(2,1)} custom-call(s32[20]{0:T(128)} %order_ref.15, s32[20]{0:T(128)} %window_ref.15, s32[3]{0:T(128)} %swap_ref.15, bf16[20,128,128]{2,1,0:T(8,128)(2,1)} %gates_ref.15, bf16[128,64,128]{2,1,0:T(8,128)(2,1)} %bitcast.17), custom_call_target="tpu_custom_call" | custom-call | tf_op jit(solution)/shard_map/pallas_call | solution.py:137
  182.4 19.2 %all-to-all-done.2 = bf16[64,2,64,128]{3,2,1,0:T(8,128)(2,1)S(1)} async-done(((bf16[64,2,64,128]{3,2,1,0:T(8,128)(2,1)}), bf16[64,2,64,128]{3,2,1,0:T(8,128)(2,1)S(1)}, u32[]{:S(2)}, u32[]{:S(2)}) %all-to-all-start.2) | async-done | bytes 2097184 | tf_op jit(solution)/shard_map/all_to_all | solution.py:149
  201.5 1.3 copy-done
  202.9 5.1 %all-to-all-start.5 = ((bf16[64,2,64,128]{3,2,1,0:T(8,128)(2,1)}), bf16[64,2,64,128]{3,2,1,0:T(8,128)(2,1)}, u32[]{:S(2)}, u32[]{:S(2)}) async-start(bf16[64,2,64,128]{3,2,1,0:T(8,128)(2,1)} %bitcast.19), calls=%async_computation.5 | async-start | bytes 4194304 | tf_op jit(solution)/shard_map/all_to_all | solution.py:149
  208.0 7.5 %reshape.58.refs_1_ = bf16[4096,512]{1,0:T(8,128)(2,1)} reshape(bf16[128,128,128]{2,1,0:T(8,128)(2,1)} %param.7) | data formatting | bytes 8388608 | tf_op jit(solution)/shard_map/reshape | solution.py:177
  215.6 12.4 %shard_map.80 = (bf16[64,128,128]{2,1,0:T(8,128)(2,1)}, f32[512,512]{1,0:T(8,128)}) custom-call(s32[20]{0:T(128)} %order_ref.15, s32[20]{0:T(128)} %window_ref.15, s32[3]{0:T(128)} %swap_ref.15, bf16[20,128,128]{2,1,0:T(8,128)(2,1)} %gates_ref.15, bf16[128,64,128]{2,1,0:T(8,128)(2,1)} %bitcast.15, bf16[4096,512]{1,0:T(8,128)(2,1)} %reshape.58.refs_1_), custom_call_target="tpu_custom_call" | custom-call | tf_op jit(solution)/shard_map/pallas_call | solution.py:137
  228.0 10.4 %all-to-all-done.5 = bf16[64,2,64,128]{3,2,1,0:T(8,128)(2,1)} async-done(((bf16[64,2,64,128]{3,2,1,0:T(8,128)(2,1)}), bf16[64,2,64,128]{3,2,1,0:T(8,128)(2,1)}, u32[]{:S(2)}, u32[]{:S(2)}) %all-to-all-start.5) | async-done | bytes 2097184 | tf_op jit(solution)/shard_map/all_to_all | solution.py:149
  238.4 12.6 %shard_map.84 = (bf16[64,128,128]{2,1,0:T(8,128)(2,1)}, f32[512,512]{1,0:T(8,128)}) custom-call(s32[20]{0:T(128)} %order_ref.15, s32[20]{0:T(128)} %window_ref.15, s32[3]{0:T(128)} %swap_ref.15, bf16[20,128,128]{2,1,0:T(8,128)(2,1)} %gates_ref.15, bf16[128,64,128]{2,1,0:T(8,128)(2,1)} %bitcast.11.refs_0_, bf16[4096,512]{1,0:T(8,128)(2,1)} %reshape.58.refs_1_), custom_call_target="tpu_custom_call" | custom-call | tf_op jit(solution)/shard_map/pallas_call | solution.py:137
  251.0 1.4 add_convert_fusion
  252.7 21.7 %all_to_all.40 = bf16[128,16,128]{2,1,0:T(8,128)(2,1)S(1)} all-to-all(bf16[128,16,128]{2,1,0:T(8,128)(2,1)S(1)} %convert_element_type.17), channel_id=1, replica_groups=mesh['amp'=64,'grp'=2] {'amp','grp'}, dimensions={0} | all-to-all | bytes 1048576 | tf_op jit(solution)/shard_map/all_to_all | solution.py:156
  275.4 4.9 %all-to-all-start.7 = ((bf16[128,16,128]{2,1,0:T(8,128)(2,1)}), bf16[128,16,128]{2,1,0:T(8,128)(2,1)S(1)}, u32[]{:S(2)}, u32[]{:S(2)}) async-start(bf16[128,16,128]{2,1,0:T(8,128)(2,1)} %broadcast_in_dim.10), calls=%async_computation.7 | async-start | bytes 1048576 | tf_op jit(solution)/shard_map/all_to_all | solution.py:159
  280.4 4.0 %pad_maximum_fusion = bf16[128,128,128]{2,1,0:T(8,128)(2,1)} fusion(bf16[64,128,128]{2,1,0:T(8,128)(2,1)} %get-tuple-element.7, bf16[64,128,128]{2,1,0:T(8,128)(2,1)S(1)} %copy-done.4), kind=kLoop, calls=%fused_computation | loop fusion | flops 2097152 | bytes 8388608 | tf_op jit(solution)/shard_map/concatenate | solution.py:188
  284.3 9.2 %all-to-all-done.7 = bf16[128,16,128]{2,1,0:T(8,128)(2,1)S(1)} async-done(((bf16[128,16,128]{2,1,0:T(8,128)(2,1)}), bf16[128,16,128]{2,1,0:T(8,128)(2,1)S(1)}, u32[]{:S(2)}, u32[]{:S(2)}) %all-to-all-start.7) | async-done | bytes 524320 | tf_op jit(solution)/shard_map/all_to_all | solution.py:159
  293.9 1.1 select_reduce_fusion
  295.6 1.3 fusion.1
  (12 shorter events, 1.7 us)
Async XLA Ops:
  12.9 42.9 %all-to-all-start = ((bf16[64,2,64,128]{3,2,1,0:T(8,128)(2,1)}), bf16[64,2,64,128]{3,2,1,0:T(8,128)(2,1)S(1)}, u32[]{:S(2)}, u32[]{:S(2)}) async-start(bf16[64,2,64,128]{3,2,1,0:T(8,128)(2,1)} %bitcast.24), calls=%async_computation | async-start | bytes 4194304 | tf_op jit(solution)/shard_map/all_to_all | solution.py:149
  55.8 1.3 copy-start.3
  57.2 35.4 %all-to-all-start.3 = ((bf16[64,2,64,128]{3,2,1,0:T(8,128)(2,1)}), bf16[64,2,64,128]{3,2,1,0:T(8,128)(2,1)S(1)}, u32[]{:S(2)}, u32[]{:S(2)}) async-start(bf16[64,2,64,128]{3,2,1,0:T(8,128)(2,1)} %bitcast.23), calls=%async_computation.3 | async-start | bytes 4194304 | tf_op jit(solution)/shard_map/all_to_all | solution.py:149
  92.6 1.3 copy-start.1
  93.9 35.5 %all-to-all-start.1 = ((bf16[64,2,64,128]{3,2,1,0:T(8,128)(2,1)}), bf16[64,2,64,128]{3,2,1,0:T(8,128)(2,1)}, u32[]{:S(2)}, u32[]{:S(2)}) async-start(bf16[64,2,64,128]{3,2,1,0:T(8,128)(2,1)} %bitcast.20), calls=%async_computation.1 | async-start | bytes 4194304 | tf_op jit(solution)/shard_map/all_to_all | solution.py:149
  129.4 35.4 %all-to-all-start.4 = ((bf16[64,2,64,128]{3,2,1,0:T(8,128)(2,1)}), bf16[64,2,64,128]{3,2,1,0:T(8,128)(2,1)S(1)}, u32[]{:S(2)}, u32[]{:S(2)}) async-start(bf16[64,2,64,128]{3,2,1,0:T(8,128)(2,1)} %bitcast.21), calls=%async_computation.4 | async-start | bytes 4194304 | tf_op jit(solution)/shard_map/all_to_all | solution.py:149
  164.8 1.3 copy-start.2
  166.1 35.4 %all-to-all-start.2 = ((bf16[64,2,64,128]{3,2,1,0:T(8,128)(2,1)}), bf16[64,2,64,128]{3,2,1,0:T(8,128)(2,1)S(1)}, u32[]{:S(2)}, u32[]{:S(2)}) async-start(bf16[64,2,64,128]{3,2,1,0:T(8,128)(2,1)} %bitcast.22), calls=%async_computation.2 | async-start | bytes 4194304 | tf_op jit(solution)/shard_map/all_to_all | solution.py:149
  201.5 1.4 copy-start
  202.9 35.5 %all-to-all-start.5 = ((bf16[64,2,64,128]{3,2,1,0:T(8,128)(2,1)}), bf16[64,2,64,128]{3,2,1,0:T(8,128)(2,1)}, u32[]{:S(2)}, u32[]{:S(2)}) async-start(bf16[64,2,64,128]{3,2,1,0:T(8,128)(2,1)} %bitcast.19), calls=%async_computation.5 | async-start | bytes 4194304 | tf_op jit(solution)/shard_map/all_to_all | solution.py:149
  238.4 12.6 %copy-start.5 = (f32[512,512]{1,0:T(8,128)S(1)}, f32[512,512]{1,0:T(8,128)}, u32[]{:S(2)}) copy-start(f32[512,512]{1,0:T(8,128)} %get-tuple-element.8) | copy-start | bytes 3145732
  252.4 28.0 %copy-start.4 = (bf16[64,128,128]{2,1,0:T(8,128)(2,1)S(1)}, bf16[64,128,128]{2,1,0:T(8,128)(2,1)}, u32[]{:S(2)}) copy-start(bf16[64,128,128]{2,1,0:T(8,128)(2,1)} %get-tuple-element.6) | copy-start | bytes 6291460
  275.4 18.1 %all-to-all-start.7 = ((bf16[128,16,128]{2,1,0:T(8,128)(2,1)}), bf16[128,16,128]{2,1,0:T(8,128)(2,1)S(1)}, u32[]{:S(2)}, u32[]{:S(2)}) async-start(bf16[128,16,128]{2,1,0:T(8,128)(2,1)} %broadcast_in_dim.10), calls=%async_computation.7 | async-start | bytes 1048576 | tf_op jit(solution)/shard_map/all_to_all | solution.py:159
